TPU v7x, 128 devices: a whole 4x4x4 slice. The times are simulated.
128 devices in a mesh: req: 32 (over x, z, core), mlp: 4 (over y).
Axes of the slice: x: 4, y: 4, z: 4, core: 2. Of those that a mesh axis runs over, the one named last changes fastest.
Arguments:
- hidden_in: bfloat16 [4096, 4096], P('req'), may hold values from -6 to 6
- attn_gain: bfloat16 [4096], replicated, may hold values from 0.5 to 1.5
- w_query: bfloat16 [4096, 2048], P(None, 'mlp'), may hold values from -0.09375 to 0.09375
- w_key: bfloat16 [4096, 512], P(None, 'mlp'), may hold values from -0.09375 to 0.09375
- w_value: bfloat16 [4096, 512], P(None, 'mlp'), may hold values from -0.09375 to 0.09375
- w_out: bfloat16 [2048, 4096], P('mlp'), may hold values from -0.125 to 0.125
- mlp_gain: bfloat16 [4096], replicated, may hold values from 0.5 to 1.5
- w_gate: bfloat16 [4096, 14336], P('mlp', 'req'), may hold values from -0.09375 to 0.09375
- w_up: bfloat16 [4096, 14336], P('mlp', 'req'), may hold values from -0.09375 to 0.09375
- w_down: bfloat16 [14336, 4096], P('req', 'mlp'), may hold values from -0.046875 to 0.046875
- prefix_kv: bfloat16 [65536, 2, 512], P('req', None, 'mlp'), may hold values from -512 to 512
- suffix_lengths: int32 [32, 4], P('req'), may hold values from 1 to 125, as said below
- prefix_owner: int32 [8, 4], replicated, may hold values from 0 to 3, each once within a row
Outputs:
- hidden_out: bfloat16 [4096, 4096], P('req', 'mlp')
- suffix_kv: bfloat16 [4096, 2, 512], P('req', None, 'mlp')
Inputs may be any that keep to these rules, and one draw needn't show every extreme that they name: `suffix_lengths`: the lengths of one index of req sum to at most 128; in every draw some index sums to exactly 128. `prefix_owner`: each row is a permutation.
All inputs are finite; a program needn't handle non-finite values.
Results may differ from a plain program's by a relative error of at most 0.02.
The roundings to bfloat16 on the way count: a program that leaves them out, or rounds other values in their place, can miss the bound.
Values may be sent and summed in bfloat16 or wider, within the bound.
No kernel may reach another device: no remote copies, remote signals or barrier semaphores. Data moves between devices by JAX's collectives and lax.ppermute only.
A program may use at most 128 MiB of HBM per device.

v0:
```python
import math

import jax
import jax.numpy as jnp
from jax import lax
from jax.sharding import PartitionSpec as P

HEAD_DIM = 128
PREFIX = 8192
GSPAN = 4


rope_base = 500000.0
eps = 1e-05


def from_partner(value, axis, stride):
    mask = 2**stride
    pairs = [(source, source ^ mask) for source in range(lax.axis_size(axis))]
    return lax.ppermute(value, axis, pairs)


def rope(values, positions):
    half = values.shape[-1] // 2
    freq = rope_base ** (-jnp.arange(half, dtype=jnp.float32) * 2.0 / values.shape[-1])
    angle = positions.astype(jnp.float32)[:, None] * freq[None, :]
    cosine = jnp.cos(angle)[:, None, :]
    sine = jnp.sin(angle)[:, None, :]
    former = values[..., :half]
    latter = values[..., half:]
    return jnp.concatenate(
        [former * cosine - latter * sine, latter * cosine + former * sine], axis=-1
    )


def rms_norm(values, gain):
    return (
        values
        * lax.rsqrt(jnp.mean(values * values, axis=-1, keepdims=True) + eps)
        * gain.astype(jnp.float32)
    )


def slot_layout(lengths, slot_count):
    ends = jnp.cumsum(lengths)
    starts = ends - lengths
    slot_ids = jnp.arange(slot_count, dtype=jnp.int32)
    request_of = jnp.sum((slot_ids[:, None] >= ends[None, :]).astype(jnp.int32), axis=1)
    picks = (request_of[:, None] == jnp.arange(lengths.shape[0], dtype=jnp.int32)[None, :]).astype(
        jnp.int32
    )
    start_of = jnp.sum(picks * starts[None, :], axis=1)
    positions = PREFIX + slot_ids - start_of
    return (request_of, request_of < lengths.shape[0], positions)


def partial_attention(grouped_queries, key_block, value_block, allowed):
    scores = jnp.einsum(
        "qkgd,nkd->kgqn", grouped_queries, key_block, preferred_element_type=jnp.float32
    ) / math.sqrt(grouped_queries.shape[-1])
    if allowed is not None:
        scores = jnp.where(allowed[None, None], scores, -jnp.inf)
    peak = jnp.max(scores, axis=-1)
    weights = jnp.exp(scores - peak[..., None])
    weight_sum = jnp.sum(weights, axis=-1)
    summed = jnp.einsum(
        "kgqn,nkd->kgqd",
        weights.astype(jnp.bfloat16),
        value_block,
        preferred_element_type=jnp.float32,
    )
    return (summed, peak, weight_sum)


def combine_states(former, latter):
    peak = jnp.maximum(former[1], latter[1])
    scale_former = jnp.exp(former[1] - peak)
    scale_latter = jnp.exp(latter[1] - peak)
    summed = former[0] * scale_former[..., None] + latter[0] * scale_latter[..., None]
    return (summed, peak, former[2] * scale_former + latter[2] * scale_latter)


def shards(
    hidden_in,
    attn_gain,
    w_query,
    w_key,
    w_value,
    w_out,
    mlp_gain,
    w_gate,
    w_up,
    w_down,
    prefix_kv,
    suffix_lengths,
    prefix_owner,
):
    slots_here = hidden_in.shape[0]
    head_dim = HEAD_DIM
    kv_heads = w_key.shape[1] // head_dim
    q_heads = w_query.shape[1] // head_dim
    group = q_heads // kv_heads
    block_len = prefix_kv.shape[0]
    span_bits = GSPAN.bit_length() - 1
    width_part = w_gate.shape[0]
    unit_count = w_gate.shape[1]
    request_of, live, positions = slot_layout(suffix_lengths[0], slots_here)
    hidden_f = hidden_in.astype(jnp.float32)
    normed = rms_norm(hidden_f, attn_gain).astype(jnp.bfloat16)
    query_rows = rope(
        jnp.dot(normed, w_query, preferred_element_type=jnp.float32).reshape(
            slots_here, q_heads, head_dim
        ),
        positions,
    ).astype(jnp.bfloat16)
    key_rows = rope(
        jnp.dot(normed, w_key, preferred_element_type=jnp.float32).reshape(
            slots_here, kv_heads, head_dim
        ),
        positions,
    ).astype(jnp.bfloat16)
    value_rows = (
        jnp.dot(normed, w_value, preferred_element_type=jnp.float32)
        .astype(jnp.bfloat16)
        .reshape(slots_here, kv_heads, head_dim)
    )
    grouped_queries = query_rows.reshape(slots_here, kv_heads, group, head_dim)
    place = lax.axis_index("req") % GSPAN
    group_id = lax.axis_index("req") // GSPAN
    owners = lax.dynamic_index_in_dim(prefix_owner, group_id, 0, keepdims=False)
    quarter = jnp.sum(jnp.where(owners == place, jnp.arange(GSPAN, dtype=jnp.int32), 0))
    prefix_pos = quarter * block_len + jnp.arange(block_len, dtype=jnp.int32)
    stored_keys = rope(
        prefix_kv[:, 0].reshape(block_len, kv_heads, head_dim).astype(jnp.float32), prefix_pos
    ).astype(jnp.bfloat16)
    stored_values = prefix_kv[:, 1].reshape(block_len, kv_heads, head_dim)
    blocks = jnp.stack([stored_keys, stored_values], axis=0)
    for bit_pos in range(span_bits):
        remote = from_partner(blocks, "req", bit_pos)
        blocks = jnp.concatenate([blocks, remote], axis=1)
    prefix_state = partial_attention(grouped_queries, blocks[0], blocks[1], None)
    slot_ids = jnp.arange(slots_here, dtype=jnp.int32)
    allowed = (request_of[:, None] == request_of[None, :]) & (
        slot_ids[None, :] <= slot_ids[:, None]
    )
    suffix_state = partial_attention(grouped_queries, key_rows, value_rows, allowed)
    merged, peak, weight_sum = combine_states(prefix_state, suffix_state)
    attended = (
        jnp.transpose(merged / weight_sum[..., None], (2, 0, 1, 3))
        .reshape(slots_here, q_heads * head_dim)
        .astype(jnp.bfloat16)
    )
    head_terms = jnp.dot(attended, w_out, preferred_element_type=jnp.float32)
    head_total = lax.psum(head_terms, "mlp")
    residual = (hidden_f + head_total).astype(jnp.bfloat16)
    normed_mlp = rms_norm(residual.astype(jnp.float32), mlp_gain).astype(jnp.bfloat16)
    width_start = lax.axis_index("mlp") * width_part
    normed_part = lax.dynamic_slice_in_dim(normed_mlp, width_start, width_part, 1)
    both_weights = jnp.concatenate([w_gate, w_up], axis=1)
    partial_sums = jnp.dot(
        lax.all_gather(normed_part, "req", axis=0, tiled=True),
        both_weights,
        preferred_element_type=jnp.float32,
    )
    gate_up = lax.psum(partial_sums, "mlp")
    act = (jax.nn.silu(gate_up[:, :unit_count]) * gate_up[:, unit_count:]).astype(jnp.bfloat16)
    down = lax.psum_scatter(
        jnp.dot(act, w_down, preferred_element_type=jnp.float32).astype(jnp.bfloat16),
        "req",
        scatter_dimension=0,
        tiled=True,
    ).astype(jnp.float32)
    residual_part = lax.dynamic_slice_in_dim(residual, width_start, width_part, 1).astype(
        jnp.float32
    )
    hidden_out = jnp.where(live[:, None], residual_part + down, 0.0).astype(jnp.bfloat16)
    stacked_kv = jnp.stack(
        [
            key_rows.reshape(slots_here, kv_heads * head_dim),
            value_rows.reshape(slots_here, kv_heads * head_dim),
        ],
        axis=1,
    )
    suffix_kv = jnp.where(live[:, None, None], stacked_kv, jnp.zeros_like(stacked_kv))
    return (hidden_out, suffix_kv)


def solution(mesh):
    placed = (
        P("req", None),
        P(),
        P(None, "mlp"),
        P(None, "mlp"),
        P(None, "mlp"),
        P("mlp", None),
        P(),
        P("mlp", "req"),
        P("mlp", "req"),
        P("req", "mlp"),
        P("req", None, "mlp"),
        P("req", None),
        P(),
    )
    return jax.shard_map(
        shards,
        mesh=mesh,
        in_specs=placed,
        out_specs=(P("req", "mlp"), P("req", None, "mlp")),
        check_vma=False,
    )
```

profile of v0, /device:TPU:0, one launch (start us, length us, event | category | flops | bytes accessed | tf_op | source)
XLA Modules:
  0.0 613.3 jit_solution(10236745792863355686)
XLA Ops:
  7.2 0.0 copy-start
  7.2 0.0 all-reduce.3.cloned.1.call-start
  7.3 0.9 fusion.62
  8.2 0.6 select_reduce_fusion.1
  9.5 3.3 fusion.76
  12.9 0.1 copy_convert_fusion
  12.9 0.0 copy-start.11
  12.9 0.0 copy-start.6
  13.0 0.1 copy.52
  13.0 4.8 fusion.42
  17.9 1.3 pad_maximum_fusion.2
  19.2 0.0 collective-permute-start
  19.2 0.2 reduce-window.4
  19.4 0.1 convert_reduce_fusion
  19.4 0.1 select_reduce_fusion
  19.5 1.5 fusion.8
  21.1 3.3 fusion.71
  24.3 0.0 collective-permute-done
  24.4 2.9 pad_maximum_fusion.1
  27.2 2.0 collective-permute-start.1
  29.3 0.1 reshape.468
  29.4 0.0 copy-start.8
  29.4 0.1 fusion.48
  29.5 1.9 convolution_bitcast_fusion
  31.4 0.2 fusion.54
  31.6 0.3 multiply_cosine_fusion.1
  32.0 0.2 fusion.77
  32.2 0.1 subtract_convert_fusion
  32.2 0.3 fusion.78
  32.5 0.1 fusion.43
  32.6 1.9 convolution_convert_fusion.1
  34.5 41.4 %collective-permute-done.1 = bf16[2,4096,1,128]{3,1,2,0:T(8,128)(2,1)} collective-permute-done((bf16[2,4096,1,128]{3,1,2,0:T(8,128)(2,1)}, bf16[2,4096,1,128]{3,1,2,0:T(8,128)(2,1)}, u32[]{:S(2)}, u32[]{:S(2)}) %collective-permute-start.1) | collective-permute-done | bytes 2097184 | tf_op jit(solution)/shard_map/ppermute | solution.py:20
  75.9 0.0 copy-done.3
  75.9 5.6 pad_maximum_fusion
  81.5 8.1 %bitcast_reduce_fusion = (f32[4,128]{1,0:T(4,128)S(1)}, f32[8192,128,4]{1,0,2:T(8,128)}) fusion(bf16[128,4,64]{2,0,1:T(8,128)(2,1)S(1)} %get-tuple-element.16, bf16[128,4,64]{2,0,1:T(8,128)(2,1)S(1)} %get-tuple-element.15, bf16[2,8192,1,128]{3,1,2,0:T(8,128)(2,1)S(1)} %pad_maximum_fusion), kind=kOutput, calls=%fused_computation.1 | convolution fusion | flops 1082392064 | bytes 19138560 | tf_op jit(solution)/shard_map/qkgd,nkd->kgqn/dot_general | solution.py:58
  89.6 8.5 %fusion.1 = f32[4,128]{1,0:T(4,128)S(1)} fusion(f32[8192,128,4]{1,0,2:T(8,128)} %get-tuple-element.26, f32[4,128]{1,0:T(4,128)S(1)} %get-tuple-element.25), kind=kLoop, calls=%fused_computation.3 | loop fusion | flops 12582400 | bytes 16781312 | tf_op jit(solution)/shard_map/reduce_sum | solution.py:65
  98.1 0.2 convolution_multiply_fusion
  98.3 0.0 copy-start.5
  98.4 7.6 %fusion.32 = bf16[4,128,128]{1,2,0:T(8,128)(2,1)S(1)} fusion(f32[4,128,128]{1,2,0:T(8,128)S(1)} %convolution_multiply_fusion, bf16[2,8192,1,128]{3,1,2,0:T(8,128)(2,1)S(1)} %pad_maximum_fusion, f32[8192,128,4]{1,0,2:T(8,128)} %get-tuple-element.26, f32[4,128]{1,0:T(4,128)S(1)} %get-tuple-element.25, f32[4,128]{1,0:T(4,128)S(1)} %get-tuple-element.8, ...), kind=kOutput, calls=%fused_computation.42 | convolution fusion | flops 1086586880 | bytes 19273728 | tf_op jit(solution)/shard_map/kgqn,nkd->kgqd/dot_general | solution.py:66
  106.0 0.0 copy-start.7
  106.0 0.0 copy-start.4
  106.0 2.0 fusion.79
  108.0 0.0 all-reduce.3.cloned.1.call-update
  108.1 0.0 all-gather.2.cloned.1.call-start
  108.1 0.0 copy-done.7
  108.1 0.0 copy-start.9
  108.2 60.9 %all-reduce.3.cloned.1.call-done = f32[128,4096]{1,0:T(8,128)} async-done(((f32[128,4096]{1,0:T(8,128)}), f32[128,4096]{1,0:T(8,128)}) %all-reduce.3.cloned.1.call-update) | async-done | bytes 2097168 | tf_op jit(solution)/shard_map/psum | solution.py:154
  169.1 2.0 multiply_reduce_fusion
  171.1 0.2 convert_element_type.119
  171.3 0.8 fusion.40
  172.2 0.0 all-gather.2.cloned.1.call-update
  172.2 0.0 all-reduce.5.cloned.1.call-start
  172.2 52.7 %all-gather.2.cloned.1.call-done = bf16[4096,1024]{1,0:T(8,128)(2,1)} async-done(((bf16[128,1024]{1,0:T(8,128)(2,1)}), bf16[4096,1024]{1,0:T(8,128)(2,1)}) %all-gather.2.cloned.1.call-update) | async-done | bytes 8388624 | tf_op jit(solution)/shard_map/all_gather | solution.py:161
  225.0 0.0 copy-done.9
  225.0 14.6 %fusion.13 = f32[4096,896]{1,0:T(8,128)} fusion(bf16[4096,1024]{1,0:T(8,128)(2,1)} %all-gather.2.cloned.1.call-done, bf16[1024,448]{0,1:T(8,128)(2,1)S(1)} %copy-done.9, bf16[1024,448]{0,1:T(8,128)(2,1)} %param.20), kind=kOutput, calls=%fused_computation.23 | convolution fusion | flops 7519862784 | bytes 24903680 | tf_op jit(solution)/shard_map/dot_general | solution.py:160
  239.6 0.0 all-reduce.5.cloned.1.call-update
  239.6 0.0 reduce-scatter.2.cloned.1.call-start
  239.6 261.4 %all-reduce.5.cloned.1.call-done = f32[4096,896]{1,0:T(8,128)} async-done(((f32[4096,896]{1,0:T(8,128)}), f32[4096,896]{1,0:T(8,128)}) %all-reduce.5.cloned.1.call-update) | async-done | bytes 14680080 | tf_op jit(solution)/shard_map/psum | solution.py:165
  501.1 10.8 %convolution_convert_fusion = bf16[4096,1024]{1,0:T(8,128)(2,1)} fusion(bf16[448,1024]{1,0:T(8,128)(2,1)S(1)} %copy-done.10, f32[4096,896]{1,0:T(8,128)} %all-reduce.5.cloned.1.call-done), kind=kOutput, calls=%fused_computation.9 | convolution fusion | flops 3773300736 | bytes 26083328 | tf_op jit(solution)/shard_map/dot_general | solution.py:168
  511.9 0.0 reduce-scatter.2.cloned.1.call-update
  512.0 0.8 copy.34
  512.7 92.2 %reduce-scatter.2.cloned.1.call-done = bf16[128,1024]{1,0:T(8,128)(2,1)} async-done(((bf16[4096,1024]{1,0:T(8,128)(2,1)}), bf16[128,1024]{1,0:T(8,128)(2,1)}) %reduce-scatter.2.cloned.1.call-update) | async-done | bytes 262160 | tf_op jit(solution)/shard_map/reduce_scatter | solution.py:167
  605.0 1.7 select_convert_fusion
  606.7 0.0 copy-done.1
  (23 shorter events, 0.1 us)
Async XLA Ops:
  7.2 22.3 %copy-start = (bf16[4096,128]{1,0:T(8,128)(2,1)S(1)}, bf16[4096,128]{1,0:T(8,128)(2,1)}, u32[]{:S(2)}) copy-start(bf16[4096,128]{1,0:T(8,128)(2,1)} %param.16) | copy-start | bytes 3145732
  7.2 161.9 %all-reduce.3.cloned.1.call-start = ((), (), s32[]{:S(2)}) async-start(), calls=%async_computation.1 | async-start | bytes 4194304 | tf_op jit(solution)/shard_map/psum | solution.py:154
  12.9 6.2 %copy-start.11 = (s32[1,4]{1,0:T(1,128)S(1)}, s32[1,4]{1,0:T(1,128)}, u32[]{:S(2)}) copy-start(s32[1,4]{1,0:T(1,128)} %param.24) | copy-start | bytes 52
  12.9 6.4 %copy-start.6 = (bf16[4096]{0:T(1024)(128)(2,1)S(1)}, bf16[4096]{0:T(1024)(128)(2,1)}, u32[]{:S(2)}) copy-start(bf16[4096]{0:T(1024)(128)(2,1)} %param.14) | copy-start | bytes 24580
  17.9 6.5 %copy-start.2 = (bf16[1,2048,1,64]{3,1,2,0:T(8,128)(2,1)}, bf16[1,2048,1,64]{3,1,2,0:T(8,128)(2,1)S(1)}, u32[]{:S(2)}) copy-start(bf16[1,2048,1,64]{3,1,2,0:T(8,128)(2,1)S(1)} %get-tuple-element.12) | copy-start | bytes 786436
  19.2 5.2 collective-permute-start
  27.2 48.6 %collective-permute-start.1 = (bf16[2,4096,1,128]{3,1,2,0:T(8,128)(2,1)}, bf16[2,4096,1,128]{3,1,2,0:T(8,128)(2,1)}, u32[]{:S(2)}, u32[]{:S(2)}) collective-permute-start(bf16[2,4096,1,128]{3,1,2,0:T(8,128)(2,1)} %pad_maximum_fusion.1), channel_id=1, source_target_pairs={{0,8},{4,12},{8,0},{12,4},{16,24},{20,28},{24,16},{28,20},{32,40},... | collective-permute-start | bytes 6291464 | tf_op jit(solution)/shard_map/ppermute | solution.py:20
  29.4 3.2 copy-start.8
  29.4 46.5 %copy-start.3 = (bf16[1,2048,1,64]{3,1,2,0:T(8,128)(2,1)S(1)}, bf16[1,2048,1,64]{3,1,2,0:T(8,128)(2,1)}, u32[]{:S(2)}) copy-start(bf16[1,2048,1,64]{3,1,2,0:T(8,128)(2,1)} %copy-done.2) | copy-start | bytes 786436
  98.3 7.6 %copy-start.5 = (bf16[512,4096]{1,0:T(8,128)(2,1)S(1)}, bf16[512,4096]{1,0:T(8,128)(2,1)}, u32[]{:S(2)}) copy-start(bf16[512,4096]{1,0:T(8,128)(2,1)} %param.18) | copy-start | bytes 12582916
  106.0 2.1 copy-start.7
  106.0 63.1 %copy-start.4 = (bf16[128,4096]{1,0:T(8,128)(2,1)S(1)}, bf16[128,4096]{1,0:T(8,128)(2,1)}, u32[]{:S(2)}) copy-start(bf16[128,4096]{1,0:T(8,128)(2,1)} %param.13) | copy-start | bytes 3145732
  108.1 116.9 %all-gather.2.cloned.1.call-start = ((), (), s32[]{:S(2)}) async-start(), calls=%async_computation.2 | async-start | bytes 8650752 | tf_op jit(solution)/shard_map/all_gather | solution.py:161
  108.1 116.8 %copy-start.9 = (bf16[1024,448]{0,1:T(8,128)(2,1)S(1)}, bf16[1024,448]{0,1:T(8,128)(2,1)}, u32[]{:S(2)}) copy-start(bf16[1024,448]{0,1:T(8,128)(2,1)} %param.21) | copy-start | bytes 2752516
  172.2 328.9 %all-reduce.5.cloned.1.call-start = ((), (), s32[]{:S(2)}) async-start(), calls=%async_computation.3 | async-start | bytes 29360128 | tf_op jit(solution)/shard_map/psum | solution.py:165
  239.6 261.5 %copy-start.10 = (bf16[448,1024]{1,0:T(8,128)(2,1)S(1)}, bf16[448,1024]{1,0:T(8,128)(2,1)}, u32[]{:S(2)}) copy-start(bf16[448,1024]{1,0:T(8,128)(2,1)} %param.22) | copy-start | bytes 2752516
  239.6 365.4 %reduce-scatter.2.cloned.1.call-start = ((), (), s32[]{:S(2)}) async-start(), calls=%async_computation.4 | async-start | bytes 8650752 | tf_op jit(solution)/shard_map/reduce_scatter | solution.py:167
  511.9 94.8 %copy-start.1 = (bf16[4096,128]{1,0:T(8,128)(2,1)S(1)}, bf16[4096,128]{1,0:T(8,128)(2,1)}, u32[]{:S(2)}) copy-start(bf16[4096,128]{1,0:T(8,128)(2,1)} %param.16) | copy-start | bytes 3145732
Sparse Core Ops, SparseCore 0:
  108.2 60.8 all-reduce.2
  172.3 52.6 all-gather.1
  239.7 261.3 all-reduce.4
  512.1 92.8 reduce-scatter.1
where the time goes:
time: 614 us; the launch traced here: 613 us
  waiting for transfers between devices  509 us (83%)
  matrix products  50.8 us (8%)
  other arithmetic  32.2 us (5%)
  between operations  14.8 us (2%)
    psum x1, waiting for transfers between devices, shards(): gate_up = lax.psum(partial_sums, 'mlp')  261 us
    reduce_scatter x1, waiting for transfers between devices, shards(): lax.psum_scatter(jnp.dot(act, w_down, preferred_element_type=jnp.float32)...  92.2 us
    psum x1, waiting for transfers between devices, shards(): head_total = lax.psum(head_terms, 'mlp')  60.9 us
    all_gather x1, waiting for transfers between devices, shards(): lax.all_gather(normed_part, 'req', axis=0, tiled=True)  52.7 us
    ppermute x2, waiting for transfers between devices, from_partner(): return lax.ppermute(value, axis, pairs)  41.4 us
    dot_general x1, matrix products, shards(): jnp.dot(lax.all_gather(normed_part, 'req', axis=0, tiled=True), both_weig...  14.6 us
  transfers between devices with their start and end apart: 6, of which 5 were waited for; matrix products, arithmetic and copies ran while one was open for 2% of the time, Pallas kernels for 0%

commit v1 on v0

--- a/solution.py
+++ b/solution.py
@@ -2,21 +2,25 @@
 
 import jax
 import jax.numpy as jnp
+import numpy as np
 from jax import lax
+from jax.sharding import Mesh
 from jax.sharding import PartitionSpec as P
+
 
 HEAD_DIM = 128
 PREFIX = 8192
 GSPAN = 4
 
+REQ = ("rx", "rc")
 
 rope_base = 500000.0
 eps = 1e-05
 
 
-def from_partner(value, axis, stride):
+def from_partner(value, axis, stride, size):
     mask = 2**stride
-    pairs = [(source, source ^ mask) for source in range(lax.axis_size(axis))]
+    pairs = [(source, source ^ mask) for source in range(size)]
     return lax.ppermute(value, axis, pairs)
 
 
@@ -80,7 +84,7 @@
     return (summed, peak, former[2] * scale_former + latter[2] * scale_latter)
 
 
-def shards(
+def layer(
     hidden_in,
     attn_gain,
     w_query,
@@ -102,8 +106,21 @@
     group = q_heads // kv_heads
     block_len = prefix_kv.shape[0]
     span_bits = GSPAN.bit_length() - 1
+    unit_count = w_gate.shape[1]
+    n_rx = lax.axis_size("rx")
+    n_rc = lax.axis_size("rc")
+    n_mlp = lax.axis_size("mlp")
+    n_req = n_rx * n_rc
+    req_index = lax.axis_index("rx") * n_rc + lax.axis_index("rc")
+    mlp_index = lax.axis_index("mlp")
+
     width_part = w_gate.shape[0]
-    unit_count = w_gate.shape[1]
+    gate_up_part = jnp.concatenate([w_gate, w_up], axis=1)
+    gate_up_pair = lax.all_gather(gate_up_part, ("rc", "mlp"), axis=0, tiled=False)
+    gate_up_pair = gate_up_pair.reshape(n_rc, n_mlp * width_part, 2 * unit_count)
+    down_pair = lax.all_gather(w_down, ("rc", "mlp"), axis=0, tiled=False)
+    down_pair = down_pair.reshape(n_rc, n_mlp, unit_count, width_part)
+
     request_of, live, positions = slot_layout(suffix_lengths[0], slots_here)
     hidden_f = hidden_in.astype(jnp.float32)
     normed = rms_norm(hidden_f, attn_gain).astype(jnp.bfloat16)
@@ -125,8 +142,8 @@
         .reshape(slots_here, kv_heads, head_dim)
     )
     grouped_queries = query_rows.reshape(slots_here, kv_heads, group, head_dim)
-    place = lax.axis_index("req") % GSPAN
-    group_id = lax.axis_index("req") // GSPAN
+    place = req_index % GSPAN
+    group_id = req_index // GSPAN
     owners = lax.dynamic_index_in_dim(prefix_owner, group_id, 0, keepdims=False)
     quarter = jnp.sum(jnp.where(owners == place, jnp.arange(GSPAN, dtype=jnp.int32), 0))
     prefix_pos = quarter * block_len + jnp.arange(block_len, dtype=jnp.int32)
@@ -136,7 +153,7 @@
     stored_values = prefix_kv[:, 1].reshape(block_len, kv_heads, head_dim)
     blocks = jnp.stack([stored_keys, stored_values], axis=0)
     for bit_pos in range(span_bits):
-        remote = from_partner(blocks, "req", bit_pos)
+        remote = from_partner(blocks, REQ, bit_pos, n_req)
         blocks = jnp.concatenate([blocks, remote], axis=1)
     prefix_state = partial_attention(grouped_queries, blocks[0], blocks[1], None)
     slot_ids = jnp.arange(slots_here, dtype=jnp.int32)
@@ -144,36 +161,44 @@
         slot_ids[None, :] <= slot_ids[:, None]
     )
     suffix_state = partial_attention(grouped_queries, key_rows, value_rows, allowed)
-    merged, peak, weight_sum = combine_states(prefix_state, suffix_state)
+    merged, _, weight_sum = combine_states(prefix_state, suffix_state)
     attended = (
         jnp.transpose(merged / weight_sum[..., None], (2, 0, 1, 3))
         .reshape(slots_here, q_heads * head_dim)
         .astype(jnp.bfloat16)
     )
+
     head_terms = jnp.dot(attended, w_out, preferred_element_type=jnp.float32)
-    head_total = lax.psum(head_terms, "mlp")
-    residual = (hidden_f + head_total).astype(jnp.bfloat16)
+    head_rows = lax.psum_scatter(head_terms, "mlp", scatter_dimension=0, tiled=True)
+    rows_here = slots_here // n_mlp
+    row_start = mlp_index * rows_here
+    hidden_rows = lax.dynamic_slice_in_dim(hidden_f, row_start, rows_here, 0)
+    live_rows = lax.dynamic_slice_in_dim(live, row_start, rows_here, 0)
+    residual = (hidden_rows + head_rows).astype(jnp.bfloat16)
     normed_mlp = rms_norm(residual.astype(jnp.float32), mlp_gain).astype(jnp.bfloat16)
-    width_start = lax.axis_index("mlp") * width_part
-    normed_part = lax.dynamic_slice_in_dim(normed_mlp, width_start, width_part, 1)
-    both_weights = jnp.concatenate([w_gate, w_up], axis=1)
-    partial_sums = jnp.dot(
-        lax.all_gather(normed_part, "req", axis=0, tiled=True),
-        both_weights,
-        preferred_element_type=jnp.float32,
-    )
-    gate_up = lax.psum(partial_sums, "mlp")
-    act = (jax.nn.silu(gate_up[:, :unit_count]) * gate_up[:, unit_count:]).astype(jnp.bfloat16)
+
+    tokens = lax.all_gather(normed_mlp, "rx", axis=0, tiled=True)
+    acts = []
+    for core in range(n_rc):
+        gate_up = jnp.dot(tokens, gate_up_pair[core], preferred_element_type=jnp.float32)
+        gate = gate_up[:, :unit_count]
+        up_part = gate_up[:, unit_count:]
+        acts.append((jax.nn.silu(gate) * up_part).astype(jnp.bfloat16))
+    down_sum = None
+    for core in range(n_rc):
+        term = jnp.einsum(
+            "tu,mud->tmd", acts[core], down_pair[core], preferred_element_type=jnp.float32
+        ).astype(jnp.bfloat16)
+        term = term.reshape(term.shape[0], -1).astype(jnp.float32)
+        down_sum = term if down_sum is None else down_sum + term
     down = lax.psum_scatter(
-        jnp.dot(act, w_down, preferred_element_type=jnp.float32).astype(jnp.bfloat16),
-        "req",
-        scatter_dimension=0,
-        tiled=True,
+        down_sum.astype(jnp.bfloat16), "rx", scatter_dimension=0, tiled=True
     ).astype(jnp.float32)
-    residual_part = lax.dynamic_slice_in_dim(residual, width_start, width_part, 1).astype(
-        jnp.float32
-    )
-    hidden_out = jnp.where(live[:, None], residual_part + down, 0.0).astype(jnp.bfloat16)
+    out_rows = jnp.where(
+        live_rows[:, None], residual.astype(jnp.float32) + down, 0.0
+    ).astype(jnp.bfloat16)
+    hidden_out = lax.all_to_all(out_rows, "mlp", 1, 0, tiled=True)
+
     stacked_kv = jnp.stack(
         [
             key_rows.reshape(slots_here, kv_heads * head_dim),
@@ -186,25 +211,29 @@
 
 
 def solution(mesh):
+    req_size, mlp_size = mesh.devices.shape
+    view = Mesh(
+        np.asarray(mesh.devices).reshape(req_size // 2, 2, mlp_size), ("rx", "rc", "mlp")
+    )
     placed = (
-        P("req", None),
+        P(REQ, None),
         P(),
         P(None, "mlp"),
         P(None, "mlp"),
         P(None, "mlp"),
         P("mlp", None),
         P(),
-        P("mlp", "req"),
-        P("mlp", "req"),
-        P("req", "mlp"),
-        P("req", None, "mlp"),
-        P("req", None),
+        P("mlp", REQ),
+        P("mlp", REQ),
+        P(REQ, "mlp"),
+        P(REQ, None, "mlp"),
+        P(REQ, None),
         P(),
     )
     return jax.shard_map(
-        shards,
-        mesh=mesh,
+        layer,
+        mesh=view,
         in_specs=placed,
-        out_specs=(P("req", "mlp"), P("req", None, "mlp")),
+        out_specs=(P(REQ, "mlp"), P(REQ, None, "mlp")),
         check_vma=False,
     )

time: 614 us -> 430 us (0.70)
  waiting for transfers between devices: 509 us -> 307 us
  local copies, waits for them, and re-layouts: 4.53 us -> 17.2 us
    psum x2 -> x0, waiting for transfers between devices: 322 us -> none  [the longest x1 261 us: shards(): gate_up = lax.psum(partial_sums, 'mlp')]
    all_gather x1 -> x3, waiting for transfers between devices: 52.7 us -> 129 us  [the longest x1 77.1 us: layer(): lax.all_gather(gate_up_part, ('rc', 'mlp'), axis=0, tiled=False)]
    reduce_scatter x1 -> x2, waiting for transfers between devices: 92.2 us -> 130 us  [the longest x1 79 us: layer(): lax.psum_scatter(down_sum.astype(jnp.bfloat16), 'rx', scatter_dimension=0...]
    slice x1 -> x2, local copies, waits for them, and re-layouts: 3.33 us -> 10.3 us  [the longest x1 6.91 us: layer(): down_pair[core]]
    dot_general x6 -> x8, matrix products: 34.5 us -> 32.4 us  [the longest x2 14.8 us: layer(): jnp.dot(tokens, gate_up_pair[core], preferred_element_type=jnp.float32)]
  transfers between devices with their start and end apart: 6 -> 8, of which waited for: 5 -> 7; matrix products, arithmetic and copies ran while one was open for 2% -> 5% of each run, Pallas kernels for 0% -> 0%
where the time goes in v1:
time: 430 us; the launch traced here: 429 us
  waiting for transfers between devices  307 us (71%)
  matrix products  48.6 us (11%)
  other arithmetic  32.8 us (8%)
  local copies, waits for them, and re-layouts  17.2 us (4%)
  between operations  16.8 us (4%)
  starting transfers between devices  6.48 us (2%)
    reduce_scatter x1, waiting for transfers between devices, layer(): lax.psum_scatter(down_sum.astype(jnp.bfloat16), 'rx', scatter_dimension=0...  79 us
    all_gather x1, waiting for transfers between devices, layer(): lax.all_gather(gate_up_part, ('rc', 'mlp'), axis=0, tiled=False)  77.1 us
    reduce_scatter x1, waiting for transfers between devices, layer(): lax.psum_scatter(head_terms, 'mlp', scatter_dimension=0, tiled=True)  51.2 us
    all_gather x1, waiting for transfers between devices, layer(): tokens = lax.all_gather(normed_mlp, 'rx', axis=0, tiled=True)  46.6 us
    ppermute x2, waiting for transfers between devices, from_partner(): return lax.ppermute(value, axis, pairs)  41.7 us
    dot_general x2, matrix products, layer(): jnp.dot(tokens, gate_up_pair[core], preferred_element_type=jnp.float32)  14.8 us
    dot_general x2, matrix products, layer(): jnp.einsum('tu,mud->tmd', acts[core], down_pair[core], preferred_element_...  8.98 us
  transfers between devices with their start and end apart: 8, of which 7 were waited for; matrix products, arithmetic and copies ran while one was open for 5% of the time, Pallas kernels for 0%

profile of v1, /device:TPU:0, one launch (start us, length us, event | category | flops | bytes accessed | tf_op | source)
XLA Modules:
  0.0 429.1 jit_solution(16087997619639087764)
XLA Ops:
  8.0 0.0 reduce-scatter.3.cloned.1.call-start
  8.1 3.4 fusion.78
  11.5 0.1 copy.81
  11.6 0.1 copy_convert_fusion
  11.7 0.2 fusion.67
  11.9 0.6 select_reduce_fusion.1
  13.2 4.8 %fusion.47 = (bf16[1,2048,1,64]{3,1,2,0:T(8,128)(2,1)S(1)}, bf16[1,2048,1,64]{3,1,2,0:T(8,128)(2,1)S(1)}) fusion(f32[2048,1,128]{2,0,1:T(8,128)S(1)} %copy_convert_fusion, f32[64]{0:T(128)S(1)} %multiply_power_fusion, f32[2048]{0:T(1024)S(1)} %add_convert_fusion.3), kind=kLoop, calls=%fused_computation.61 | loop fusion | flops 1179648 | bytes 1581312 | tf_op jit(solution)/shard_map/concatenate | solution.py:35
  18.1 0.8 copy-done.2
  18.9 1.3 pad_maximum_fusion.3
  20.2 0.2 reduce-window.4
  20.4 0.1 convert_reduce_fusion
  20.5 0.1 select_reduce_fusion
  20.5 1.5 multiply_reduce_fusion
  22.1 4.0 fusion.74
  26.1 2.9 pad_maximum_fusion.1
  29.0 2.0 collective-permute-start.1
  31.0 1.0 reshape.485
  32.1 0.1 fusion.53
  32.2 1.9 convolution_bitcast_fusion
  34.1 0.2 fusion.59
  34.3 0.3 multiply_cosine_fusion.1
  34.6 0.2 fusion.79
  34.8 0.1 subtract_convert_fusion
  34.9 0.3 fusion.80
  35.2 0.1 fusion.48
  35.3 0.6 convolution_convert_fusion
  35.9 41.7 %collective-permute-done.1 = bf16[2,4096,1,128]{3,1,2,0:T(8,128)(2,1)} collective-permute-done((bf16[2,4096,1,128]{3,1,2,0:T(8,128)(2,1)}, bf16[2,4096,1,128]{3,1,2,0:T(8,128)(2,1)}, u32[]{:S(2)}, u32[]{:S(2)}) %collective-permute-start.1) | collective-permute-done | bytes 2097184 | tf_op jit(solution)/shard_map/ppermute | solution.py:24
  77.6 5.6 %pad_maximum_fusion = bf16[2,8192,1,128]{3,1,2,0:T(8,128)(2,1)S(1)} fusion(bf16[2,4096,1,128]{3,1,2,0:T(8,128)(2,1)} %collective-permute-done.1, bf16[2,2048,1,128]{3,1,2,0:T(8,128)(2,1)} %collective-permute-done, bf16[1,2048,1,128]{3,1,2,0:T(8,128)(2,1)S(1)} %bitcast.125, bf16[1,2048,1,64]{3,1,2,0:T(8,128)(2,1)S(1)} %copy-done.4, ...), kind=kLoop, calls=%fused_computation.13 | loop fusion | flops 20971520 | bytes 8388608 | tf_op jit(solution)/shard_map/concatenate | solution.py:157
  83.2 8.1 %bitcast_reduce_fusion = (f32[4,128]{1,0:T(4,128)S(1)}, f32[8192,128,4]{1,0,2:T(8,128)}) fusion(bf16[128,4,64]{2,0,1:T(8,128)(2,1)S(1)} %get-tuple-element.20, bf16[128,4,64]{2,0,1:T(8,128)(2,1)S(1)} %get-tuple-element.19, bf16[2,8192,1,128]{3,1,2,0:T(8,128)(2,1)S(1)} %pad_maximum_fusion), kind=kOutput, calls=%fused_computation.1 | convolution fusion | flops 1082392064 | bytes 19138560 | tf_op jit(solution)/shard_map/qkgd,nkd->kgqn/dot_general | solution.py:62
  91.4 8.5 %fusion.1 = f32[4,128]{1,0:T(4,128)S(1)} fusion(f32[8192,128,4]{1,0,2:T(8,128)} %get-tuple-element.30, f32[4,128]{1,0:T(4,128)S(1)} %get-tuple-element.29), kind=kLoop, calls=%fused_computation.3 | loop fusion | flops 12582400 | bytes 16781312 | tf_op jit(solution)/shard_map/reduce_sum | solution.py:69
  99.9 0.2 convolution_multiply_fusion
  100.1 7.6 %fusion.27 = bf16[4,128,128]{1,2,0:T(8,128)(2,1)S(1)} fusion(f32[4,128,128]{1,2,0:T(8,128)S(1)} %convolution_multiply_fusion, bf16[2,8192,1,128]{3,1,2,0:T(8,128)(2,1)S(1)} %pad_maximum_fusion, f32[8192,128,4]{1,0,2:T(8,128)} %get-tuple-element.30, f32[4,128]{1,0:T(4,128)S(1)} %get-tuple-element.29, f32[4,128]{1,0:T(4,128)S(1)} %get-tuple-element.10, ...), kind=kOutput, calls=%fused_computation.36 | convolution fusion | flops 1086586880 | bytes 19273728 | tf_op jit(solution)/shard_map/kgqn,nkd->kgqd/dot_general | solution.py:70
  107.7 2.1 fusion.81
  109.8 0.0 reduce-scatter.3.cloned.1.call-update
  109.8 0.0 all-gather.10.cloned.1.call-start
  109.9 0.5 all-gather.10.cloned.1.call-update
  110.4 0.0 all-gather.6.cloned.1.call-start
  110.5 0.2 convert_element_type.122
  110.7 51.2 %reduce-scatter.3.cloned.1.call-done = f32[32,4096]{1,0:T(8,128)} async-done(((f32[128,4096]{1,0:T(8,128)}), f32[32,4096]{1,0:T(8,128)}) %reduce-scatter.3.cloned.1.call-update) | async-done | bytes 524304 | tf_op jit(solution)/shard_map/reduce_scatter | solution.py:172
  161.9 1.2 fusion.36
  163.1 0.8 fusion.38
  164.0 0.0 all-gather.6.cloned.1.call-update
  164.0 0.0 all-gather.8.cloned.1.call-start
  164.1 2.8 pad_maximum_fusion.2
  166.9 0.0 all-gather.8.cloned.1.call-update
  166.9 0.0 reduce-scatter.5.cloned.1.call-start
  167.0 5.0 %all-gather.10.cloned.1.call-done = bf16[3584,1024]{1,0:T(8,128)(2,1)} async-done(((bf16[448,1024]{1,0:T(8,128)(2,1)}), bf16[3584,1024]{1,0:T(8,128)(2,1)}) %all-gather.10.cloned.1.call-update) | async-done | bytes 7340048 | tf_op jit(solution)/shard_map/all_gather | solution.py:121
  172.0 6.9 %fusion.77 = (bf16[1792,1024]{1,0:T(8,128)(2,1)}, bf16[1792,1024]{1,0:T(8,128)(2,1)}) fusion(bf16[3584,1024]{1,0:T(8,128)(2,1)} %all-gather.10.cloned.1.call-done), kind=kLoop, calls=%fused_computation.116 | loop fusion | bytes 14680064 | tf_op jit(solution)/shard_map/slice | solution.py:190
  178.9 46.6 %all-gather.6.cloned.1.call-done = bf16[512,4096]{1,0:T(8,128)(2,1)} async-done(((bf16[32,4096]{1,0:T(8,128)(2,1)}), bf16[512,4096]{1,0:T(8,128)(2,1)}) %all-gather.6.cloned.1.call-update) | async-done | bytes 4194320 | tf_op jit(solution)/shard_map/all_gather | solution.py:180
  225.5 77.1 %all-gather.8.cloned.1.call-done = bf16[8192,896]{0,1:T(8,128)(2,1)} async-done(((bf16[1024,896]{0,1:T(8,128)(2,1)}), bf16[8192,896]{0,1:T(8,128)(2,1)}) %all-gather.8.cloned.1.call-update) | async-done | bytes 14680080 | tf_op jit(solution)/shard_map/all_gather | solution.py:119
  302.7 10.3 %fusion.8 = f32[512,896]{1,0:T(8,128)S(1)} fusion(bf16[512,4096]{1,0:T(8,128)(2,1)} %all-gather.6.cloned.1.call-done, bf16[8192,896]{0,1:T(8,128)(2,1)} %all-gather.8.cloned.1.call-done), kind=kOutput, calls=%fused_computation.10 | convolution fusion | flops 3758096384 | bytes 13369344 | tf_op jit(solution)/shard_map/dot_general | solution.py:183
  312.9 4.4 %fusion.42 = bf16[512,4,1024]{2,0,1:T(8,128)(2,1)} fusion(bf16[4,448,1024]{2,1,0:T(8,128)(2,1)S(1)} %bitcast.127, f32[512,896]{1,0:T(8,128)S(1)} %fusion.8), kind=kOutput, calls=%fused_computation.57 | convolution fusion | flops 1880424448 | bytes 9961472 | tf_op jit(solution)/shard_map/tu,mud->tmd/dot_general | solution.py:189
  317.4 4.5 %fusion.6 = f32[512,896]{1,0:T(8,128)S(1)} fusion(bf16[512,4096]{1,0:T(8,128)(2,1)S(1)} %copy-done.13, bf16[8192,896]{0,1:T(8,128)(2,1)S(1)} %bitcast.135), kind=kOutput, calls=%fused_computation.8 | convolution fusion | flops 3758096384 | bytes 13369344 | tf_op jit(solution)/shard_map/dot_general | solution.py:183
  321.9 4.6 %fusion.10 = bf16[4,64,8,1024]{3,2,1,0:T(8,128)(2,1)S(1)} fusion(bf16[512,4,1024]{2,0,1:T(8,128)(2,1)} %fusion.42, bf16[4,448,1024]{2,1,0:T(8,128)(2,1)S(1)} %bitcast.126, f32[512,896]{1,0:T(8,128)S(1)} %fusion.6), kind=kOutput, calls=%fused_computation.12 | convolution fusion | flops 1890910208 | bytes 14155776 | tf_op jit(solution)/shard_map/tu,mud->tmd/dot_general | solution.py:189
  326.5 2.4 copy.73
  328.9 0.0 reduce-scatter.5.cloned.1.call-update
  329.0 0.1 dynamic_slice.10
  329.0 79.0 %reduce-scatter.5.cloned.1.call-done = bf16[32,4096]{1,0:T(8,128)(2,1)} async-done(((bf16[512,4096]{1,0:T(8,128)(2,1)}), bf16[32,4096]{1,0:T(8,128)(2,1)}) %reduce-scatter.5.cloned.1.call-update) | async-done | bytes 262160 | tf_op jit(solution)/shard_map/reduce_scatter | solution.py:194
  408.0 1.0 fusion.40
  409.1 0.7 copy.82
  409.8 4.2 all-to-all-start
  414.1 0.8 copy.56
  414.8 5.9 %all-to-all-done = bf16[32,4,1024]{2,0,1:T(8,128)(2,1)S(1)} async-done(((bf16[32,4,1024]{2,0,1:T(8,128)(2,1)}), bf16[32,4,1024]{2,0,1:T(8,128)(2,1)S(1)}, u32[]{:S(2)}, u32[]{:S(2)}) %all-to-all-start) | async-done | bytes 262176 | tf_op jit(solution)/shard_map/all_to_all | solution.py:200
  420.7 0.7 copy.84
  (53 shorter events, 0.2 us)
Async XLA Ops:
  8.0 24.1 %copy-start = (bf16[4096,128]{1,0:T(8,128)(2,1)S(1)}, bf16[4096,128]{1,0:T(8,128)(2,1)}, u32[]{:S(2)}) copy-start(bf16[4096,128]{1,0:T(8,128)(2,1)} %param.16) | copy-start | bytes 3145732
  8.0 3.7 copy-start.12
  8.0 153.9 %reduce-scatter.3.cloned.1.call-start = ((), (), s32[]{:S(2)}) async-start(), calls=%async_computation.3 | async-start | bytes 2621440 | tf_op jit(solution)/shard_map/reduce_scatter | solution.py:172
  11.6 8.6 %copy-start.15 = (s32[1,4]{1,0:T(1,128)S(1)}, s32[1,4]{1,0:T(1,128)}, u32[]{:S(2)}) copy-start(s32[1,4]{1,0:T(1,128)} %param.24) | copy-start | bytes 52
  11.6 8.8 %copy-start.10 = (bf16[4096]{0:T(1024)(128)(2,1)S(1)}, bf16[4096]{0:T(1024)(128)(2,1)}, u32[]{:S(2)}) copy-start(bf16[4096]{0:T(1024)(128)(2,1)} %param.14) | copy-start | bytes 24580
  18.1 0.8 copy-start.2
  20.2 5.9 %copy-start.3 = (bf16[1,2048,1,64]{3,1,2,0:T(8,128)(2,1)S(1)}, bf16[1,2048,1,64]{3,1,2,0:T(8,128)(2,1)}, u32[]{:S(2)}) copy-start(bf16[1,2048,1,64]{3,1,2,0:T(8,128)(2,1)} %copy-done.2) | copy-start | bytes 786436
  20.2 5.9 %collective-permute-start = (bf16[2,2048,1,128]{3,1,2,0:T(8,128)(2,1)}, bf16[2,2048,1,128]{3,1,2,0:T(8,128)(2,1)}, u32[]{:S(2)}, u32[]{:S(2)}) collective-permute-start(bf16[2,2048,1,128]{3,1,2,0:T(8,128)(2,1)} %pad_maximum_fusion.3), channel_id=1, source_target_pairs={{0,4},{4,0},{8,12},{12,8},{16,20},{20,16},{24,28},{28,24},{32,36},... | collective-permute-start | bytes 3145736 | tf_op jit(solution)/shard_map/ppermute | solution.py:24
  29.0 6.3 %copy-start.5 = (bf16[128,4096]{1,0:T(8,128)(2,1)S(1)}, bf16[128,4096]{1,0:T(8,128)(2,1)}, u32[]{:S(2)}) copy-start(bf16[128,4096]{1,0:T(8,128)(2,1)} %param.13) | copy-start | bytes 3145732
  29.0 48.6 %collective-permute-start.1 = (bf16[2,4096,1,128]{3,1,2,0:T(8,128)(2,1)}, bf16[2,4096,1,128]{3,1,2,0:T(8,128)(2,1)}, u32[]{:S(2)}, u32[]{:S(2)}) collective-permute-start(bf16[2,4096,1,128]{3,1,2,0:T(8,128)(2,1)} %pad_maximum_fusion.1), channel_id=1, source_target_pairs={{0,8},{4,12},{8,0},{12,4},{16,24},{20,28},{24,16},{28,20},{32,40},... | collective-permute-start | bytes 6291464 | tf_op jit(solution)/shard_map/ppermute | solution.py:24
  32.0 3.2 copy-start.14
  32.0 45.6 %copy-start.4 = (bf16[1,2048,1,64]{3,1,2,0:T(8,128)(2,1)S(1)}, bf16[1,2048,1,64]{3,1,2,0:T(8,128)(2,1)}, u32[]{:S(2)}) copy-start(bf16[1,2048,1,64]{3,1,2,0:T(8,128)(2,1)} %copy-done.2) | copy-start | bytes 786436
  100.1 7.6 %copy-start.7 = (bf16[512,4096]{1,0:T(8,128)(2,1)S(1)}, bf16[512,4096]{1,0:T(8,128)(2,1)}, u32[]{:S(2)}) copy-start(bf16[512,4096]{1,0:T(8,128)(2,1)} %param.18) | copy-start | bytes 12582916
  107.7 2.8 copy-start.6
  109.8 0.9 copy-start.11
  109.8 62.1 %all-gather.10.cloned.1.call-start = ((), (), s32[]{:S(2)}) async-start(), calls=%async_computation.7 | async-start | bytes 8257536 | tf_op jit(solution)/shard_map/all_gather | solution.py:121
  110.4 115.1 %all-gather.6.cloned.1.call-start = ((), (), s32[]{:S(2)}) async-start(), calls=%async_computation.4 | async-start | bytes 4456448 | tf_op jit(solution)/shard_map/all_gather | solution.py:180
  164.0 138.6 %all-gather.8.cloned.1.call-start = ((), (), s32[]{:S(2)}) async-start(), calls=%async_computation.6 | async-start | bytes 16515072 | tf_op jit(solution)/shard_map/all_gather | solution.py:119
  166.9 241.1 %reduce-scatter.5.cloned.1.call-start = ((), (), s32[]{:S(2)}) async-start(), calls=%async_computation.5 | async-start | bytes 4456448 | tf_op jit(solution)/shard_map/reduce_scatter | solution.py:194
  302.6 10.3 %copy-start.9 = (bf16[1792,1024]{1,0:T(8,128)(2,1)S(1)}, bf16[1792,1024]{1,0:T(8,128)(2,1)}, u32[]{:S(2)}) copy-start(bf16[1792,1024]{1,0:T(8,128)(2,1)} %get-tuple-element.14) | copy-start | bytes 11010052
  302.6 14.7 %slice-start = ((s8[14680064]{0:T(1024)(128)(4,1)}), s8[4194304]{0:T(1024)(128)(4,1)S(1)}, s32[]{:S(2)}) async-start(s8[14680064]{0:T(1024)(128)(4,1)} %bitcast.134), calls=%async_computation.8 | async-start | bytes 8388608
  302.7 14.7 %slice-start.1 = ((s8[14680064]{0:T(1024)(128)(4,1)}), s8[4194304]{0:T(1024)(128)(4,1)S(1)}, s32[]{:S(2)}) async-start(s8[14680064]{0:T(1024)(128)(4,1)} %bitcast.134), calls=%async_computation.9 | async-start | bytes 8388608
  302.7 14.7 %slice-start.2 = ((s8[14680064]{0:T(1024)(128)(4,1)}), s8[4194304]{0:T(1024)(128)(4,1)S(1)}, s32[]{:S(2)}) async-start(s8[14680064]{0:T(1024)(128)(4,1)} %bitcast.134), calls=%async_computation.10 | async-start | bytes 8388608
  312.9 4.4 %slice-start.3 = ((s8[14680064]{0:T(1024)(128)(4,1)}), s8[2097152]{0:T(1024)(128)(4,1)S(1)}, s32[]{:S(2)}) async-start(s8[14680064]{0:T(1024)(128)(4,1)} %bitcast.134), calls=%async_computation.11 | async-start | bytes 4194304
  312.9 4.4 %copy-start.13 = (bf16[512,4096]{1,0:T(8,128)(2,1)S(1)}, bf16[512,4096]{1,0:T(8,128)(2,1)}, u32[]{:S(2)}) copy-start(bf16[512,4096]{1,0:T(8,128)(2,1)} %all-gather.6.cloned.1.call-done) | copy-start | bytes 12582916
  317.4 4.5 %copy-start.8 = (bf16[1792,1024]{1,0:T(8,128)(2,1)S(1)}, bf16[1792,1024]{1,0:T(8,128)(2,1)}, u32[]{:S(2)}) copy-start(bf16[1792,1024]{1,0:T(8,128)(2,1)} %get-tuple-element.13) | copy-start | bytes 11010052
  326.5 94.9 %copy-start.1 = (bf16[4096,128]{1,0:T(8,128)(2,1)S(1)}, bf16[4096,128]{1,0:T(8,128)(2,1)}, u32[]{:S(2)}) copy-start(bf16[4096,128]{1,0:T(8,128)(2,1)} %param.16) | copy-start | bytes 3145732
  409.8 10.9 %all-to-all-start = ((bf16[32,4,1024]{2,0,1:T(8,128)(2,1)}), bf16[32,4,1024]{2,0,1:T(8,128)(2,1)S(1)}, u32[]{:S(2)}, u32[]{:S(2)}) async-start(bf16[32,4,1024]{2,0,1:T(8,128)(2,1)} %bitcast.121), calls=%async_computation.2 | async-start | bytes 524288 | tf_op jit(solution)/shard_map/all_to_all | solution.py:200
Sparse Core Ops, SparseCore 0:
  110.0 51.9 reduce-scatter.2
Sparse Core Ops, SparseCore 1:
  112.0 59.9 all-gather.9
  174.6 50.9 all-gather.5
  227.1 75.5 all-gather.7
  329.0 79.0 reduce-scatter.4

commit v2 on v1

--- a/solution.py
+++ b/solution.py
@@ -12,16 +12,14 @@
 PREFIX = 8192
 GSPAN = 4
 
-REQ = ("rx", "rc")
+REQ = ("ax", "az", "rc")
 
 rope_base = 500000.0
 eps = 1e-05
 
 
-def from_partner(value, axis, stride, size):
-    mask = 2**stride
-    pairs = [(source, source ^ mask) for source in range(size)]
-    return lax.ppermute(value, axis, pairs)
+def swap_with_partner(value, axis, size):
+    return lax.ppermute(value, axis, [(source, source ^ 1) for source in range(size)])
 
 
 def rope(values, positions):
@@ -73,15 +71,22 @@
         value_block,
         preferred_element_type=jnp.float32,
     )
-    return (summed, peak, weight_sum)
+    return jnp.concatenate([summed, peak[..., None], weight_sum[..., None]], axis=-1)
 
 
 def combine_states(former, latter):
-    peak = jnp.maximum(former[1], latter[1])
-    scale_former = jnp.exp(former[1] - peak)
-    scale_latter = jnp.exp(latter[1] - peak)
-    summed = former[0] * scale_former[..., None] + latter[0] * scale_latter[..., None]
-    return (summed, peak, former[2] * scale_former + latter[2] * scale_latter)
+    head_dim = former.shape[-1] - 2
+    peak = jnp.maximum(former[..., head_dim], latter[..., head_dim])
+    scale_former = jnp.exp(former[..., head_dim] - peak)
+    scale_latter = jnp.exp(latter[..., head_dim] - peak)
+    summed = (
+        former[..., :head_dim] * scale_former[..., None]
+        + latter[..., :head_dim] * scale_latter[..., None]
+    )
+    weight_sum = (
+        former[..., head_dim + 1] * scale_former + latter[..., head_dim + 1] * scale_latter
+    )
+    return jnp.concatenate([summed, peak[..., None], weight_sum[..., None]], axis=-1)
 
 
 def layer(
@@ -105,16 +110,16 @@
     q_heads = w_query.shape[1] // head_dim
     group = q_heads // kv_heads
     block_len = prefix_kv.shape[0]
-    span_bits = GSPAN.bit_length() - 1
     unit_count = w_gate.shape[1]
-    n_rx = lax.axis_size("rx")
+    width_part = w_gate.shape[0]
+    n_az = lax.axis_size("az")
     n_rc = lax.axis_size("rc")
     n_mlp = lax.axis_size("mlp")
-    n_req = n_rx * n_rc
-    req_index = lax.axis_index("rx") * n_rc + lax.axis_index("rc")
+    az_index = lax.axis_index("az")
+    rc_index = lax.axis_index("rc")
+    req_index = (lax.axis_index("ax") * n_az + az_index) * n_rc + rc_index
     mlp_index = lax.axis_index("mlp")
 
-    width_part = w_gate.shape[0]
     gate_up_part = jnp.concatenate([w_gate, w_up], axis=1)
     gate_up_pair = lax.all_gather(gate_up_part, ("rc", "mlp"), axis=0, tiled=False)
     gate_up_pair = gate_up_pair.reshape(n_rc, n_mlp * width_part, 2 * unit_count)
@@ -142,6 +147,7 @@
         .reshape(slots_here, kv_heads, head_dim)
     )
     grouped_queries = query_rows.reshape(slots_here, kv_heads, group, head_dim)
+
     place = req_index % GSPAN
     group_id = req_index // GSPAN
     owners = lax.dynamic_index_in_dim(prefix_owner, group_id, 0, keepdims=False)
@@ -151,19 +157,41 @@
         prefix_kv[:, 0].reshape(block_len, kv_heads, head_dim).astype(jnp.float32), prefix_pos
     ).astype(jnp.bfloat16)
     stored_values = prefix_kv[:, 1].reshape(block_len, kv_heads, head_dim)
-    blocks = jnp.stack([stored_keys, stored_values], axis=0)
-    for bit_pos in range(span_bits):
-        remote = from_partner(blocks, REQ, bit_pos, n_req)
-        blocks = jnp.concatenate([blocks, remote], axis=1)
-    prefix_state = partial_attention(grouped_queries, blocks[0], blocks[1], None)
+
+    z_bit = az_index % 2
+    core_other = swap_with_partner(grouped_queries, "rc", n_rc)
+    pair = jnp.where(
+        rc_index == 0,
+        jnp.stack([grouped_queries, core_other]),
+        jnp.stack([core_other, grouped_queries]),
+    )
+    z_other = swap_with_partner(pair, "az", n_az)
+    group_queries = jnp.where(
+        z_bit == 0, jnp.concatenate([pair, z_other]), jnp.concatenate([z_other, pair])
+    )
+    runs = group_queries.shape[0]
+    states = partial_attention(
+        group_queries.reshape(runs * slots_here, kv_heads, group, head_dim),
+        stored_keys,
+        stored_values,
+        None,
+    )
+    states = states.reshape(kv_heads, group, runs, slots_here, head_dim + 2)
+    keep = lax.dynamic_slice_in_dim(states, z_bit * 2, 2, 2)
+    send = lax.dynamic_slice_in_dim(states, (1 - z_bit) * 2, 2, 2)
+    states = combine_states(keep, swap_with_partner(send, "az", n_az))
+    keep = lax.dynamic_slice_in_dim(states, rc_index, 1, 2)
+    send = lax.dynamic_slice_in_dim(states, 1 - rc_index, 1, 2)
+    prefix_state = combine_states(keep, swap_with_partner(send, "rc", n_rc))[:, :, 0]
+
     slot_ids = jnp.arange(slots_here, dtype=jnp.int32)
     allowed = (request_of[:, None] == request_of[None, :]) & (
         slot_ids[None, :] <= slot_ids[:, None]
     )
     suffix_state = partial_attention(grouped_queries, key_rows, value_rows, allowed)
-    merged, _, weight_sum = combine_states(prefix_state, suffix_state)
+    merged = combine_states(prefix_state, suffix_state)
     attended = (
-        jnp.transpose(merged / weight_sum[..., None], (2, 0, 1, 3))
+        jnp.transpose(merged[..., :head_dim] / merged[..., head_dim + 1 :], (2, 0, 1, 3))
         .reshape(slots_here, q_heads * head_dim)
         .astype(jnp.bfloat16)
     )
@@ -177,7 +205,8 @@
     residual = (hidden_rows + head_rows).astype(jnp.bfloat16)
     normed_mlp = rms_norm(residual.astype(jnp.float32), mlp_gain).astype(jnp.bfloat16)
 
-    tokens = lax.all_gather(normed_mlp, "rx", axis=0, tiled=True)
+    tokens = lax.all_gather(normed_mlp, "az", axis=0, tiled=True)
+    tokens = lax.all_gather(tokens, "ax", axis=0, tiled=True)
     acts = []
     for core in range(n_rc):
         gate_up = jnp.dot(tokens, gate_up_pair[core], preferred_element_type=jnp.float32)
@@ -191,9 +220,8 @@
         ).astype(jnp.bfloat16)
         term = term.reshape(term.shape[0], -1).astype(jnp.float32)
         down_sum = term if down_sum is None else down_sum + term
-    down = lax.psum_scatter(
-        down_sum.astype(jnp.bfloat16), "rx", scatter_dimension=0, tiled=True
-    ).astype(jnp.float32)
+    down = lax.psum_scatter(down_sum.astype(jnp.bfloat16), "ax", scatter_dimension=0, tiled=True)
+    down = lax.psum_scatter(down, "az", scatter_dimension=0, tiled=True).astype(jnp.float32)
     out_rows = jnp.where(
         live_rows[:, None], residual.astype(jnp.float32) + down, 0.0
     ).astype(jnp.bfloat16)
@@ -212,8 +240,9 @@
 
 def solution(mesh):
     req_size, mlp_size = mesh.devices.shape
+    x_size = req_size // 8
     view = Mesh(
-        np.asarray(mesh.devices).reshape(req_size // 2, 2, mlp_size), ("rx", "rc", "mlp")
+        np.asarray(mesh.devices).reshape(x_size, 4, 2, mlp_size), ("ax", "az", "rc", "mlp")
     )
     placed = (
         P(REQ, None),

time: 430 us -> 441 us (1.026)
  waiting for transfers between devices: 307 us -> 317 us
    all_gather x1, waiting for transfers between devices: 4.99 us -> 45.5 us  [layer(): down_pair = lax.all_gather(w_down, ('rc', 'mlp'), axis=0, tiled=False)]
    ppermute x2 -> x4, waiting for transfers between devices: 41.7 us -> 16.5 us  [swap_with_partner(): lax.ppermute(value, axis, [(source, source ^ 1) for source in range(size)])]
    reduce_scatter x1, waiting for transfers between devices: 51.2 us -> 30.2 us  [layer(): lax.psum_scatter(head_terms, 'mlp', scatter_dimension=0, tiled=True)]
    all_gather x1 -> x2, waiting for transfers between devices: 46.6 us -> 66.3 us  [the longest x1 42.9 us: layer(): tokens = lax.all_gather(tokens, 'ax', axis=0, tiled=True)]
    convert_element_type x0 -> x1, other arithmetic: none -> 10.4 us  [partial_attention(): weights.astype(jnp.bfloat16)]
    reduce_sum x2 -> x1, other arithmetic: 8.56 us -> 0.06 us  [partial_attention(): weight_sum = jnp.sum(weights, axis=-1)]
    concatenate x2, other arithmetic: 8.49 us -> 0.13 us  [the longest x1 0.09 us: partial_attention(): jnp.concatenate([summed, peak[..., None], weight_sum[..., None]], axis=-1)]
    reduce_scatter x1 -> x2, waiting for transfers between devices: 79 us -> 73.4 us  [the longest x1 47.4 us: layer(): lax.psum_scatter(down_sum.astype(jnp.bfloat16), 'ax', scatter_dimension=0...]
  transfers between devices with their start and end apart: 8 -> 12, of which waited for: 7 -> 11; matrix products, arithmetic and copies ran while one was open for 5% -> 6% of each run, Pallas kernels for 0% -> 0%
where the time goes in v2:
time: 441 us; the launch traced here: 440 us
  waiting for transfers between devices  317 us (72%)
  matrix products  50.7 us (11%)
  other arithmetic  31.2 us (7%)
  local copies, waits for them, and re-layouts  17.7 us (4%)
  between operations  15.3 us (3%)
  starting transfers between devices  8.69 us (2%)
    all_gather x1, waiting for transfers between devices, layer(): lax.all_gather(gate_up_part, ('rc', 'mlp'), axis=0, tiled=False)  78 us
    reduce_scatter x1, waiting for transfers between devices, layer(): lax.psum_scatter(down_sum.astype(jnp.bfloat16), 'ax', scatter_dimension=0...  47.4 us
    all_gather x1, waiting for transfers between devices, layer(): down_pair = lax.all_gather(w_down, ('rc', 'mlp'), axis=0, tiled=False)  45.5 us
    all_gather x1, waiting for transfers between devices, layer(): tokens = lax.all_gather(tokens, 'ax', axis=0, tiled=True)  42.9 us
    reduce_scatter x1, waiting for transfers between devices, layer(): lax.psum_scatter(head_terms, 'mlp', scatter_dimension=0, tiled=True)  30.2 us
    reduce_scatter x1, waiting for transfers between devices, layer(): lax.psum_scatter(down, 'az', scatter_dimension=0, tiled=True)  26 us
    all_gather x1, waiting for transfers between devices, layer(): tokens = lax.all_gather(normed_mlp, 'az', axis=0, tiled=True)  23.4 us
    ppermute x4, waiting for transfers between devices, swap_with_partner(): lax.ppermute(value, axis, [(source, source ^ 1) for source in range(size)])  16.5 us
  transfers between devices with their start and end apart: 12, of which 11 were waited for; matrix products, arithmetic and copies ran while one was open for 6% of the time, Pallas kernels for 0%

profile of v2, /device:TPU:0, one launch (start us, length us, event | category | flops | bytes accessed | tf_op | source)
XLA Modules:
  0.0 440.2 jit_solution(2886697499610472031)
XLA Ops:
  7.3 0.8 convert_element_type.139
  8.0 1.5 multiply_reduce_fusion
  9.6 0.6 copy-done.22
  10.1 3.3 fusion.75
  13.5 0.1 reshape.700
  13.6 0.2 fusion.81
  13.8 0.2 reduce-window.4
  14.0 0.1 convert_reduce_fusion
  14.1 0.1 select_reduce_fusion
  14.2 0.5 copy-done.17
  14.7 0.3 multiply_cosine_fusion.1
  15.1 0.8 pad_maximum_fusion.3
  15.8 2.3 fusion.79
  18.2 0.9 fusion.69
  19.2 0.7 select_reduce_fusion.1
  20.5 6.3 %fusion.40 = (bf16[2048,64]{1,0:T(8,128)(2,1)}, bf16[2048,64]{1,0:T(8,128)(2,1)}) fusion(f32[2048,1,128]{2,0,1:T(8,128)S(1)} %copy_convert_fusion, f32[64]{0:T(128)} %copy-done.13, f32[2048]{0:T(1024)S(1)} %add_convert_fusion.3), kind=kLoop, calls=%fused_computation.64 | loop fusion | flops 1179648 | bytes 1581312 | tf_op jit(solution)/shard_map/concatenate | solution.py:33
  26.8 0.1 maximum_bitcast_fusion.3
  26.9 0.7 maximum_select_fusion.1
  27.6 2.0 collective-permute-start.1
  29.7 1.3 convolution_bitcast_fusion.1
  31.0 1.8 copy.86
  32.8 0.2 fusion.56
  33.0 3.9 collective-permute-done.1
  37.0 1.3 maximum_select_fusion
  38.3 9.2 %bitcast_reduce_fusion = (f32[4,512]{1,0:T(4,128)S(1)}, f32[2048,512,4]{0,1,2:T(8,128)}) fusion(bf16[512,4,128]{2,0,1:T(8,128)(2,1)S(1)} %bitcast.123, bf16[2048,64]{1,0:T(8,128)(2,1)} %get-tuple-element.28, bf16[2048,64]{1,0:T(8,128)(2,1)S(1)} %copy-done.9), kind=kOutput, calls=%fused_computation.1 | convolution fusion | flops 1083176960 | bytes 17833984 | tf_op jit(solution)/shard_map/qkgd,nkd->kgqn/dot_general | solution.py:60
  47.6 10.4 %fusion.2 = (bf16[1,4,512,2048]{3,2,1,0:T(8,128)(2,1)}, f32[4,512]{1,0:T(4,128)S(1)}) fusion(f32[2048,512,4]{0,1,2:T(8,128)} %get-tuple-element.42, f32[4,512]{1,0:T(4,128)S(1)} %get-tuple-element.41), kind=kLoop, calls=%fused_computation.4 | loop fusion | flops 16775168 | bytes 25182208 | tf_op jit(solution)/shard_map/convert_element_type | solution.py:70
  58.0 6.3 %convolution_bitcast_fusion = f32[1,4,4,128,128]{3,4,2,1,0:T(8,128)S(1)} fusion(bf16[4,4,128,2048]{3,2,1,0:T(8,128)(2,1)} %bitcast.119, bf16[2048,1,128]{0,2,1:T(8,128)(2,1)S(1)} %copy-done.8), kind=kOutput, calls=%fused_computation.20 | convolution fusion | flops 1073741824 | bytes 9961472 | tf_op jit(solution)/shard_map/kgqn,nkd->kgqd/dot_general | solution.py:68
  64.3 0.1 pad_maximum_fusion.1
  64.4 0.2 copy.62
  64.6 1.8 collective-permute-start.2
  66.5 0.1 fusion.50
  66.6 0.3 fusion.82
  66.9 11.7 %collective-permute-done.2 = f32[1,4,2,128,130]{3,1,4,2,0:T(4,128)S(1)} collective-permute-done((f32[1,4,2,128,130]{3,1,4,2,0:T(4,128)S(1)}, f32[1,4,2,128,130]{3,1,4,2,0:T(4,128)S(1)}, u32[]{:S(2)}, u32[]{:S(2)}) %collective-permute-start.2) | collective-permute-done | bytes 532512 | tf_op jit(solution)/shard_map/ppermute | solution.py:22
  78.9 0.1 collective-permute-start.3
  79.0 0.6 convolution_convert_fusion
  79.7 0.9 collective-permute-done.3
  80.7 0.2 fusion.16
  80.9 0.1 copy-done.3
  81.0 2.1 fusion.83
  83.2 1.5 convert_element_type.136
  84.8 30.2 %reduce-scatter.4.cloned.1.call-done = f32[32,4096]{1,0:T(8,128)} async-done(((f32[128,4096]{1,0:T(8,128)}), f32[32,4096]{1,0:T(8,128)}) %reduce-scatter.4.cloned.1.call-update) | async-done | bytes 524304 | tf_op jit(solution)/shard_map/reduce_scatter | solution.py:200
  114.9 1.4 fusion.24
  116.3 0.8 fusion.26
  117.2 0.7 all-gather.13.cloned.1.call-update
  118.0 23.4 %all-gather.7.cloned.1.call-done = bf16[128,4096]{1,0:T(8,128)(2,1)} async-done(((bf16[32,4096]{1,0:T(8,128)(2,1)}), bf16[128,4096]{1,0:T(8,128)(2,1)}) %all-gather.7.cloned.1.call-update) | async-done | bytes 1048592 | tf_op jit(solution)/shard_map/all_gather | solution.py:208
  141.5 1.4 pad_maximum_fusion
  142.9 0.2 reduce-scatter.6.cloned.1.call-start
  143.1 45.5 %all-gather.13.cloned.1.call-done = bf16[3584,1024]{1,0:T(8,128)(2,1)} async-done(((bf16[448,1024]{1,0:T(8,128)(2,1)}), bf16[3584,1024]{1,0:T(8,128)(2,1)}) %all-gather.13.cloned.1.call-update) | async-done | bytes 7340048 | tf_op jit(solution)/shard_map/all_gather | solution.py:126
  188.6 6.9 %fusion.78 = (bf16[1792,1024]{1,0:T(8,128)(2,1)}, bf16[1792,1024]{1,0:T(8,128)(2,1)}) fusion(bf16[3584,1024]{1,0:T(8,128)(2,1)} %all-gather.13.cloned.1.call-done), kind=kLoop, calls=%fused_computation.147 | loop fusion | bytes 14680064 | tf_op jit(solution)/shard_map/slice | solution.py:219
  195.5 42.9 %all-gather.9.cloned.1.call-done = bf16[512,4096]{1,0:T(8,128)(2,1)} async-done(((bf16[128,4096]{1,0:T(8,128)(2,1)}), bf16[512,4096]{1,0:T(8,128)(2,1)}) %all-gather.9.cloned.1.call-update) | async-done | bytes 4194320 | tf_op jit(solution)/shard_map/all_gather | solution.py:209
  238.4 78.0 %all-gather.11.cloned.1.call-done = bf16[8192,896]{0,1:T(8,128)(2,1)} async-done(((bf16[1024,896]{0,1:T(8,128)(2,1)}), bf16[8192,896]{0,1:T(8,128)(2,1)}) %all-gather.11.cloned.1.call-update) | async-done | bytes 14680080 | tf_op jit(solution)/shard_map/all_gather | solution.py:124
  316.5 10.3 %fusion.5 = f32[512,896]{1,0:T(8,128)} fusion(bf16[512,4096]{1,0:T(8,128)(2,1)} %all-gather.9.cloned.1.call-done, bf16[8192,896]{0,1:T(8,128)(2,1)} %all-gather.11.cloned.1.call-done), kind=kOutput, calls=%fused_computation.8 | convolution fusion | flops 3758096384 | bytes 13369344 | tf_op jit(solution)/shard_map/dot_general | solution.py:212
  326.7 6.1 %fusion.35 = bf16[512,4,1024]{2,0,1:T(8,128)(2,1)} fusion(bf16[4,448,1024]{2,1,0:T(8,128)(2,1)S(1)} %bitcast.122, f32[512,896]{1,0:T(8,128)} %fusion.5), kind=kOutput, calls=%fused_computation.60 | convolution fusion | flops 1880424448 | bytes 9961472 | tf_op jit(solution)/shard_map/tu,mud->tmd/dot_general | solution.py:218
  332.9 5.8 %fusion.3 = f32[512,896]{1,0:T(8,128)} fusion(bf16[512,4096]{1,0:T(8,128)(2,1)S(1)} %copy-done.19, bf16[8192,896]{0,1:T(8,128)(2,1)S(1)} %bitcast.145), kind=kOutput, calls=%fused_computation.6 | convolution fusion | flops 3758096384 | bytes 13369344 | tf_op jit(solution)/shard_map/dot_general | solution.py:212
  338.6 5.2 %fusion.7 = bf16[4,64,8,1024]{3,2,1,0:T(8,128)(2,1)S(1)} fusion(bf16[512,4,1024]{2,0,1:T(8,128)(2,1)} %fusion.35, bf16[4,448,1024]{2,1,0:T(8,128)(2,1)S(1)} %bitcast.121, f32[512,896]{1,0:T(8,128)} %fusion.3), kind=kOutput, calls=%fused_computation.10 | convolution fusion | flops 1890910208 | bytes 14155776 | tf_op jit(solution)/shard_map/tu,mud->tmd/dot_general | solution.py:218
  343.9 2.4 copy.91
  346.4 47.4 %reduce-scatter.6.cloned.1.call-done = bf16[128,4096]{1,0:T(8,128)(2,1)} async-done(((bf16[512,4096]{1,0:T(8,128)(2,1)}), bf16[128,4096]{1,0:T(8,128)(2,1)}) %reduce-scatter.6.cloned.1.call-update) | async-done | bytes 1048592 | tf_op jit(solution)/shard_map/reduce_scatter | solution.py:223
  393.9 26.0 %reduce-scatter.8.cloned.1.call-done = bf16[32,4096]{1,0:T(8,128)(2,1)} async-done(((bf16[128,4096]{1,0:T(8,128)(2,1)}), bf16[32,4096]{1,0:T(8,128)(2,1)}) %reduce-scatter.8.cloned.1.call-update) | async-done | bytes 262160 | tf_op jit(solution)/shard_map/reduce_scatter | solution.py:224
  419.9 1.0 fusion.28
  421.0 0.7 copy.108
  421.7 4.3 all-to-all-start
  426.0 0.8 copy.73
  426.8 5.9 %all-to-all-done = bf16[32,4,1024]{2,0,1:T(8,128)(2,1)S(1)} async-done(((bf16[32,4,1024]{2,0,1:T(8,128)(2,1)}), bf16[32,4,1024]{2,0,1:T(8,128)(2,1)S(1)}, u32[]{:S(2)}, u32[]{:S(2)}) %all-to-all-start) | async-done | bytes 262176 | tf_op jit(solution)/shard_map/all_to_all | solution.py:228
  432.7 0.7 copy.110
  (95 shorter events, 1.3 us)
Async XLA Ops:
  7.2 22.5 %copy-start = (bf16[4096,128]{1,0:T(8,128)(2,1)S(1)}, bf16[4096,128]{1,0:T(8,128)(2,1)}, u32[]{:S(2)}) copy-start(bf16[4096,128]{1,0:T(8,128)(2,1)} %param.16) | copy-start | bytes 3145732
  7.2 107.8 %reduce-scatter.4.cloned.1.call-start = ((), (), s32[]{:S(2)}) async-start(), calls=%async_computation.4 | async-start | bytes 2621440 | tf_op jit(solution)/shard_map/reduce_scatter | solution.py:200
  7.2 7.4 %copy-start.13 = (f32[64]{0:T(128)}, f32[64]{0:T(128)S(1)}, u32[]{:S(2)}) copy-start(f32[64]{0:T(128)S(1)} %multiply_power_fusion) | copy-start | bytes 772
  9.5 4.2 copy-start.21
  9.6 0.6 copy-start.22
  10.1 5.7 %copy-start.4 = (bf16[2048,2,128]{2,1,0:T(2,128)(2,1)S(1)}, bf16[2048,2,128]{2,1,0:T(2,128)(2,1)}, u32[]{:S(2)}) copy-start(bf16[2048,2,128]{2,1,0:T(2,128)(2,1)} %param.23) | copy-start | bytes 3145732
  14.1 0.6 copy-start.17
  14.7 3.5 copy-start.15
  15.8 11.1 %collective-permute-start = (bf16[128,1,4,128]{3,0,2,1:T(8,128)(2,1)}, bf16[128,1,4,128]{3,0,2,1:T(8,128)(2,1)S(1)}, u32[]{:S(2)}, u32[]{:S(2)}) collective-permute-start(bf16[128,1,4,128]{3,0,2,1:T(8,128)(2,1)} %pad_maximum_fusion.3), channel_id=1, source_target_pairs={{0,4},{4,0},{1,5},{5,1},{2,6},{6,2},{3,7},{7,3},{8,12},{12,8},{9,1... | collective-permute-start | bytes 393224 | tf_op jit(solution)/shard_map/ppermute | solution.py:22
  18.1 11.6 %copy-start.2 = (bf16[128,4096]{1,0:T(8,128)(2,1)S(1)}, bf16[128,4096]{1,0:T(8,128)(2,1)}, u32[]{:S(2)}) copy-start(bf16[128,4096]{1,0:T(8,128)(2,1)} %param.13) | copy-start | bytes 3145732
  26.8 4.2 copy-start.5
  27.6 5.2 %copy-start.14 = (f32[64]{0:T(128)S(1)}, f32[64]{0:T(128)}, u32[]{:S(2)}) copy-start(f32[64]{0:T(128)} %copy-done.13) | copy-start | bytes 772
  27.6 5.2 %copy-start.16 = (f32[128]{0:T(128)S(1)}, f32[128]{0:T(128)}, u32[]{:S(2)}) copy-start(f32[128]{0:T(128)} %copy-done.15) | copy-start | bytes 1540
  27.6 9.3 %collective-permute-start.1 = (bf16[2,128,1,4,128]{4,1,3,2,0:T(8,128)(2,1)}, bf16[2,128,1,4,128]{4,1,3,2,0:T(8,128)(2,1)}, u32[]{:S(2)}, u32[]{:S(2)}) collective-permute-start(bf16[2,128,1,4,128]{4,1,3,2,0:T(8,128)(2,1)} %maximum_select_fusion.1), channel_id=1, source_target_pairs={{0,8},{8,0},{16,24},{24,16},{1,9},{9,1},{17,25},{25,17},{2,10},{10... | collective-permute-start | bytes 786440 | tf_op jit(solution)/shard_map/ppermute | solution.py:22
  30.9 7.4 %copy-start.9 = (bf16[2048,64]{1,0:T(8,128)(2,1)S(1)}, bf16[2048,64]{1,0:T(8,128)(2,1)}, u32[]{:S(2)}) copy-start(bf16[2048,64]{1,0:T(8,128)(2,1)} %get-tuple-element.27) | copy-start | bytes 786436
  47.6 10.4 %copy-start.8 = (bf16[2048,1,128]{0,2,1:T(8,128)(2,1)S(1)}, bf16[2048,1,128]{0,2,1:T(8,128)(2,1)}, u32[]{:S(2)}) copy-start(bf16[2048,1,128]{0,2,1:T(8,128)(2,1)} %copy.86) | copy-start | bytes 1572868
  64.2 2.2 copy-start.18
  64.3 14.7 %copy-start.20 = (bf16[4096,128]{1,0:T(8,128)(2,1)S(1)}, bf16[4096,128]{1,0:T(8,128)(2,1)}, u32[]{:S(2)}) copy-start(bf16[4096,128]{1,0:T(8,128)(2,1)} %param.17) | copy-start | bytes 3145732
  64.4 14.7 %copy-start.23 = (f32[128]{0:T(128)S(1)}, f32[128]{0:T(128)}, u32[]{:S(2)}) copy-start(f32[128]{0:T(128)} %copy-done.22) | copy-start | bytes 1540
  64.6 14.0 %collective-permute-start.2 = (f32[1,4,2,128,130]{3,1,4,2,0:T(4,128)S(1)}, f32[1,4,2,128,130]{3,1,4,2,0:T(4,128)S(1)}, u32[]{:S(2)}, u32[]{:S(2)}) collective-permute-start(f32[1,4,2,128,130]{3,1,4,2,0:T(4,128)S(1)} %copy.62), channel_id=1, source_target_pairs={{0,8},{8,0},{16,24},{24,16},{1,9},{9,1},{17,25},{25,17},{2,10},{10... | collective-permute-start | bytes 1597448 | tf_op jit(solution)/shard_map/ppermute | solution.py:22
  78.8 2.2 copy-start.3
  78.9 1.6 collective-permute-start.3
  83.1 1.6 copy-start.12
  83.1 58.3 %copy-start.10 = (bf16[1024,448]{0,1:T(8,128)(2,1)S(1)}, bf16[1024,448]{0,1:T(8,128)(2,1)}, u32[]{:S(2)}) copy-start(bf16[1024,448]{0,1:T(8,128)(2,1)} %param.21) | copy-start | bytes 2752516
  83.2 58.3 %copy-start.11 = (bf16[1024,448]{0,1:T(8,128)(2,1)S(1)}, bf16[1024,448]{0,1:T(8,128)(2,1)}, u32[]{:S(2)}) copy-start(bf16[1024,448]{0,1:T(8,128)(2,1)} %param.20) | copy-start | bytes 2752516
  83.2 58.2 %all-gather.7.cloned.1.call-start = ((), (), s32[]{:S(2)}) async-start(), calls=%async_computation.5 | async-start | bytes 1310720 | tf_op jit(solution)/shard_map/all_gather | solution.py:208
  117.2 71.4 %all-gather.13.cloned.1.call-start = ((), (), s32[]{:S(2)}) async-start(), calls=%async_computation.10 | async-start | bytes 8257536 | tf_op jit(solution)/shard_map/all_gather | solution.py:126
  117.9 120.5 %all-gather.9.cloned.1.call-start = ((), (), s32[]{:S(2)}) async-start(), calls=%async_computation.6 | async-start | bytes 5242880 | tf_op jit(solution)/shard_map/all_gather | solution.py:209
  141.4 175.0 %all-gather.11.cloned.1.call-start = ((), (), s32[]{:S(2)}) async-start(), calls=%async_computation.9 | async-start | bytes 16515072 | tf_op jit(solution)/shard_map/all_gather | solution.py:124
  142.9 250.9 %reduce-scatter.6.cloned.1.call-start = ((), (), s32[]{:S(2)}) async-start(), calls=%async_computation.7 | async-start | bytes 5242880 | tf_op jit(solution)/shard_map/reduce_scatter | solution.py:223
  316.4 10.3 %copy-start.7 = (bf16[1792,1024]{1,0:T(8,128)(2,1)S(1)}, bf16[1792,1024]{1,0:T(8,128)(2,1)}, u32[]{:S(2)}) copy-start(bf16[1792,1024]{1,0:T(8,128)(2,1)} %get-tuple-element.26) | copy-start | bytes 11010052
  316.4 16.4 %slice-start = ((s8[14680064]{0:T(1024)(128)(4,1)}), s8[4194304]{0:T(1024)(128)(4,1)S(1)}, s32[]{:S(2)}) async-start(s8[14680064]{0:T(1024)(128)(4,1)} %bitcast.144), calls=%async_computation.11 | async-start | bytes 8388608
  316.4 16.4 %slice-start.1 = ((s8[14680064]{0:T(1024)(128)(4,1)}), s8[4194304]{0:T(1024)(128)(4,1)S(1)}, s32[]{:S(2)}) async-start(s8[14680064]{0:T(1024)(128)(4,1)} %bitcast.144), calls=%async_computation.12 | async-start | bytes 8388608
  316.4 16.4 %slice-start.2 = ((s8[14680064]{0:T(1024)(128)(4,1)}), s8[4194304]{0:T(1024)(128)(4,1)S(1)}, s32[]{:S(2)}) async-start(s8[14680064]{0:T(1024)(128)(4,1)} %bitcast.144), calls=%async_computation.13 | async-start | bytes 8388608
  326.7 6.1 %slice-start.3 = ((s8[14680064]{0:T(1024)(128)(4,1)}), s8[2097152]{0:T(1024)(128)(4,1)S(1)}, s32[]{:S(2)}) async-start(s8[14680064]{0:T(1024)(128)(4,1)} %bitcast.144), calls=%async_computation.14 | async-start | bytes 4194304
  326.7 6.1 %copy-start.19 = (bf16[512,4096]{1,0:T(8,128)(2,1)S(1)}, bf16[512,4096]{1,0:T(8,128)(2,1)}, u32[]{:S(2)}) copy-start(bf16[512,4096]{1,0:T(8,128)(2,1)} %all-gather.9.cloned.1.call-done) | copy-start | bytes 12582916
  332.9 5.8 %copy-start.6 = (bf16[1792,1024]{1,0:T(8,128)(2,1)S(1)}, bf16[1792,1024]{1,0:T(8,128)(2,1)}, u32[]{:S(2)}) copy-start(bf16[1792,1024]{1,0:T(8,128)(2,1)} %get-tuple-element.25) | copy-start | bytes 11010052
  346.3 87.1 %copy-start.1 = (bf16[4096,128]{1,0:T(8,128)(2,1)S(1)}, bf16[4096,128]{1,0:T(8,128)(2,1)}, u32[]{:S(2)}) copy-start(bf16[4096,128]{1,0:T(8,128)(2,1)} %param.16) | copy-start | bytes 3145732
  346.3 73.6 %reduce-scatter.8.cloned.1.call-start = ((), (), s32[]{:S(2)}) async-start(), calls=%async_computation.8 | async-start | bytes 1310720 | tf_op jit(solution)/shard_map/reduce_scatter | solution.py:224
  421.7 11.0 %all-to-all-start = ((bf16[32,4,1024]{2,0,1:T(8,128)(2,1)}), bf16[32,4,1024]{2,0,1:T(8,128)(2,1)S(1)}, u32[]{:S(2)}, u32[]{:S(2)}) async-start(bf16[32,4,1024]{2,0,1:T(8,128)(2,1)} %bitcast.118), calls=%async_computation.3 | async-start | bytes 524288 | tf_op jit(solution)/shard_map/all_to_all | solution.py:228
Sparse Core Ops, SparseCore 0:
  83.3 31.6 reduce-scatter.3
  117.3 24.0 all-gather.6
  143.1 45.4 all-gather.12
  190.1 48.2 all-gather.8
  240.0 76.4 all-gather.10
  346.4 47.2 reduce-scatter.5
  396.2 23.7 reduce-scatter.7

commit v3 on v2

--- a/solution.py
+++ b/solution.py
@@ -120,11 +120,31 @@
     req_index = (lax.axis_index("ax") * n_az + az_index) * n_rc + rc_index
     mlp_index = lax.axis_index("mlp")
 
-    gate_up_part = jnp.concatenate([w_gate, w_up], axis=1)
-    gate_up_pair = lax.all_gather(gate_up_part, ("rc", "mlp"), axis=0, tiled=False)
-    gate_up_pair = gate_up_pair.reshape(n_rc, n_mlp * width_part, 2 * unit_count)
-    down_pair = lax.all_gather(w_down, ("rc", "mlp"), axis=0, tiled=False)
-    down_pair = down_pair.reshape(n_rc, n_mlp, unit_count, width_part)
+    own = (jnp.concatenate([w_gate, w_up], axis=1), w_down)
+    from_left = lax.ppermute(own, "mlp", [(i, (i + 1) % n_mlp) for i in range(n_mlp)])
+    from_right = lax.ppermute(own, "mlp", [(i, (i - 1) % n_mlp) for i in range(n_mlp)])
+    half_gu = width_part // 2
+    half_wd = unit_count // 2
+    relay_a = lax.ppermute(
+        (from_left[0][:half_gu], from_left[1][:half_wd]),
+        "mlp",
+        [(i, (i + 1) % n_mlp) for i in range(n_mlp)],
+    )
+    relay_b = lax.ppermute(
+        (from_right[0][half_gu:], from_right[1][half_wd:]),
+        "mlp",
+        [(i, (i - 1) % n_mlp) for i in range(n_mlp)],
+    )
+    across = (
+        jnp.concatenate([relay_a[0], relay_b[0]], axis=0),
+        jnp.concatenate([relay_a[1], relay_b[1]], axis=0),
+    )
+    gate_up_ring = jnp.stack([own[0], from_left[0], across[0], from_right[0]])
+    down_ring = jnp.stack([own[1], from_left[1], across[1], from_right[1]])
+    gate_up_other, down_other = swap_with_partner((gate_up_ring, down_ring), "rc", n_rc)
+    gate_up_pair = (gate_up_ring, gate_up_other)
+    down_pair = (down_ring, down_other)
+    quarter_of = [(mlp_index - ring) % n_mlp for ring in range(n_mlp)]
 
     request_of, live, positions = slot_layout(suffix_lengths[0], slots_here)
     hidden_f = hidden_in.astype(jnp.float32)
@@ -205,11 +225,18 @@
     residual = (hidden_rows + head_rows).astype(jnp.bfloat16)
     normed_mlp = rms_norm(residual.astype(jnp.float32), mlp_gain).astype(jnp.bfloat16)
 
-    tokens = lax.all_gather(normed_mlp, "az", axis=0, tiled=True)
-    tokens = lax.all_gather(tokens, "ax", axis=0, tiled=True)
+    tokens = lax.all_gather(normed_mlp, REQ[:2], axis=0, tiled=True)
+    tokens_ring = jnp.concatenate(
+        [
+            lax.dynamic_slice_in_dim(tokens, quarter_of[ring] * width_part, width_part, 1)
+            for ring in range(n_mlp)
+        ],
+        axis=1,
+    )
     acts = []
     for core in range(n_rc):
-        gate_up = jnp.dot(tokens, gate_up_pair[core], preferred_element_type=jnp.float32)
+        weights_here = gate_up_pair[core].reshape(n_mlp * width_part, 2 * unit_count)
+        gate_up = jnp.dot(tokens_ring, weights_here, preferred_element_type=jnp.float32)
         gate = gate_up[:, :unit_count]
         up_part = gate_up[:, unit_count:]
         acts.append((jax.nn.silu(gate) * up_part).astype(jnp.bfloat16))
@@ -221,7 +248,11 @@
         term = term.reshape(term.shape[0], -1).astype(jnp.float32)
         down_sum = term if down_sum is None else down_sum + term
     down = lax.psum_scatter(down_sum.astype(jnp.bfloat16), "ax", scatter_dimension=0, tiled=True)
-    down = lax.psum_scatter(down, "az", scatter_dimension=0, tiled=True).astype(jnp.float32)
+    down = lax.psum_scatter(down, "az", scatter_dimension=0, tiled=True)
+    down = down.reshape(rows_here, n_mlp, width_part)
+    natural = jnp.stack([(mlp_index - j) % n_mlp for j in range(n_mlp)])
+    down = jnp.take(down, natural, axis=1).reshape(rows_here, n_mlp * width_part)
+    down = down.astype(jnp.float32)
     out_rows = jnp.where(
         live_rows[:, None], residual.astype(jnp.float32) + down, 0.0
     ).astype(jnp.bfloat16)

time: 441 us -> 359 us (0.81)
  waiting for transfers between devices: 317 us -> 199 us
  starting transfers between devices: 8.69 us -> 22.8 us
  local copies, waits for them, and re-layouts: 17.7 us -> 31.1 us
  other arithmetic: 31.2 us -> 42.3 us
    all_gather x4 -> x1, waiting for transfers between devices: 190 us -> 0.01 us  [layer(): tokens = lax.all_gather(normed_mlp, REQ[:2], axis=0, tiled=True)]
    reduce_scatter x2 -> x0, waiting for transfers between devices: 73.4 us -> none  [the longest x1 47.4 us: layer(): lax.psum_scatter(down_sum.astype(jnp.bfloat16), 'ax', scatter_dimension=0...]
    unnamed x7 -> x6, waiting for transfers between devices: 0.78 us -> 72.2 us
    ppermute x0 -> x8, waiting for transfers between devices: none -> 64.6 us  [the longest x2 20.9 us: layer(): lax.ppermute((from_left[0][:half_gu], from_left[1][:half_wd]), 'mlp', [(i...]
    ppermute x0 -> x8, starting transfers between devices: none -> 14.1 us  [the longest x2 6.72 us: layer(): lax.ppermute((from_right[0][half_gu:], from_right[1][half_wd:]), 'mlp', [...]
    another operation x3 -> x8, other arithmetic: 0.45 us -> 12.1 us  [the longest x3 6.62 us: layer(): gate_up_ring = jnp.stack([own[0], from_left[0], across[0], from_right[0]])]
    reduce_scatter x1, waiting for transfers between devices: 30.2 us -> 40.1 us  [layer(): lax.psum_scatter(head_terms, 'mlp', scatter_dimension=0, tiled=True)]
    unnamed x59 -> x53, local copies, waits for them, and re-layouts: 4.59 us -> 14.2 us
  transfers between devices with their start and end apart: 12 -> 19, of which waited for: 11 -> 13; matrix products, arithmetic and copies ran while one was open for 6% -> 16% of each run, Pallas kernels for 0% -> 0%
where the time goes in v3:
time: 359 us; the launch traced here: 358 us
  waiting for transfers between devices  199 us (55%)
  matrix products  47.6 us (13%)
  other arithmetic  42.3 us (12%)
  local copies, waits for them, and re-layouts  31.1 us (9%)
  starting transfers between devices  22.8 us (6%)
  between operations  15 us (4%)
    unnamed x6, waiting for transfers between devices  72.2 us
    reduce_scatter x1, waiting for transfers between devices, layer(): lax.psum_scatter(head_terms, 'mlp', scatter_dimension=0, tiled=True)  40.1 us
    ppermute x2, waiting for transfers between devices, layer(): lax.ppermute((from_left[0][:half_gu], from_left[1][:half_wd]), 'mlp', [(i...  20.9 us
    ppermute x2, waiting for transfers between devices, layer(): lax.ppermute(own, 'mlp', [(i, (i - 1) % n_mlp) for i in range(n_mlp)])  20.2 us
    ppermute x6, waiting for transfers between devices, swap_with_partner(): lax.ppermute(value, axis, [(source, source ^ 1) for source in range(size)])  16.6 us
    dot_general x2, matrix products, layer(): jnp.dot(tokens_ring, weights_here, preferred_element_type=jnp.float32)  15.3 us
    unnamed x53, local copies, waits for them, and re-layouts  14.2 us
    ppermute x2, waiting for transfers between devices, layer(): lax.ppermute(own, 'mlp', [(i, (i + 1) % n_mlp) for i in range(n_mlp)])  13.3 us
  transfers between devices with their start and end apart: 19, of which 13 were waited for; matrix products, arithmetic and copies ran while one was open for 16% of the time, Pallas kernels for 0%

profile of v3, /device:TPU:0, one launch (start us, length us, event | category | flops | bytes accessed | tf_op | source)
XLA Modules:
  0.0 358.2 jit_solution(17530373576296346814)
XLA Ops:
  7.3 0.9 reduce-window.4
  8.2 0.7 fusion.68
  9.4 0.7 convert_element_type.139
  10.1 1.5 multiply_reduce_fusion
  12.1 3.3 fusion.75
  16.2 0.8 pad_maximum_fusion.8
  17.2 0.7 select_reduce_fusion.1
  18.5 2.3 fusion.78
  20.8 6.4 %fusion.37 = (bf16[2048,64]{1,0:T(8,128)(2,1)}, bf16[2048,64]{1,0:T(8,128)(2,1)}) fusion(f32[2048,1,128]{2,0,1:T(8,128)S(1)} %copy_convert_fusion, f32[64]{0:T(128)} %copy-done.12, f32[2048]{0:T(1024)S(1)} %add_convert_fusion.3), kind=kLoop, calls=%fused_computation.67 | loop fusion | flops 1179648 | bytes 1581312 | tf_op jit(solution)/shard_map/concatenate | solution.py:33
  27.3 0.7 maximum_select_fusion.1
  28.1 2.0 collective-permute-start.1
  30.1 1.2 convolution_bitcast_fusion.1
  31.3 1.8 copy.122
  33.4 4.0 %collective-permute-done.1 = bf16[2,128,1,4,128]{4,1,3,2,0:T(8,128)(2,1)} collective-permute-done((bf16[2,128,1,4,128]{4,1,3,2,0:T(8,128)(2,1)}, bf16[2,128,1,4,128]{4,1,3,2,0:T(8,128)(2,1)}, u32[]{:S(2)}, u32[]{:S(2)}) %collective-permute-start.1) | collective-permute-done | bytes 262176 | tf_op jit(solution)/shard_map/ppermute | solution.py:22
  37.4 1.3 maximum_select_fusion
  38.7 9.2 %bitcast_reduce_fusion = (f32[4,512]{1,0:T(4,128)S(1)}, f32[2048,512,4]{0,1,2:T(8,128)}) fusion(bf16[512,4,128]{2,0,1:T(8,128)(2,1)S(1)} %bitcast.151, bf16[2048,64]{1,0:T(8,128)(2,1)} %get-tuple-element.32, bf16[2048,64]{1,0:T(8,128)(2,1)S(1)} %copy-done.7), kind=kOutput, calls=%fused_computation.2 | convolution fusion | flops 1083176960 | bytes 17833984 | tf_op jit(solution)/shard_map/qkgd,nkd->kgqn/dot_general | solution.py:60
  47.9 10.3 %fusion.2 = (bf16[1,4,512,2048]{3,2,1,0:T(8,128)(2,1)}, f32[4,512]{1,0:T(4,128)S(1)}) fusion(f32[2048,512,4]{0,1,2:T(8,128)} %get-tuple-element.46, f32[4,512]{1,0:T(4,128)S(1)} %get-tuple-element.45), kind=kLoop, calls=%fused_computation.5 | loop fusion | flops 16775168 | bytes 25182208 | tf_op jit(solution)/shard_map/convert_element_type | solution.py:70
  58.3 6.3 %convolution_bitcast_fusion = f32[1,4,4,128,128]{3,4,2,1,0:T(8,128)S(1)} fusion(bf16[4,4,128,2048]{3,2,1,0:T(8,128)(2,1)} %bitcast.148, bf16[2048,1,128]{0,2,1:T(8,128)(2,1)S(1)} %copy-done.6), kind=kOutput, calls=%fused_computation.20 | convolution fusion | flops 1073741824 | bytes 9961472 | tf_op jit(solution)/shard_map/kgqn,nkd->kgqd/dot_general | solution.py:68
  64.9 1.8 collective-permute-start.2
  67.2 11.7 %collective-permute-done.2 = f32[1,4,2,128,130]{3,1,4,2,0:T(4,128)S(1)} collective-permute-done((f32[1,4,2,128,130]{3,1,4,2,0:T(4,128)S(1)}, f32[1,4,2,128,130]{3,1,4,2,0:T(4,128)S(1)}, u32[]{:S(2)}, u32[]{:S(2)}) %collective-permute-start.2) | collective-permute-done | bytes 532512 | tf_op jit(solution)/shard_map/ppermute | solution.py:22
  79.5 0.6 convolution_convert_fusion
  80.2 0.9 collective-permute-done.3
  81.4 2.1 fusion.82
  83.5 0.5 copy.94
  84.1 1.5 copy.95
  85.6 1.8 pad_maximum_fusion.3
  87.4 1.5 collective-permute-start.4
  88.9 1.8 collective-permute-start.6
  90.6 1.5 convert_element_type.136
  92.1 40.1 %reduce-scatter.8.cloned.1.call-done = f32[32,4096]{1,0:T(8,128)} async-done(((f32[128,4096]{1,0:T(8,128)}), f32[32,4096]{1,0:T(8,128)}) %reduce-scatter.8.cloned.1.call-update) | async-done | bytes 524304 | tf_op jit(solution)/shard_map/reduce_scatter | solution.py:220
  132.3 1.4 fusion.21
  133.6 0.8 fusion.23
  134.6 13.3 %collective-permute-done.4 = bf16[1024,896]{1,0:T(8,128)(2,1)} collective-permute-done((bf16[1024,896]{1,0:T(8,128)(2,1)}, bf16[1024,896]{1,0:T(8,128)(2,1)}, u32[]{:S(2)}, u32[]{:S(2)}) %collective-permute-start.4) | collective-permute-done | bytes 1835040 | tf_op jit(solution)/shard_map/ppermute | solution.py:124
  147.8 1.3 slice.146
  149.4 1.3 slice.147
  150.7 3.0 collective-permute-start.7
  153.7 0.6 fusion.93
  154.3 17.6 %collective-permute-done.5 = bf16[512,896]{1,0:T(8,128)(2,1)S(1)} collective-permute-done((bf16[512,896]{1,0:T(8,128)(2,1)S(1)}, bf16[512,896]{1,0:T(8,128)(2,1)S(1)}, u32[]{:S(2)}, u32[]{:S(2)}) %collective-permute-start.5) | collective-permute-done | bytes 917536 | tf_op jit(solution)/shard_map/ppermute | solution.py:128
  171.9 0.6 collective-permute-done.7
  172.7 5.9 %pad_maximum_fusion = bf16[4,1024,896]{2,1,0:T(8,128)(2,1)} fusion(bf16[1,1024,896]{2,1,0:T(8,128)(2,1)} %bitcast.50, bf16[1,1024,896]{2,1,0:T(8,128)(2,1)S(1)} %maximum_bitcast_fusion, bf16[1,1024,896]{2,1,0:T(8,128)(2,1)} %bitcast.48, bf16[1,1024,896]{2,1,0:T(8,128)(2,1)S(1)} %fusion.93), kind=kLoop, calls=%fused_computation.7 | loop fusion | flops 11010048 | bytes 14680064 | tf_op jit(solution)/shard_map/stack | solution.py:142
  178.6 3.7 %collective-permute-start.10 = (bf16[448,1024]{1,0:T(8,128)(2,1)S(1)}, bf16[448,1024]{1,0:T(8,128)(2,1)S(1)}, u32[]{:S(2)}, u32[]{:S(2)}) collective-permute-start(bf16[448,1024]{1,0:T(8,128)(2,1)S(1)} %copy-done.8), channel_id=1, source_target_pairs={{0,3},{1,0},{2,1},{3,2},{4,7},{5,4},{6,5},{7,6},{8,11},{9,8},{10,9... | collective-permute-start | bytes 2752520 | tf_op jit(solution)/shard_map/ppermute | solution.py:125
  182.3 20.2 %collective-permute-done.10 = bf16[448,1024]{1,0:T(8,128)(2,1)S(1)} collective-permute-done((bf16[448,1024]{1,0:T(8,128)(2,1)S(1)}, bf16[448,1024]{1,0:T(8,128)(2,1)S(1)}, u32[]{:S(2)}, u32[]{:S(2)}) %collective-permute-start.10) | collective-permute-done | bytes 917536 | tf_op jit(solution)/shard_map/ppermute | solution.py:125
  202.5 0.8 slice.151
  203.3 3.7 %collective-permute-start.11 = (bf16[224,1024]{1,0:T(8,128)(2,1)}, bf16[224,1024]{1,0:T(8,128)(2,1)}, u32[]{:S(2)}, u32[]{:S(2)}) collective-permute-start(bf16[224,1024]{1,0:T(8,128)(2,1)} %slice.151), channel_id=1, source_target_pairs={{0,3},{1,0},{2,1},{3,2},{4,7},{5,4},{6,5},{7,6},{8,11},{9,8},{10,9... | collective-permute-start | bytes 1376264 | tf_op jit(solution)/shard_map/ppermute | solution.py:133
  207.2 9.6 %collective-permute-done.11 = bf16[224,1024]{1,0:T(8,128)(2,1)} collective-permute-done((bf16[224,1024]{1,0:T(8,128)(2,1)}, bf16[224,1024]{1,0:T(8,128)(2,1)}, u32[]{:S(2)}, u32[]{:S(2)}) %collective-permute-start.11) | collective-permute-done | bytes 458784 | tf_op jit(solution)/shard_map/ppermute | solution.py:133
  216.8 3.3 collective-permute-done.9
  220.2 1.2 maximum_bitcast_fusion.1
  221.4 3.1 pad_maximum_fusion.2
  224.5 2.6 constant_dynamic-slice_fusion.5
  227.1 7.7 %fusion.20 = f32[512,896]{1,0:T(8,128)S(1)} fusion(bf16[4096,896]{1,0:T(8,128)(2,1)} %bitcast.51, bf16[512,1024]{1,0:T(8,128)(2,1)S(1)} %get-tuple-element.28, bf16[512,1024]{1,0:T(8,128)(2,1)S(1)} %get-tuple-element.29, bf16[512,1024]{1,0:T(8,128)(2,1)S(1)} %get-tuple-element.30, bf16[512,1024]{1,0:T(8,128)(2,1)S(1)} %get-tuple-element.27), kind=kOutput, calls=%fused_computation.45 | convolution fusion | flops 3774873600 | bytes 13369344 | tf_op jit(solution)/shard_map/dot_general | solution.py:239
  234.8 2.7 fusion.32
  237.5 7.6 %fusion.19 = f32[512,896]{1,0:T(8,128)S(1)} fusion(bf16[4096,896]{1,0:T(8,128)(2,1)} %bitcast.57, bf16[512,1024]{1,0:T(8,128)(2,1)S(1)} %get-tuple-element.28, bf16[512,1024]{1,0:T(8,128)(2,1)S(1)} %get-tuple-element.29, bf16[512,1024]{1,0:T(8,128)(2,1)S(1)} %get-tuple-element.30, bf16[512,1024]{1,0:T(8,128)(2,1)S(1)} %get-tuple-element.27), kind=kOutput, calls=%fused_computation.44 | convolution fusion | flops 3774873600 | bytes 13369344 | tf_op jit(solution)/shard_map/dot_general | solution.py:239
  245.1 6.4 %add_convert_fusion = bf16[512,4,1024]{2,0,1:T(8,128)(2,1)} fusion(bf16[512,4,1024]{2,0,1:T(8,128)(2,1)S(1)} %fusion.32, bf16[4,448,1024]{2,1,0:T(8,128)(2,1)} %collective-permute-done.13, f32[512,896]{1,0:T(8,128)S(1)} %fusion.19), kind=kOutput, calls=%fused_computation.6 | convolution fusion | flops 1890910208 | bytes 14155776 | tf_op jit(solution)/shard_map/tu,mud->tmd/dot_general | solution.py:245
  251.6 6.2 %copy.98 = bf16[512,4,1024]{0,2,1:T(8,128)(2,1)} copy(bf16[512,4,1024]{2,0,1:T(8,128)(2,1)} %add_convert_fusion) | data formatting | bytes 8388608 | tf_op jit(solution)/shard_map/convert_element_type | solution.py:250
  257.8 6.4 %copy.115 = bf16[512,4096]{1,0:T(8,128)(2,1)} copy(bf16[512,4096]{0,1:T(8,128)(2,1)} %bitcast.149) | data formatting | bytes 8388608
  264.3 46.5 %reduce-scatter.10.cloned.1.call-done = bf16[128,4096]{1,0:T(8,128)(2,1)} async-done(((bf16[512,4096]{1,0:T(8,128)(2,1)}), bf16[128,4096]{1,0:T(8,128)(2,1)}) %reduce-scatter.10.cloned.1.call-update) | async-done | bytes 1048592
  311.1 25.6 %reduce-scatter.12.cloned.1.call-done = bf16[32,4096]{1,0:T(8,128)(2,1)} async-done(((bf16[128,4096]{1,0:T(8,128)(2,1)}), bf16[32,4096]{1,0:T(8,128)(2,1)}) %reduce-scatter.12.cloned.1.call-update) | async-done | bytes 262160
  336.7 1.4 copy.118
  338.5 0.6 gather_fusion
  339.2 0.7 copy.146
  339.9 4.4 %all-to-all-start = ((bf16[32,4,1024]{2,0,1:T(8,128)(2,1)}), bf16[32,4,1024]{2,0,1:T(8,128)(2,1)S(1)}, u32[]{:S(2)}, u32[]{:S(2)}) async-start(bf16[32,4,1024]{2,0,1:T(8,128)(2,1)} %bitcast.146), calls=%async_computation.1 | async-start | bytes 524288 | tf_op jit(solution)/shard_map/all_to_all | solution.py:259
  344.3 0.8 copy.103
  345.1 5.9 %all-to-all-done = bf16[32,4,1024]{2,0,1:T(8,128)(2,1)S(1)} async-done(((bf16[32,4,1024]{2,0,1:T(8,128)(2,1)}), bf16[32,4,1024]{2,0,1:T(8,128)(2,1)S(1)}, u32[]{:S(2)}, u32[]{:S(2)}) %all-to-all-start) | async-done | bytes 262176 | tf_op jit(solution)/shard_map/all_to_all | solution.py:259
  351.0 0.7 copy.149
  (114 shorter events, 5.8 us)
Async XLA Ops:
  7.2 22.9 %copy-start = (bf16[4096,128]{1,0:T(8,128)(2,1)S(1)}, bf16[4096,128]{1,0:T(8,128)(2,1)}, u32[]{:S(2)}) copy-start(bf16[4096,128]{1,0:T(8,128)(2,1)} %param.16) | copy-start | bytes 3145732
  7.2 125.1 %reduce-scatter.8.cloned.1.call-start = ((), (), s32[]{:S(2)}) async-start(), calls=%async_computation.4 | async-start | bytes 2621440 | tf_op jit(solution)/shard_map/reduce_scatter | solution.py:220
  7.2 8.6 %copy-start.12 = (f32[64]{0:T(128)}, f32[64]{0:T(128)S(1)}, u32[]{:S(2)}) copy-start(f32[64]{0:T(128)S(1)} %multiply_power_fusion) | copy-start | bytes 772
  8.9 0.5 copy-start.16
  9.4 6.4 %copy-start.14 = (f32[128]{0:T(128)}, f32[128]{0:T(128)S(1)}, u32[]{:S(2)}) copy-start(f32[128]{0:T(128)S(1)} %subtract_convert_fusion.1) | copy-start | bytes 1540
  11.7 0.5 copy-start.20
  12.1 4.8 %copy-start.18 = (s32[8,4]{0,1:T(4,128)S(1)}, s32[8,4]{0,1:T(4,128)}, u32[]{:S(2)}) copy-start(s32[8,4]{0,1:T(4,128)} %param.25) | copy-start | bytes 388
  12.1 6.3 %copy-start.4 = (bf16[2048,2,128]{2,1,0:T(2,128)(2,1)S(1)}, bf16[2048,2,128]{2,1,0:T(2,128)(2,1)}, u32[]{:S(2)}) copy-start(bf16[2048,2,128]{2,1,0:T(2,128)(2,1)} %param.23) | copy-start | bytes 3145732
  17.0 10.4 %collective-permute-start = (bf16[128,1,4,128]{3,0,2,1:T(8,128)(2,1)}, bf16[128,1,4,128]{3,0,2,1:T(8,128)(2,1)S(1)}, u32[]{:S(2)}, u32[]{:S(2)}) collective-permute-start(bf16[128,1,4,128]{3,0,2,1:T(8,128)(2,1)} %pad_maximum_fusion.8), channel_id=1, source_target_pairs={{0,4},{4,0},{1,5},{5,1},{2,6},{6,2},{3,7},{7,3},{8,12},{12,8},{9,1... | collective-permute-start | bytes 393224 | tf_op jit(solution)/shard_map/ppermute | solution.py:22
  20.8 9.4 %copy-start.2 = (bf16[128,4096]{1,0:T(8,128)(2,1)S(1)}, bf16[128,4096]{1,0:T(8,128)(2,1)}, u32[]{:S(2)}) copy-start(bf16[128,4096]{1,0:T(8,128)(2,1)} %param.13) | copy-start | bytes 3145732
  20.8 10.5 %copy-start.5 = (bf16[2048,1,128]{2,1,0:T(2,128)(2,1)S(1)}, bf16[2048,1,128]{2,1,0:T(2,128)(2,1)}, u32[]{:S(2)}) copy-start(bf16[2048,1,128]{2,1,0:T(2,128)(2,1)} %get-tuple-element.33) | copy-start | bytes 1572868
  28.1 5.1 %copy-start.13 = (f32[64]{0:T(128)S(1)}, f32[64]{0:T(128)}, u32[]{:S(2)}) copy-start(f32[64]{0:T(128)} %copy-done.12) | copy-start | bytes 772
  28.1 5.1 %copy-start.15 = (f32[128]{0:T(128)S(1)}, f32[128]{0:T(128)}, u32[]{:S(2)}) copy-start(f32[128]{0:T(128)} %copy-done.14) | copy-start | bytes 1540
  28.1 9.3 %collective-permute-start.1 = (bf16[2,128,1,4,128]{4,1,3,2,0:T(8,128)(2,1)}, bf16[2,128,1,4,128]{4,1,3,2,0:T(8,128)(2,1)}, u32[]{:S(2)}, u32[]{:S(2)}) collective-permute-start(bf16[2,128,1,4,128]{4,1,3,2,0:T(8,128)(2,1)} %maximum_select_fusion.1), channel_id=1, source_target_pairs={{0,8},{8,0},{16,24},{24,16},{1,9},{9,1},{17,25},{25,17},{2,10},{10... | collective-permute-start | bytes 786440 | tf_op jit(solution)/shard_map/ppermute | solution.py:22
  31.3 7.4 %copy-start.7 = (bf16[2048,64]{1,0:T(8,128)(2,1)S(1)}, bf16[2048,64]{1,0:T(8,128)(2,1)}, u32[]{:S(2)}) copy-start(bf16[2048,64]{1,0:T(8,128)(2,1)} %get-tuple-element.31) | copy-start | bytes 786436
  47.9 10.3 %copy-start.6 = (bf16[2048,1,128]{0,2,1:T(8,128)(2,1)S(1)}, bf16[2048,1,128]{0,2,1:T(8,128)(2,1)}, u32[]{:S(2)}) copy-start(bf16[2048,1,128]{0,2,1:T(8,128)(2,1)} %copy.122) | copy-start | bytes 1572868
  64.5 2.2 copy-start.17
  64.7 14.8 %copy-start.19 = (bf16[4096,128]{1,0:T(8,128)(2,1)S(1)}, bf16[4096,128]{1,0:T(8,128)(2,1)}, u32[]{:S(2)}) copy-start(bf16[4096,128]{1,0:T(8,128)(2,1)} %param.17) | copy-start | bytes 3145732
  64.7 14.8 %copy-start.21 = (f32[128]{0:T(128)S(1)}, f32[128]{0:T(128)}, u32[]{:S(2)}) copy-start(f32[128]{0:T(128)} %copy-done.20) | copy-start | bytes 1540
  64.9 14.0 %collective-permute-start.2 = (f32[1,4,2,128,130]{3,1,4,2,0:T(4,128)S(1)}, f32[1,4,2,128,130]{3,1,4,2,0:T(4,128)S(1)}, u32[]{:S(2)}, u32[]{:S(2)}) collective-permute-start(f32[1,4,2,128,130]{3,1,4,2,0:T(4,128)S(1)} %copy.87), channel_id=1, source_target_pairs={{0,8},{8,0},{16,24},{24,16},{1,9},{9,1},{17,25},{25,17},{2,10},{10... | collective-permute-start | bytes 1597448 | tf_op jit(solution)/shard_map/ppermute | solution.py:22
  79.1 2.3 copy-start.3
  79.2 1.8 collective-permute-start.3
  81.4 2.2 copy-start.10
  83.5 141.0 %all-gather.2.cloned.1.call-start = ((), (), s32[]{:S(2)}) async-start(), calls=%async_computation.5 | async-start | bytes 4456448 | tf_op jit(solution)/shard_map/all_gather | solution.py:228
  85.6 6.6 %copy-start.11 = (bf16[4096]{0:T(1024)(128)(2,1)S(1)}, bf16[4096]{0:T(1024)(128)(2,1)}, u32[]{:S(2)}) copy-start(bf16[4096]{0:T(1024)(128)(2,1)} %param.19) | copy-start | bytes 24580
  87.4 60.4 %collective-permute-start.4 = (bf16[1024,896]{1,0:T(8,128)(2,1)}, bf16[1024,896]{1,0:T(8,128)(2,1)}, u32[]{:S(2)}, u32[]{:S(2)}) collective-permute-start(bf16[1024,896]{1,0:T(8,128)(2,1)} %pad_maximum_fusion.3), channel_id=1, source_target_pairs={{0,1},{1,2},{2,3},{3,0},{4,5},{5,6},{6,7},{7,4},{8,9},{9,10},{10,1... | collective-permute-start | bytes 5505032 | tf_op jit(solution)/shard_map/ppermute | solution.py:124
  88.9 60.6 %collective-permute-start.6 = (bf16[1024,896]{1,0:T(8,128)(2,1)}, bf16[1024,896]{1,0:T(8,128)(2,1)}, u32[]{:S(2)}, u32[]{:S(2)}) collective-permute-start(bf16[1024,896]{1,0:T(8,128)(2,1)} %pad_maximum_fusion.3), channel_id=1, source_target_pairs={{0,3},{1,0},{2,1},{3,2},{4,7},{5,4},{6,5},{7,6},{8,11},{9,8},{10,9... | collective-permute-start | bytes 5505032 | tf_op jit(solution)/shard_map/ppermute | solution.py:125
  134.5 176.3 %reduce-scatter.10.cloned.1.call-start = ((), (), s32[]{:S(2)}) async-start(), calls=%async_computation.6 | async-start | bytes 5242880
  149.1 22.8 %collective-permute-start.5 = (bf16[512,896]{1,0:T(8,128)(2,1)S(1)}, bf16[512,896]{1,0:T(8,128)(2,1)S(1)}, u32[]{:S(2)}, u32[]{:S(2)}) collective-permute-start(bf16[512,896]{1,0:T(8,128)(2,1)S(1)} %slice.146), channel_id=1, source_target_pairs={{0,1},{1,2},{2,3},{3,0},{4,5},{5,6},{6,7},{7,4},{8,9},{9,10},{10,1... | collective-permute-start | bytes 2752520 | tf_op jit(solution)/shard_map/ppermute | solution.py:128
  150.7 21.8 %collective-permute-start.7 = (bf16[512,896]{1,0:T(8,128)(2,1)S(1)}, bf16[512,896]{1,0:T(8,128)(2,1)S(1)}, u32[]{:S(2)}, u32[]{:S(2)}) collective-permute-start(bf16[512,896]{1,0:T(8,128)(2,1)S(1)} %slice.147), channel_id=1, source_target_pairs={{0,3},{1,0},{2,1},{3,2},{4,7},{5,4},{6,5},{7,6},{8,11},{9,8},{10,9... | collective-permute-start | bytes 2752520 | tf_op jit(solution)/shard_map/ppermute | solution.py:133
  172.7 5.9 %copy-start.8 = (bf16[448,1024]{1,0:T(8,128)(2,1)S(1)}, bf16[448,1024]{1,0:T(8,128)(2,1)}, u32[]{:S(2)}) copy-start(bf16[448,1024]{1,0:T(8,128)(2,1)} %param.22) | copy-start | bytes 2752516
  178.6 59.0 %collective-permute-start.12 = (bf16[4,1024,896]{2,1,0:T(8,128)(2,1)}, bf16[4,1024,896]{2,1,0:T(8,128)(2,1)}, u32[]{:S(2)}, u32[]{:S(2)}) collective-permute-start(bf16[4,1024,896]{2,1,0:T(8,128)(2,1)} %pad_maximum_fusion), channel_id=1, source_target_pairs={{0,4},{4,0},{1,5},{5,1},{2,6},{6,2},{3,7},{7,3},{8,12},{12,8},{9,1... | collective-permute-start | bytes 22020104 | tf_op jit(solution)/shard_map/ppermute | solution.py:22
  178.6 23.9 %collective-permute-start.10 = (bf16[448,1024]{1,0:T(8,128)(2,1)S(1)}, bf16[448,1024]{1,0:T(8,128)(2,1)S(1)}, u32[]{:S(2)}, u32[]{:S(2)}) collective-permute-start(bf16[448,1024]{1,0:T(8,128)(2,1)S(1)} %copy-done.8), channel_id=1, source_target_pairs={{0,3},{1,0},{2,1},{3,2},{4,7},{5,4},{6,5},{7,6},{8,11},{9,8},{10,9... | collective-permute-start | bytes 2752520 | tf_op jit(solution)/shard_map/ppermute | solution.py:125
  182.3 24.7 %collective-permute-start.8 = (bf16[448,1024]{1,0:T(8,128)(2,1)S(1)}, bf16[448,1024]{1,0:T(8,128)(2,1)S(1)}, u32[]{:S(2)}, u32[]{:S(2)}) collective-permute-start(bf16[448,1024]{1,0:T(8,128)(2,1)S(1)} %copy-done.8), channel_id=1, source_target_pairs={{0,1},{1,2},{2,3},{3,0},{4,5},{5,6},{6,7},{7,4},{8,9},{9,10},{10,1... | collective-permute-start | bytes 2752520 | tf_op jit(solution)/shard_map/ppermute | solution.py:124
  203.3 13.5 %collective-permute-start.11 = (bf16[224,1024]{1,0:T(8,128)(2,1)}, bf16[224,1024]{1,0:T(8,128)(2,1)}, u32[]{:S(2)}, u32[]{:S(2)}) collective-permute-start(bf16[224,1024]{1,0:T(8,128)(2,1)} %slice.151), channel_id=1, source_target_pairs={{0,3},{1,0},{2,1},{3,2},{4,7},{5,4},{6,5},{7,6},{8,11},{9,8},{10,9... | collective-permute-start | bytes 1376264 | tf_op jit(solution)/shard_map/ppermute | solution.py:133
  207.0 13.1 %collective-permute-start.9 = (bf16[224,1024]{1,0:T(8,128)(2,1)S(1)}, bf16[224,1024]{1,0:T(8,128)(2,1)}, u32[]{:S(2)}, u32[]{:S(2)}) collective-permute-start(bf16[224,1024]{1,0:T(8,128)(2,1)S(1)} %slice.150), channel_id=1, source_target_pairs={{0,1},{1,2},{2,3},{3,0},{4,5},{5,6},{6,7},{7,4},{8,9},{9,10},{10,1... | collective-permute-start | bytes 1376264 | tf_op jit(solution)/shard_map/ppermute | solution.py:128
  224.5 20.7 %collective-permute-start.13 = (bf16[4,448,1024]{2,1,0:T(8,128)(2,1)}, bf16[4,448,1024]{2,1,0:T(8,128)(2,1)}, u32[]{:S(2)}, u32[]{:S(2)}) collective-permute-start(bf16[4,448,1024]{2,1,0:T(8,128)(2,1)} %pad_maximum_fusion.2), channel_id=1, source_target_pairs={{0,4},{4,0},{1,5},{5,1},{2,6},{6,2},{3,7},{7,3},{8,12},{12,8},{9,1... | collective-permute-start | bytes 11010056 | tf_op jit(solution)/shard_map/ppermute | solution.py:22
  227.1 7.7 %copy-start.9 = (bf16[448,1024]{1,0:T(8,128)(2,1)S(1)}, bf16[448,1024]{1,0:T(8,128)(2,1)}, u32[]{:S(2)}) copy-start(bf16[448,1024]{1,0:T(8,128)(2,1)} %param.22) | copy-start | bytes 2752516
  264.2 72.5 %reduce-scatter.12.cloned.1.call-start = ((), (), s32[]{:S(2)}) async-start(), calls=%async_computation.7 | async-start | bytes 1310720
  310.8 40.9 %copy-start.1 = (bf16[4096,128]{1,0:T(8,128)(2,1)S(1)}, bf16[4096,128]{1,0:T(8,128)(2,1)}, u32[]{:S(2)}) copy-start(bf16[4096,128]{1,0:T(8,128)(2,1)} %param.16) | copy-start | bytes 3145732
  339.9 11.0 %all-to-all-start = ((bf16[32,4,1024]{2,0,1:T(8,128)(2,1)}), bf16[32,4,1024]{2,0,1:T(8,128)(2,1)S(1)}, u32[]{:S(2)}, u32[]{:S(2)}) async-start(bf16[32,4,1024]{2,0,1:T(8,128)(2,1)} %bitcast.146), calls=%async_computation.1 | async-start | bytes 524288 | tf_op jit(solution)/shard_map/all_to_all | solution.py:259
Sparse Core Ops, SparseCore 0:
  83.6 48.6 reduce-scatter.7
  135.0 51.1 all-gather.1
  264.4 46.3 reduce-scatter.9
  313.0 23.6 reduce-scatter.11

commit v4 on v3

--- a/solution.py
+++ b/solution.py
@@ -140,7 +140,8 @@
         jnp.concatenate([relay_a[1], relay_b[1]], axis=0),
     )
     gate_up_ring = jnp.stack([own[0], from_left[0], across[0], from_right[0]])
-    down_ring = jnp.stack([own[1], from_left[1], across[1], from_right[1]])
+    down_ring = jnp.stack([own[1], from_left[1], across[1], from_right[1]], axis=1)
+    down_ring = down_ring.reshape(unit_count, n_mlp * width_part)
     gate_up_other, down_other = swap_with_partner((gate_up_ring, down_ring), "rc", n_rc)
     gate_up_pair = (gate_up_ring, gate_up_other)
     down_pair = (down_ring, down_other)
@@ -242,10 +243,8 @@
         acts.append((jax.nn.silu(gate) * up_part).astype(jnp.bfloat16))
     down_sum = None
     for core in range(n_rc):
-        term = jnp.einsum(
-            "tu,mud->tmd", acts[core], down_pair[core], preferred_element_type=jnp.float32
-        ).astype(jnp.bfloat16)
-        term = term.reshape(term.shape[0], -1).astype(jnp.float32)
+        term = jnp.dot(acts[core], down_pair[core], preferred_element_type=jnp.float32)
+        term = term.astype(jnp.bfloat16).astype(jnp.float32)
         down_sum = term if down_sum is None else down_sum + term
     down = lax.psum_scatter(down_sum.astype(jnp.bfloat16), "ax", scatter_dimension=0, tiled=True)
     down = lax.psum_scatter(down, "az", scatter_dimension=0, tiled=True)

time: 359 us -> 347 us (0.967)
  local copies, waits for them, and re-layouts: 31.1 us -> 18.4 us
    reduce_scatter x0 -> x2, waiting for transfers between devices: none -> 72.1 us  [the longest x1 46.5 us: layer(): lax.psum_scatter(down_sum.astype(jnp.bfloat16), 'ax', scatter_dimension=0...]
    unnamed x6 -> x4, waiting for transfers between devices: 72.2 us -> 0.07 us
    unnamed x53 -> x51, local copies, waits for them, and re-layouts: 14.2 us -> 5.49 us
    convert_element_type x1 -> x0, local copies, waits for them, and re-layouts: 6.22 us -> none  [layer(): down_sum.astype(jnp.bfloat16)]
  transfers between devices with their start and end apart: 19 -> 19, of which waited for: 13 -> 13; matrix products, arithmetic and copies ran while one was open for 16% -> 17% of each run, Pallas kernels for 0% -> 0%
where the time goes in v4:
time: 347 us; the launch traced here: 346 us
  waiting for transfers between devices  199 us (57%)
  matrix products  49.3 us (14%)
  other arithmetic  40.7 us (12%)
  starting transfers between devices  22.7 us (7%)
  local copies, waits for them, and re-layouts  18.4 us (5%)
  between operations  15.2 us (4%)
    reduce_scatter x1, waiting for transfers between devices, layer(): lax.psum_scatter(down_sum.astype(jnp.bfloat16), 'ax', scatter_dimension=0...  46.5 us
    reduce_scatter x1, waiting for transfers between devices, layer(): lax.psum_scatter(head_terms, 'mlp', scatter_dimension=0, tiled=True)  40.1 us
    reduce_scatter x1, waiting for transfers between devices, layer(): down = lax.psum_scatter(down, 'az', scatter_dimension=0, tiled=True)  25.6 us
    ppermute x2, waiting for transfers between devices, layer(): lax.ppermute((from_left[0][:half_gu], from_left[1][:half_wd]), 'mlp', [(i...  21.2 us
    ppermute x2, waiting for transfers between devices, layer(): lax.ppermute(own, 'mlp', [(i, (i - 1) % n_mlp) for i in range(n_mlp)])  20.2 us
    ppermute x6, waiting for transfers between devices, swap_with_partner(): lax.ppermute(value, axis, [(source, source ^ 1) for source in range(size)])  16.6 us
    dot_general x2, matrix products, layer(): jnp.dot(tokens_ring, weights_here, preferred_element_type=jnp.float32)  15.2 us
    ppermute x2, waiting for transfers between devices, layer(): lax.ppermute(own, 'mlp', [(i, (i + 1) % n_mlp) for i in range(n_mlp)])  13.3 us
  transfers between devices with their start and end apart: 19, of which 13 were waited for; matrix products, arithmetic and copies ran while one was open for 17% of the time, Pallas kernels for 0%

profile of v4, /device:TPU:0, one launch (start us, length us, event | category | flops | bytes accessed | tf_op | source)
XLA Modules:
  0.0 345.6 jit_solution(2930478226315166716)
XLA Ops:
  7.3 0.9 reduce-window.4
  8.2 0.7 fusion.67
  9.0 0.7 convert_element_type.134
  9.7 1.5 multiply_reduce_fusion
  11.3 3.3 fusion.74
  14.9 0.3 multiply_cosine_fusion.1
  15.3 0.8 pad_maximum_fusion.7
  16.3 0.7 select_reduce_fusion.1
  17.7 2.3 fusion.77
  20.1 6.4 %fusion.36 = (bf16[2048,64]{1,0:T(8,128)(2,1)}, bf16[2048,64]{1,0:T(8,128)(2,1)}) fusion(f32[2048,1,128]{2,0,1:T(8,128)S(1)} %copy_convert_fusion, f32[64]{0:T(128)} %copy-done.11, f32[2048]{0:T(1024)S(1)} %add_convert_fusion.3), kind=kLoop, calls=%fused_computation.68 | loop fusion | flops 1179648 | bytes 1581312 | tf_op jit(solution)/shard_map/concatenate | solution.py:33
  26.6 0.7 maximum_select_fusion.1
  27.4 2.0 collective-permute-start.1
  29.4 1.2 convolution_bitcast_fusion.1
  30.7 1.8 copy.85
  32.7 4.0 %collective-permute-done.1 = bf16[2,128,1,4,128]{4,1,3,2,0:T(8,128)(2,1)} collective-permute-done((bf16[2,128,1,4,128]{4,1,3,2,0:T(8,128)(2,1)}, bf16[2,128,1,4,128]{4,1,3,2,0:T(8,128)(2,1)}, u32[]{:S(2)}, u32[]{:S(2)}) %collective-permute-start.1) | collective-permute-done | bytes 262176 | tf_op jit(solution)/shard_map/ppermute | solution.py:22
  36.7 1.3 maximum_select_fusion
  38.0 9.2 %bitcast_reduce_fusion = (f32[4,512]{1,0:T(4,128)S(1)}, f32[2048,512,4]{0,1,2:T(8,128)}) fusion(bf16[512,4,128]{2,0,1:T(8,128)(2,1)S(1)} %bitcast.147, bf16[2048,64]{1,0:T(8,128)(2,1)} %get-tuple-element.30, bf16[2048,64]{1,0:T(8,128)(2,1)S(1)} %copy-done.7), kind=kOutput, calls=%fused_computation.2 | convolution fusion | flops 1083176960 | bytes 17833984 | tf_op jit(solution)/shard_map/qkgd,nkd->kgqn/dot_general | solution.py:60
  47.2 10.3 %fusion.2 = (bf16[1,4,512,2048]{3,2,1,0:T(8,128)(2,1)}, f32[4,512]{1,0:T(4,128)S(1)}) fusion(f32[2048,512,4]{0,1,2:T(8,128)} %get-tuple-element.44, f32[4,512]{1,0:T(4,128)S(1)} %get-tuple-element.43), kind=kLoop, calls=%fused_computation.5 | loop fusion | flops 16775168 | bytes 25182208 | tf_op jit(solution)/shard_map/convert_element_type | solution.py:70
  57.6 6.3 %convolution_bitcast_fusion = f32[1,4,4,128,128]{3,4,2,1,0:T(8,128)S(1)} fusion(bf16[4,4,128,2048]{3,2,1,0:T(8,128)(2,1)} %bitcast.146, bf16[2048,1,128]{0,2,1:T(8,128)(2,1)S(1)} %copy-done.6), kind=kOutput, calls=%fused_computation.22 | convolution fusion | flops 1073741824 | bytes 9961472 | tf_op jit(solution)/shard_map/kgqn,nkd->kgqd/dot_general | solution.py:68
  64.2 1.8 collective-permute-start.2
  66.5 11.7 %collective-permute-done.2 = f32[1,4,2,128,130]{3,1,4,2,0:T(4,128)S(1)} collective-permute-done((f32[1,4,2,128,130]{3,1,4,2,0:T(4,128)S(1)}, f32[1,4,2,128,130]{3,1,4,2,0:T(4,128)S(1)}, u32[]{:S(2)}, u32[]{:S(2)}) %collective-permute-start.2) | collective-permute-done | bytes 532512 | tf_op jit(solution)/shard_map/ppermute | solution.py:22
  78.8 0.6 convolution_convert_fusion.2
  79.4 0.9 collective-permute-done.3
  80.7 2.1 fusion.81
  82.8 0.5 copy.70
  83.4 1.5 copy.71
  84.8 1.8 pad_maximum_fusion.2
  86.7 1.5 collective-permute-start.4
  88.1 1.8 collective-permute-start.6
  89.9 1.5 convert_element_type.131
  91.4 40.1 %reduce-scatter.4.cloned.1.call-done = f32[32,4096]{1,0:T(8,128)} async-done(((f32[128,4096]{1,0:T(8,128)}), f32[32,4096]{1,0:T(8,128)}) %reduce-scatter.4.cloned.1.call-update) | async-done | bytes 524304 | tf_op jit(solution)/shard_map/reduce_scatter | solution.py:221
  131.5 1.4 fusion.21
  132.9 0.8 fusion.23
  133.8 13.3 %collective-permute-done.4 = bf16[1024,896]{1,0:T(8,128)(2,1)} collective-permute-done((bf16[1024,896]{1,0:T(8,128)(2,1)}, bf16[1024,896]{1,0:T(8,128)(2,1)}, u32[]{:S(2)}, u32[]{:S(2)}) %collective-permute-start.4) | collective-permute-done | bytes 1835040 | tf_op jit(solution)/shard_map/ppermute | solution.py:124
  147.1 1.3 slice.146
  148.4 0.3 collective-permute-start.5
  148.7 1.3 slice.147
  150.0 3.0 collective-permute-start.7
  153.0 0.6 fusion.93
  153.6 17.6 %collective-permute-done.5 = bf16[512,896]{1,0:T(8,128)(2,1)S(1)} collective-permute-done((bf16[512,896]{1,0:T(8,128)(2,1)S(1)}, bf16[512,896]{1,0:T(8,128)(2,1)S(1)}, u32[]{:S(2)}, u32[]{:S(2)}) %collective-permute-start.5) | collective-permute-done | bytes 917536 | tf_op jit(solution)/shard_map/ppermute | solution.py:128
  171.2 0.6 collective-permute-done.7
  171.9 5.9 %pad_maximum_fusion = bf16[4,1024,896]{2,1,0:T(8,128)(2,1)} fusion(bf16[1,1024,896]{2,1,0:T(8,128)(2,1)} %bitcast.50, bf16[1,1024,896]{2,1,0:T(8,128)(2,1)S(1)} %maximum_bitcast_fusion.1, bf16[1,1024,896]{2,1,0:T(8,128)(2,1)} %bitcast.48, bf16[1,1024,896]{2,1,0:T(8,128)(2,1)S(1)} %fusion.93), kind=kLoop, calls=%fused_computation.7 | loop fusion | flops 11010048 | bytes 14680064 | tf_op jit(solution)/shard_map/stack | solution.py:142
  177.9 3.7 %collective-permute-start.10 = (bf16[448,1024]{1,0:T(8,128)(2,1)S(1)}, bf16[448,1024]{1,0:T(8,128)(2,1)S(1)}, u32[]{:S(2)}, u32[]{:S(2)}) collective-permute-start(bf16[448,1024]{1,0:T(8,128)(2,1)S(1)} %copy-done.8), channel_id=1, source_target_pairs={{0,3},{1,0},{2,1},{3,2},{4,7},{5,4},{6,5},{7,6},{8,11},{9,8},{10,9... | collective-permute-start | bytes 2752520 | tf_op jit(solution)/shard_map/ppermute | solution.py:125
  181.6 20.2 %collective-permute-done.10 = bf16[448,1024]{1,0:T(8,128)(2,1)S(1)} collective-permute-done((bf16[448,1024]{1,0:T(8,128)(2,1)S(1)}, bf16[448,1024]{1,0:T(8,128)(2,1)S(1)}, u32[]{:S(2)}, u32[]{:S(2)}) %collective-permute-start.10) | collective-permute-done | bytes 917536 | tf_op jit(solution)/shard_map/ppermute | solution.py:125
  201.8 3.8 %collective-permute-start.11 = (bf16[224,1024]{1,0:T(8,128)(2,1)S(1)}, bf16[224,1024]{1,0:T(8,128)(2,1)S(1)}, u32[]{:S(2)}, u32[]{:S(2)}) collective-permute-start(bf16[224,1024]{1,0:T(8,128)(2,1)S(1)} %slice.151), channel_id=1, source_target_pairs={{0,3},{1,0},{2,1},{3,2},{4,7},{5,4},{6,5},{7,6},{8,11},{9,8},{10,9... | collective-permute-start | bytes 1376264 | tf_op jit(solution)/shard_map/ppermute | solution.py:133
  205.8 9.3 %collective-permute-done.11 = bf16[224,1024]{1,0:T(8,128)(2,1)S(1)} collective-permute-done((bf16[224,1024]{1,0:T(8,128)(2,1)S(1)}, bf16[224,1024]{1,0:T(8,128)(2,1)S(1)}, u32[]{:S(2)}, u32[]{:S(2)}) %collective-permute-start.11) | collective-permute-done | bytes 458784 | tf_op jit(solution)/shard_map/ppermute | solution.py:133
  215.1 3.6 %collective-permute-done.9 = bf16[224,1024]{1,0:T(8,128)(2,1)} collective-permute-done((bf16[224,1024]{1,0:T(8,128)(2,1)S(1)}, bf16[224,1024]{1,0:T(8,128)(2,1)}, u32[]{:S(2)}, u32[]{:S(2)}) %collective-permute-start.9) | collective-permute-done | bytes 458784 | tf_op jit(solution)/shard_map/ppermute | solution.py:128
  218.7 1.1 maximum_bitcast_fusion.2
  219.8 1.5 maximum_bitcast_fusion
  221.3 2.3 copy.91
  223.6 2.7 constant_dynamic-slice_fusion.5
  226.3 7.6 %fusion.20 = f32[512,896]{1,0:T(8,128)S(1)} fusion(bf16[4096,896]{1,0:T(8,128)(2,1)} %bitcast.51, bf16[512,1024]{1,0:T(8,128)(2,1)S(1)} %get-tuple-element.26, bf16[512,1024]{1,0:T(8,128)(2,1)S(1)} %get-tuple-element.27, bf16[512,1024]{1,0:T(8,128)(2,1)S(1)} %get-tuple-element.28, bf16[512,1024]{1,0:T(8,128)(2,1)S(1)} %get-tuple-element.25), kind=kOutput, calls=%fused_computation.47 | convolution fusion | flops 3774873600 | bytes 13369344 | tf_op jit(solution)/shard_map/dot_general | solution.py:240
  233.9 4.5 %convolution_convert_fusion.1 = bf16[512,4096]{1,0:T(8,128)(2,1)S(1)} fusion(bf16[448,4096]{1,0:T(8,128)(2,1)} %bitcast.76, f32[512,896]{1,0:T(8,128)S(1)} %fusion.20), kind=kOutput, calls=%fused_computation.9 | convolution fusion | flops 1882521600 | bytes 9961472 | tf_op jit(solution)/shard_map/dot_general | solution.py:246
  238.4 7.6 %fusion.19 = f32[512,896]{1,0:T(8,128)S(1)} fusion(bf16[4096,896]{1,0:T(8,128)(2,1)} %bitcast.56, bf16[512,1024]{1,0:T(8,128)(2,1)S(1)} %get-tuple-element.26, bf16[512,1024]{1,0:T(8,128)(2,1)S(1)} %get-tuple-element.27, bf16[512,1024]{1,0:T(8,128)(2,1)S(1)} %get-tuple-element.28, bf16[512,1024]{1,0:T(8,128)(2,1)S(1)} %get-tuple-element.25), kind=kOutput, calls=%fused_computation.46 | convolution fusion | flops 3774873600 | bytes 13369344 | tf_op jit(solution)/shard_map/dot_general | solution.py:240
  246.0 6.4 %add_convert_fusion = bf16[512,4096]{1,0:T(8,128)(2,1)} fusion(bf16[512,4096]{1,0:T(8,128)(2,1)S(1)} %convolution_convert_fusion.1, bf16[448,4096]{1,0:T(8,128)(2,1)} %collective-permute-done.13, f32[512,896]{1,0:T(8,128)S(1)} %fusion.19), kind=kOutput, calls=%fused_computation.6 | convolution fusion | flops 1890910208 | bytes 14155776 | tf_op jit(solution)/shard_map/dot_general | solution.py:246
  252.5 46.5 %reduce-scatter.6.cloned.1.call-done = bf16[128,4096]{1,0:T(8,128)(2,1)} async-done(((bf16[512,4096]{1,0:T(8,128)(2,1)}), bf16[128,4096]{1,0:T(8,128)(2,1)}) %reduce-scatter.6.cloned.1.call-update) | async-done | bytes 1048592 | tf_op jit(solution)/shard_map/reduce_scatter | solution.py:249
  299.3 25.6 %reduce-scatter.8.cloned.1.call-done = bf16[32,4096]{1,0:T(8,128)(2,1)} async-done(((bf16[128,4096]{1,0:T(8,128)(2,1)}), bf16[32,4096]{1,0:T(8,128)(2,1)}) %reduce-scatter.8.cloned.1.call-update) | async-done | bytes 262160 | tf_op jit(solution)/shard_map/reduce_scatter | solution.py:250
  325.0 1.0 copy.113
  326.0 0.6 gather_fusion
  326.7 0.7 copy.112
  327.4 4.3 %all-to-all-start = ((bf16[32,4,1024]{2,0,1:T(8,128)(2,1)}), bf16[32,4,1024]{2,0,1:T(8,128)(2,1)S(1)}, u32[]{:S(2)}, u32[]{:S(2)}) async-start(bf16[32,4,1024]{2,0,1:T(8,128)(2,1)} %bitcast.143), calls=%async_computation.3 | async-start | bytes 524288 | tf_op jit(solution)/shard_map/all_to_all | solution.py:258
  331.7 0.8 copy.76
  332.5 5.9 %all-to-all-done = bf16[32,4,1024]{2,0,1:T(8,128)(2,1)S(1)} async-done(((bf16[32,4,1024]{2,0,1:T(8,128)(2,1)}), bf16[32,4,1024]{2,0,1:T(8,128)(2,1)S(1)}, u32[]{:S(2)}, u32[]{:S(2)}) %all-to-all-start) | async-done | bytes 262176 | tf_op jit(solution)/shard_map/all_to_all | solution.py:258
  338.4 0.7 copy.116
  (112 shorter events, 3.9 us)
Async XLA Ops:
  7.2 22.2 %copy-start = (bf16[4096,128]{1,0:T(8,128)(2,1)S(1)}, bf16[4096,128]{1,0:T(8,128)(2,1)}, u32[]{:S(2)}) copy-start(bf16[4096,128]{1,0:T(8,128)(2,1)} %param.16) | copy-start | bytes 3145732
  7.2 124.3 %reduce-scatter.4.cloned.1.call-start = ((), (), s32[]{:S(2)}) async-start(), calls=%async_computation.4 | async-start | bytes 2621440 | tf_op jit(solution)/shard_map/reduce_scatter | solution.py:221
  7.2 7.7 %copy-start.11 = (f32[64]{0:T(128)}, f32[64]{0:T(128)S(1)}, u32[]{:S(2)}) copy-start(f32[64]{0:T(128)S(1)} %multiply_power_fusion) | copy-start | bytes 772
  8.9 2.3 copy-start.15
  9.0 5.9 %copy-start.13 = (f32[128]{0:T(128)}, f32[128]{0:T(128)S(1)}, u32[]{:S(2)}) copy-start(f32[128]{0:T(128)S(1)} %subtract_convert_fusion.1) | copy-start | bytes 1540
  11.2 3.4 copy-start.20
  11.2 4.9 %copy-start.18 = (s32[8,4]{0,1:T(4,128)S(1)}, s32[8,4]{0,1:T(4,128)}, u32[]{:S(2)}) copy-start(s32[8,4]{0,1:T(4,128)} %param.25) | copy-start | bytes 388
  11.3 6.5 %copy-start.4 = (bf16[2048,2,128]{2,1,0:T(2,128)(2,1)S(1)}, bf16[2048,2,128]{2,1,0:T(2,128)(2,1)}, u32[]{:S(2)}) copy-start(bf16[2048,2,128]{2,1,0:T(2,128)(2,1)} %param.23) | copy-start | bytes 3145732
  16.1 10.5 %collective-permute-start = (bf16[128,1,4,128]{3,0,2,1:T(8,128)(2,1)}, bf16[128,1,4,128]{3,0,2,1:T(8,128)(2,1)S(1)}, u32[]{:S(2)}, u32[]{:S(2)}) collective-permute-start(bf16[128,1,4,128]{3,0,2,1:T(8,128)(2,1)} %pad_maximum_fusion.7), channel_id=1, source_target_pairs={{0,4},{4,0},{1,5},{5,1},{2,6},{6,2},{3,7},{7,3},{8,12},{12,8},{9,1... | collective-permute-start | bytes 393224 | tf_op jit(solution)/shard_map/ppermute | solution.py:22
  20.0 9.4 %copy-start.2 = (bf16[128,4096]{1,0:T(8,128)(2,1)S(1)}, bf16[128,4096]{1,0:T(8,128)(2,1)}, u32[]{:S(2)}) copy-start(bf16[128,4096]{1,0:T(8,128)(2,1)} %param.13) | copy-start | bytes 3145732
  20.1 10.5 %copy-start.5 = (bf16[2048,1,128]{2,1,0:T(2,128)(2,1)S(1)}, bf16[2048,1,128]{2,1,0:T(2,128)(2,1)}, u32[]{:S(2)}) copy-start(bf16[2048,1,128]{2,1,0:T(2,128)(2,1)} %get-tuple-element.31) | copy-start | bytes 1572868
  27.3 5.1 %copy-start.12 = (f32[64]{0:T(128)S(1)}, f32[64]{0:T(128)}, u32[]{:S(2)}) copy-start(f32[64]{0:T(128)} %copy-done.11) | copy-start | bytes 772
  27.4 5.1 %copy-start.14 = (f32[128]{0:T(128)S(1)}, f32[128]{0:T(128)}, u32[]{:S(2)}) copy-start(f32[128]{0:T(128)} %copy-done.13) | copy-start | bytes 1540
  27.4 9.3 %collective-permute-start.1 = (bf16[2,128,1,4,128]{4,1,3,2,0:T(8,128)(2,1)}, bf16[2,128,1,4,128]{4,1,3,2,0:T(8,128)(2,1)}, u32[]{:S(2)}, u32[]{:S(2)}) collective-permute-start(bf16[2,128,1,4,128]{4,1,3,2,0:T(8,128)(2,1)} %maximum_select_fusion.1), channel_id=1, source_target_pairs={{0,8},{8,0},{16,24},{24,16},{1,9},{9,1},{17,25},{25,17},{2,10},{10... | collective-permute-start | bytes 786440 | tf_op jit(solution)/shard_map/ppermute | solution.py:22
  30.6 7.4 %copy-start.7 = (bf16[2048,64]{1,0:T(8,128)(2,1)S(1)}, bf16[2048,64]{1,0:T(8,128)(2,1)}, u32[]{:S(2)}) copy-start(bf16[2048,64]{1,0:T(8,128)(2,1)} %get-tuple-element.29) | copy-start | bytes 786436
  47.2 10.3 %copy-start.6 = (bf16[2048,1,128]{0,2,1:T(8,128)(2,1)S(1)}, bf16[2048,1,128]{0,2,1:T(8,128)(2,1)}, u32[]{:S(2)}) copy-start(bf16[2048,1,128]{0,2,1:T(8,128)(2,1)} %copy.85) | copy-start | bytes 1572868
  63.8 2.2 copy-start.16
  63.9 14.8 %copy-start.19 = (bf16[4096,128]{1,0:T(8,128)(2,1)S(1)}, bf16[4096,128]{1,0:T(8,128)(2,1)}, u32[]{:S(2)}) copy-start(bf16[4096,128]{1,0:T(8,128)(2,1)} %param.17) | copy-start | bytes 3145732
  63.9 14.8 %copy-start.21 = (f32[128]{0:T(128)S(1)}, f32[128]{0:T(128)}, u32[]{:S(2)}) copy-start(f32[128]{0:T(128)} %copy-done.20) | copy-start | bytes 1540
  64.2 14.0 %collective-permute-start.2 = (f32[1,4,2,128,130]{3,1,4,2,0:T(4,128)S(1)}, f32[1,4,2,128,130]{3,1,4,2,0:T(4,128)S(1)}, u32[]{:S(2)}, u32[]{:S(2)}) collective-permute-start(f32[1,4,2,128,130]{3,1,4,2,0:T(4,128)S(1)} %copy.63), channel_id=1, source_target_pairs={{0,8},{8,0},{16,24},{24,16},{1,9},{9,1},{17,25},{25,17},{2,10},{10... | collective-permute-start | bytes 1597448 | tf_op jit(solution)/shard_map/ppermute | solution.py:22
  78.4 2.3 copy-start.3
  78.5 1.8 collective-permute-start.3
  80.7 2.2 copy-start.9
  82.8 140.9 %all-gather.2.cloned.1.call-start = ((), (), s32[]{:S(2)}) async-start(), calls=%async_computation.5 | async-start | bytes 4456448 | tf_op jit(solution)/shard_map/all_gather | solution.py:229
  84.8 6.6 %copy-start.10 = (bf16[4096]{0:T(1024)(128)(2,1)S(1)}, bf16[4096]{0:T(1024)(128)(2,1)}, u32[]{:S(2)}) copy-start(bf16[4096]{0:T(1024)(128)(2,1)} %param.19) | copy-start | bytes 24580
  86.7 60.4 %collective-permute-start.4 = (bf16[1024,896]{1,0:T(8,128)(2,1)}, bf16[1024,896]{1,0:T(8,128)(2,1)}, u32[]{:S(2)}, u32[]{:S(2)}) collective-permute-start(bf16[1024,896]{1,0:T(8,128)(2,1)} %pad_maximum_fusion.2), channel_id=1, source_target_pairs={{0,1},{1,2},{2,3},{3,0},{4,5},{5,6},{6,7},{7,4},{8,9},{9,10},{10,1... | collective-permute-start | bytes 5505032 | tf_op jit(solution)/shard_map/ppermute | solution.py:124
  88.1 60.6 %collective-permute-start.6 = (bf16[1024,896]{1,0:T(8,128)(2,1)}, bf16[1024,896]{1,0:T(8,128)(2,1)}, u32[]{:S(2)}, u32[]{:S(2)}) collective-permute-start(bf16[1024,896]{1,0:T(8,128)(2,1)} %pad_maximum_fusion.2), channel_id=1, source_target_pairs={{0,3},{1,0},{2,1},{3,2},{4,7},{5,4},{6,5},{7,6},{8,11},{9,8},{10,9... | collective-permute-start | bytes 5505032 | tf_op jit(solution)/shard_map/ppermute | solution.py:125
  133.8 165.2 %reduce-scatter.6.cloned.1.call-start = ((), (), s32[]{:S(2)}) async-start(), calls=%async_computation.6 | async-start | bytes 5242880 | tf_op jit(solution)/shard_map/reduce_scatter | solution.py:249
  148.4 22.8 %collective-permute-start.5 = (bf16[512,896]{1,0:T(8,128)(2,1)S(1)}, bf16[512,896]{1,0:T(8,128)(2,1)S(1)}, u32[]{:S(2)}, u32[]{:S(2)}) collective-permute-start(bf16[512,896]{1,0:T(8,128)(2,1)S(1)} %slice.146), channel_id=1, source_target_pairs={{0,1},{1,2},{2,3},{3,0},{4,5},{5,6},{6,7},{7,4},{8,9},{9,10},{10,1... | collective-permute-start | bytes 2752520 | tf_op jit(solution)/shard_map/ppermute | solution.py:128
  150.0 21.8 %collective-permute-start.7 = (bf16[512,896]{1,0:T(8,128)(2,1)S(1)}, bf16[512,896]{1,0:T(8,128)(2,1)S(1)}, u32[]{:S(2)}, u32[]{:S(2)}) collective-permute-start(bf16[512,896]{1,0:T(8,128)(2,1)S(1)} %slice.147), channel_id=1, source_target_pairs={{0,3},{1,0},{2,1},{3,2},{4,7},{5,4},{6,5},{7,6},{8,11},{9,8},{10,9... | collective-permute-start | bytes 2752520 | tf_op jit(solution)/shard_map/ppermute | solution.py:133
  171.9 5.9 %copy-start.8 = (bf16[448,1024]{1,0:T(8,128)(2,1)S(1)}, bf16[448,1024]{1,0:T(8,128)(2,1)}, u32[]{:S(2)}) copy-start(bf16[448,1024]{1,0:T(8,128)(2,1)} %param.22) | copy-start | bytes 2752516
  177.8 60.5 %collective-permute-start.12 = (bf16[4,1024,896]{2,1,0:T(8,128)(2,1)}, bf16[4,1024,896]{2,1,0:T(8,128)(2,1)}, u32[]{:S(2)}, u32[]{:S(2)}) collective-permute-start(bf16[4,1024,896]{2,1,0:T(8,128)(2,1)} %pad_maximum_fusion), channel_id=1, source_target_pairs={{0,4},{4,0},{1,5},{5,1},{2,6},{6,2},{3,7},{7,3},{8,12},{12,8},{9,1... | collective-permute-start | bytes 22020104 | tf_op jit(solution)/shard_map/ppermute | solution.py:22
  177.9 23.9 %collective-permute-start.10 = (bf16[448,1024]{1,0:T(8,128)(2,1)S(1)}, bf16[448,1024]{1,0:T(8,128)(2,1)S(1)}, u32[]{:S(2)}, u32[]{:S(2)}) collective-permute-start(bf16[448,1024]{1,0:T(8,128)(2,1)S(1)} %copy-done.8), channel_id=1, source_target_pairs={{0,3},{1,0},{2,1},{3,2},{4,7},{5,4},{6,5},{7,6},{8,11},{9,8},{10,9... | collective-permute-start | bytes 2752520 | tf_op jit(solution)/shard_map/ppermute | solution.py:125
  181.6 24.0 %collective-permute-start.8 = (bf16[448,1024]{1,0:T(8,128)(2,1)S(1)}, bf16[448,1024]{1,0:T(8,128)(2,1)S(1)}, u32[]{:S(2)}, u32[]{:S(2)}) collective-permute-start(bf16[448,1024]{1,0:T(8,128)(2,1)S(1)} %copy-done.8), channel_id=1, source_target_pairs={{0,1},{1,2},{2,3},{3,0},{4,5},{5,6},{6,7},{7,4},{8,9},{9,10},{10,1... | collective-permute-start | bytes 2752520 | tf_op jit(solution)/shard_map/ppermute | solution.py:124
  201.8 13.3 %collective-permute-start.11 = (bf16[224,1024]{1,0:T(8,128)(2,1)S(1)}, bf16[224,1024]{1,0:T(8,128)(2,1)S(1)}, u32[]{:S(2)}, u32[]{:S(2)}) collective-permute-start(bf16[224,1024]{1,0:T(8,128)(2,1)S(1)} %slice.151), channel_id=1, source_target_pairs={{0,3},{1,0},{2,1},{3,2},{4,7},{5,4},{6,5},{7,6},{8,11},{9,8},{10,9... | collective-permute-start | bytes 1376264 | tf_op jit(solution)/shard_map/ppermute | solution.py:133
  205.6 13.1 %collective-permute-start.9 = (bf16[224,1024]{1,0:T(8,128)(2,1)S(1)}, bf16[224,1024]{1,0:T(8,128)(2,1)}, u32[]{:S(2)}, u32[]{:S(2)}) collective-permute-start(bf16[224,1024]{1,0:T(8,128)(2,1)S(1)} %slice.150), channel_id=1, source_target_pairs={{0,1},{1,2},{2,3},{3,0},{4,5},{5,6},{6,7},{7,4},{8,9},{9,10},{10,1... | collective-permute-start | bytes 1376264 | tf_op jit(solution)/shard_map/ppermute | solution.py:128
  223.6 22.3 %collective-permute-start.13 = (bf16[448,4096]{1,0:T(8,128)(2,1)}, bf16[448,4096]{1,0:T(8,128)(2,1)}, u32[]{:S(2)}, u32[]{:S(2)}) collective-permute-start(bf16[448,4096]{1,0:T(8,128)(2,1)} %bitcast.76), channel_id=1, source_target_pairs={{0,4},{4,0},{1,5},{5,1},{2,6},{6,2},{3,7},{7,3},{8,12},{12,8},{9,1... | collective-permute-start | bytes 11010056 | tf_op jit(solution)/shard_map/ppermute | solution.py:22
  252.4 46.8 %copy-start.17 = (s32[128]{0:T(128)S(1)}, s32[128]{0:T(128)}, u32[]{:S(2)}) copy-start(s32[128]{0:T(128)} %copy-done.15) | copy-start | bytes 1540
  252.4 86.6 %copy-start.1 = (bf16[4096,128]{1,0:T(8,128)(2,1)S(1)}, bf16[4096,128]{1,0:T(8,128)(2,1)}, u32[]{:S(2)}) copy-start(bf16[4096,128]{1,0:T(8,128)(2,1)} %param.16) | copy-start | bytes 3145732
  252.4 72.6 %reduce-scatter.8.cloned.1.call-start = ((), (), s32[]{:S(2)}) async-start(), calls=%async_computation.7 | async-start | bytes 1310720 | tf_op jit(solution)/shard_map/reduce_scatter | solution.py:250
  327.4 11.0 %all-to-all-start = ((bf16[32,4,1024]{2,0,1:T(8,128)(2,1)}), bf16[32,4,1024]{2,0,1:T(8,128)(2,1)S(1)}, u32[]{:S(2)}, u32[]{:S(2)}) async-start(bf16[32,4,1024]{2,0,1:T(8,128)(2,1)} %bitcast.143), calls=%async_computation.3 | async-start | bytes 524288 | tf_op jit(solution)/shard_map/all_to_all | solution.py:258
Sparse Core Ops, SparseCore 0:
  82.9 48.5 reduce-scatter.3
  134.2 51.1 all-gather.1
  252.5 46.3 reduce-scatter.5
  301.2 23.7 reduce-scatter.7

commit v5 on v4

--- a/solution.py
+++ b/solution.py
@@ -16,6 +16,43 @@
 
 rope_base = 500000.0
 eps = 1e-05
+
+
+def shifted(value, axis, size, shift):
+    return lax.ppermute(value, axis, [(i, (i + shift) % size) for i in range(size)])
+
+
+def gather_plane(rows, n_ax, n_az):
+    half = rows.shape[1] // 2
+    part_a = rows[:, :half]
+    part_b = rows[:, half:]
+    a_z = jnp.stack([part_a] + [shifted(part_a, "az", n_az, d) for d in range(1, n_az)])
+    b_x = jnp.stack([part_b] + [shifted(part_b, "ax", n_ax, d) for d in range(1, n_ax)])
+    a_zx = jnp.stack([a_z] + [shifted(a_z, "ax", n_ax, d) for d in range(1, n_ax)])
+    b_xz = jnp.stack([b_x] + [shifted(b_x, "az", n_az, d) for d in range(1, n_az)])
+    return jnp.concatenate(
+        [a_zx.reshape(-1, half), jnp.swapaxes(b_xz, 0, 1).reshape(-1, half)], axis=1
+    )
+
+
+def reduce_plane(blocks, n_ax, n_az):
+    rows = blocks.shape[0] // (n_ax * n_az)
+    half = blocks.shape[1] // 2
+    blocks = blocks.reshape(n_ax, n_az, rows, 2 * half)
+    part_a = blocks[..., :half]
+    part_b = blocks[..., half:]
+
+    def fold(stack, axis, size):
+        total = stack[0].astype(jnp.float32)
+        for d in range(1, size):
+            total = total + shifted(stack[d], axis, size, -d).astype(jnp.float32)
+        return total
+
+    a_1 = fold(part_a, "ax", n_ax).astype(jnp.bfloat16)
+    a_2 = fold(a_1, "az", n_az)
+    b_1 = fold(jnp.swapaxes(part_b, 0, 1), "az", n_az).astype(jnp.bfloat16)
+    b_2 = fold(b_1, "ax", n_ax)
+    return jnp.concatenate([a_2, b_2], axis=1)
 
 
 def swap_with_partner(value, axis, size):
@@ -226,7 +263,8 @@
     residual = (hidden_rows + head_rows).astype(jnp.bfloat16)
     normed_mlp = rms_norm(residual.astype(jnp.float32), mlp_gain).astype(jnp.bfloat16)
 
-    tokens = lax.all_gather(normed_mlp, REQ[:2], axis=0, tiled=True)
+    n_ax = lax.axis_size("ax")
+    tokens = gather_plane(normed_mlp, n_ax, n_az)
     tokens_ring = jnp.concatenate(
         [
             lax.dynamic_slice_in_dim(tokens, quarter_of[ring] * width_part, width_part, 1)
@@ -246,8 +284,7 @@
         term = jnp.dot(acts[core], down_pair[core], preferred_element_type=jnp.float32)
         term = term.astype(jnp.bfloat16).astype(jnp.float32)
         down_sum = term if down_sum is None else down_sum + term
-    down = lax.psum_scatter(down_sum.astype(jnp.bfloat16), "ax", scatter_dimension=0, tiled=True)
-    down = lax.psum_scatter(down, "az", scatter_dimension=0, tiled=True)
+    down = reduce_plane(down_sum.astype(jnp.bfloat16), n_ax, n_az)
     down = down.reshape(rows_here, n_mlp, width_part)
     natural = jnp.stack([(mlp_index - j) % n_mlp for j in range(n_mlp)])
     down = jnp.take(down, natural, axis=1).reshape(rows_here, n_mlp * width_part)

time: 347 us -> 343 us (0.988); the launches traced: 346 us -> 337 us
  waiting for transfers between devices: 199 us -> 151 us
  starting transfers between devices: 22.7 us -> 59.4 us
  local copies, waits for them, and re-layouts: 18.4 us -> 24.5 us
  matrix products: 49.3 us -> 44.5 us
    reduce_scatter x2 -> x0, waiting for transfers between devices: 72.1 us -> none  [the longest x1 46.5 us: layer(): lax.psum_scatter(down_sum.astype(jnp.bfloat16), 'ax', scatter_dimension=0...]
    ppermute x0 -> x24, waiting for transfers between devices: none -> 71.5 us  [shifted(): lax.ppermute(value, axis, [(i, (i + shift) % size) for i in range(size)])]
    reduce_scatter x1, waiting for transfers between devices: 40.1 us -> 0.01 us  [layer(): lax.psum_scatter(head_terms, 'mlp', scatter_dimension=0, tiled=True)]
    ppermute x0 -> x24, starting transfers between devices: none -> 36.8 us  [shifted(): lax.ppermute(value, axis, [(i, (i + shift) % size) for i in range(size)])]
    ppermute x2, waiting for transfers between devices: 20.2 us -> 0.01 us  [layer(): lax.ppermute(own, 'mlp', [(i, (i - 1) % n_mlp) for i in range(n_mlp)])]
    ppermute x2, waiting for transfers between devices: 21.2 us -> 31.5 us  [layer(): lax.ppermute((from_left[0][:half_gu], from_left[1][:half_wd]), 'mlp', [(i...]
    ppermute x2, waiting for transfers between devices: 13.3 us -> 20.4 us  [layer(): lax.ppermute(own, 'mlp', [(i, (i + 1) % n_mlp) for i in range(n_mlp)])]
    dot_general x2, matrix products: 10.9 us -> 4.89 us  [layer(): jnp.dot(acts[core], down_pair[core], preferred_element_type=jnp.float32)]
  transfers between devices with their start and end apart: 19 -> 40, of which waited for: 13 -> 18; matrix products, arithmetic and copies ran while one was open for 17% -> 30% of each run, Pallas kernels for 0% -> 0%
where the time goes in v5:
time: 343 us; the launch traced here: 337 us
  waiting for transfers between devices  151 us (44%)
  starting transfers between devices  59.4 us (17%)
  matrix products  44.5 us (13%)
  other arithmetic  41.7 us (12%)
  local copies, waits for them, and re-layouts  24.5 us (7%)
  between operations  15.7 us (5%)
    ppermute x24, waiting for transfers between devices, shifted(): lax.ppermute(value, axis, [(i, (i + shift) % size) for i in range(size)])  71.5 us
    ppermute x24, starting transfers between devices, shifted(): lax.ppermute(value, axis, [(i, (i + shift) % size) for i in range(size)])  36.8 us
    ppermute x2, waiting for transfers between devices, layer(): lax.ppermute((from_left[0][:half_gu], from_left[1][:half_wd]), 'mlp', [(i...  31.5 us
    ppermute x2, waiting for transfers between devices, layer(): lax.ppermute(own, 'mlp', [(i, (i + 1) % n_mlp) for i in range(n_mlp)])  20.4 us
    dot_general x2, matrix products, layer(): jnp.dot(tokens_ring, weights_here, preferred_element_type=jnp.float32)  15.2 us
    ppermute x6, waiting for transfers between devices, swap_with_partner(): lax.ppermute(value, axis, [(source, source ^ 1) for source in range(size)])  14.3 us
    convert_element_type x1, other arithmetic, partial_attention(): weights.astype(jnp.bfloat16)  10.3 us
    dot_general x2, matrix products, partial_attention(): jnp.einsum('qkgd,nkd->kgqn', grouped_queries, key_block, preferred_elemen...  9.51 us
  transfers between devices with their start and end apart: 40, of which 18 were waited for; matrix products, arithmetic and copies ran while one was open for 30% of the time, Pallas kernels for 0%

profile of v5, /device:TPU:0, one launch (start us, length us, event | category | flops | bytes accessed | tf_op | source)
XLA Modules:
  0.0 337.3 jit_solution(14087318718729694557)
XLA Ops:
  7.2 1.5 copy.96
  8.8 1.5 copy.97
  10.3 1.8 pad_maximum_fusion.3
  12.1 1.7 collective-permute-start.16
  13.8 1.5 collective-permute-start.18
  15.8 1.5 multiply_reduce_fusion
  17.8 4.0 %fusion.91 = f32[128,512]{1,0:T(8,128)} fusion(bf16[4096,512]{1,0:T(8,128)(2,1)} %param.15, f32[4096]{0:T(1024)S(1)} %convert_element_type.197, f32[128]{0:T(128)S(1)} %add_rsqrt_fusion.1, bf16[128,4096]{1,0:T(8,128)(2,1)} %param.13), kind=kOutput, calls=%fused_computation.213 | convolution fusion | flops 538968064 | bytes 5521920 | tf_op jit(solution)/shard_map/dot_general | solution.py:191
  26.5 4.1 %fusion.94 = (bf16[2048,1,128]{2,1,0:T(2,128)(2,1)}, bf16[2048,1,128]{2,1,0:T(2,128)(2,1)S(1)}) fusion(bf16[2048,2,128]{2,1,0:T(2,128)(2,1)} %param.23), kind=kLoop, calls=%fused_computation.214 | loop fusion | bytes 2097152 | tf_op jit(solution)/shard_map/slice | solution.py:217
  30.7 5.6 %fusion.46 = (bf16[2048,64]{1,0:T(8,128)(2,1)}, bf16[2048,64]{1,0:T(8,128)(2,1)}) fusion(f32[2048,1,128]{2,0,1:T(8,128)S(1)} %copy_convert_fusion, f32[64]{0:T(128)S(1)} %copy-done.10, f32[2048]{0:T(1024)S(1)} %add_convert_fusion.3), kind=kLoop, calls=%fused_computation.103 | loop fusion | flops 1179648 | bytes 1581312 | tf_op jit(solution)/shard_map/concatenate | solution.py:70
  37.2 2.2 collective-permute-start.1
  39.3 1.8 convolution_bitcast_fusion.1
  41.2 3.6 %copy.112 = bf16[2048,1,128]{0,2,1:T(8,128)(2,1)} copy(bf16[2048,1,128]{2,1,0:T(2,128)(2,1)} %get-tuple-element.39) | data formatting | bytes 1048576
  45.0 1.6 collective-permute-done.1
  46.6 1.3 maximum_select_fusion
  48.0 9.2 %bitcast_reduce_fusion = (f32[4,512]{1,0:T(4,128)S(1)}, f32[2048,512,4]{0,1,2:T(8,128)}) fusion(bf16[512,4,128]{2,0,1:T(8,128)(2,1)S(1)} %bitcast.225, bf16[2048,64]{1,0:T(8,128)(2,1)} %get-tuple-element.38, bf16[2048,64]{1,0:T(8,128)(2,1)S(1)} %copy-done.4), kind=kOutput, calls=%fused_computation.2 | convolution fusion | flops 1083176960 | bytes 17833984 | tf_op jit(solution)/shard_map/qkgd,nkd->kgqn/dot_general | solution.py:97
  57.2 10.3 %fusion.2 = (bf16[1,4,512,2048]{3,2,1,0:T(8,128)(2,1)}, f32[4,512]{1,0:T(4,128)S(1)}) fusion(f32[2048,512,4]{0,1,2:T(8,128)} %get-tuple-element.66, f32[4,512]{1,0:T(4,128)S(1)} %get-tuple-element.65), kind=kLoop, calls=%fused_computation.5 | loop fusion | flops 16775168 | bytes 25182208 | tf_op jit(solution)/shard_map/convert_element_type | solution.py:107
  67.5 6.3 %convolution_bitcast_fusion = f32[1,4,4,128,128]{3,4,2,1,0:T(8,128)S(1)} fusion(bf16[4,4,128,2048]{3,2,1,0:T(8,128)(2,1)} %bitcast.217, bf16[2048,1,128]{0,2,1:T(8,128)(2,1)} %copy.112), kind=kOutput, calls=%fused_computation.33 | convolution fusion | flops 1073741824 | bytes 9961472 | tf_op jit(solution)/shard_map/kgqn,nkd->kgqd/dot_general | solution.py:105
  74.2 1.8 collective-permute-start.2
  76.5 11.8 %collective-permute-done.2 = f32[1,4,2,128,130]{3,1,4,2,0:T(4,128)S(1)} collective-permute-done((f32[1,4,2,128,130]{3,1,4,2,0:T(4,128)S(1)}, f32[1,4,2,128,130]{3,1,4,2,0:T(4,128)S(1)}, u32[]{:S(2)}, u32[]{:S(2)}) %collective-permute-start.2) | collective-permute-done | bytes 532512 | tf_op jit(solution)/shard_map/ppermute | solution.py:59
  90.6 2.0 fusion.98
  92.7 1.3 slice.229
  94.3 1.3 slice.230
  95.5 3.0 collective-permute-start.19
  99.1 31.5 %collective-permute-done.17 = bf16[512,896]{1,0:T(8,128)(2,1)S(1)} collective-permute-done((bf16[512,896]{1,0:T(8,128)(2,1)S(1)}, bf16[512,896]{1,0:T(8,128)(2,1)S(1)}, u32[]{:S(2)}, u32[]{:S(2)}) %collective-permute-start.17) | collective-permute-done | bytes 917536 | tf_op jit(solution)/shard_map/ppermute | solution.py:165
  130.6 4.3 %collective-permute-done.19 = bf16[512,896]{1,0:T(8,128)(2,1)S(1)} collective-permute-done((bf16[512,896]{1,0:T(8,128)(2,1)S(1)}, bf16[512,896]{1,0:T(8,128)(2,1)S(1)}, u32[]{:S(2)}, u32[]{:S(2)}) %collective-permute-start.19) | collective-permute-done | bytes 917536 | tf_op jit(solution)/shard_map/ppermute | solution.py:170
  135.1 5.8 %pad_maximum_fusion = bf16[4,1024,896]{2,1,0:T(8,128)(2,1)} fusion(bf16[1,1024,896]{2,1,0:T(8,128)(2,1)} %bitcast.69, bf16[1,1024,896]{2,1,0:T(8,128)(2,1)S(1)} %maximum_bitcast_fusion.2, bf16[1,1024,896]{2,1,0:T(8,128)(2,1)} %bitcast.67, bf16[1,1024,896]{2,1,0:T(8,128)(2,1)S(1)} %fusion.110), kind=kLoop, calls=%fused_computation.7 | loop fusion | flops 11010048 | bytes 14680064 | tf_op jit(solution)/shard_map/stack | solution.py:179
  140.9 4.2 %collective-permute-start.22 = (bf16[448,1024]{1,0:T(8,128)(2,1)}, bf16[448,1024]{1,0:T(8,128)(2,1)}, u32[]{:S(2)}, u32[]{:S(2)}) collective-permute-start(bf16[448,1024]{1,0:T(8,128)(2,1)} %param.22), channel_id=1, source_target_pairs={{0,3},{1,0},{2,1},{3,2},{4,7},{5,4},{6,5},{7,6},{8,11},{9,8},{10,9... | collective-permute-start | bytes 2752520 | tf_op jit(solution)/shard_map/ppermute | solution.py:162
  145.5 20.4 %collective-permute-done.20 = bf16[448,1024]{1,0:T(8,128)(2,1)} collective-permute-done((bf16[448,1024]{1,0:T(8,128)(2,1)}, bf16[448,1024]{1,0:T(8,128)(2,1)}, u32[]{:S(2)}, u32[]{:S(2)}) %collective-permute-start.20) | collective-permute-done | bytes 917536 | tf_op jit(solution)/shard_map/ppermute | solution.py:161
  165.9 1.8 slice.233
  167.7 1.2 fusion.31
  169.8 1.4 collective-permute-start.10
  171.2 2.8 collective-permute-start.11
  173.9 1.4 collective-permute-start.12
  175.4 1.8 slice.234
  177.2 3.2 collective-permute-start.23
  180.4 1.6 collective-permute-start.4
  182.1 2.0 collective-permute-start.13
  184.1 1.8 collective-permute-start.14
  186.0 3.5 %collective-permute-done.23 = bf16[224,1024]{1,0:T(8,128)(2,1)} collective-permute-done((bf16[224,1024]{1,0:T(8,128)(2,1)}, bf16[224,1024]{1,0:T(8,128)(2,1)}, u32[]{:S(2)}, u32[]{:S(2)}) %collective-permute-start.23) | collective-permute-done | bytes 458784 | tf_op jit(solution)/shard_map/ppermute | solution.py:170
  189.5 3.5 %collective-permute-start.5 = (bf16[32,2048]{1,0:T(8,128)(2,1)}, bf16[32,2048]{1,0:T(8,128)(2,1)S(1)}, u32[]{:S(2)}, u32[]{:S(2)}) collective-permute-start(bf16[32,2048]{1,0:T(8,128)(2,1)} %get-tuple-element.58), channel_id=1, source_target_pairs={{0,16},{8,24},{16,0},{24,8},{1,17},{9,25},{17,1},{25,9},{2,18},{10... | collective-permute-start | bytes 393224 | tf_op jit(solution)/shard_map/ppermute | solution.py:22
  194.4 1.2 maximum_bitcast_fusion.3
  195.6 17.5 %collective-permute-done.5 = bf16[32,2048]{1,0:T(8,128)(2,1)S(1)} collective-permute-done((bf16[32,2048]{1,0:T(8,128)(2,1)}, bf16[32,2048]{1,0:T(8,128)(2,1)S(1)}, u32[]{:S(2)}, u32[]{:S(2)}) %collective-permute-start.5) | collective-permute-done | bytes 131104 | tf_op jit(solution)/shard_map/ppermute | solution.py:22
  214.6 2.1 collective-permute-start.8
  217.8 2.0 maximum_bitcast_fusion
  220.1 4.6 %collective-permute-done.15 = bf16[4,32,2048]{2,1,0:T(8,128)(2,1)S(1)} collective-permute-done((bf16[4,32,2048]{2,1,0:T(8,128)(2,1)S(1)}, bf16[4,32,2048]{2,1,0:T(8,128)(2,1)S(1)}, u32[]{:S(2)}, u32[]{:S(2)}) %collective-permute-start.15) | collective-permute-done | bytes 524320 | tf_op jit(solution)/shard_map/ppermute | solution.py:22
  225.3 13.0 %collective-permute-done.7 = bf16[4,32,2048]{2,1,0:T(8,128)(2,1)S(1)} collective-permute-done((bf16[4,32,2048]{2,1,0:T(8,128)(2,1)S(1)}, bf16[4,32,2048]{2,1,0:T(8,128)(2,1)S(1)}, u32[]{:S(2)}, u32[]{:S(2)}) %collective-permute-start.7) | collective-permute-done | bytes 524320 | tf_op jit(solution)/shard_map/ppermute | solution.py:22
  239.2 2.5 fusion.18
  241.7 7.6 %fusion.30 = f32[512,896]{1,0:T(8,128)S(1)} fusion(bf16[4096,896]{1,0:T(8,128)(2,1)} %bitcast.70, bf16[512,1024]{1,0:T(8,128)(2,1)S(1)} %get-tuple-element.33, bf16[512,1024]{1,0:T(8,128)(2,1)S(1)} %get-tuple-element.32, bf16[512,1024]{1,0:T(8,128)(2,1)S(1)} %get-tuple-element.31, bf16[512,1024]{1,0:T(8,128)(2,1)S(1)} %get-tuple-element.30), kind=kOutput, calls=%fused_computation.70 | convolution fusion | flops 3774873600 | bytes 13369344 | tf_op jit(solution)/shard_map/dot_general | solution.py:278
  249.3 2.4 convolution_convert_fusion.1
  251.7 7.6 %fusion.29 = f32[512,896]{1,0:T(8,128)S(1)} fusion(bf16[4096,896]{1,0:T(8,128)(2,1)} %bitcast.75, bf16[512,1024]{1,0:T(8,128)(2,1)S(1)} %get-tuple-element.33, bf16[512,1024]{1,0:T(8,128)(2,1)S(1)} %get-tuple-element.32, bf16[512,1024]{1,0:T(8,128)(2,1)S(1)} %get-tuple-element.31, bf16[512,1024]{1,0:T(8,128)(2,1)S(1)} %get-tuple-element.30), kind=kOutput, calls=%fused_computation.69 | convolution fusion | flops 3774873600 | bytes 13369344 | tf_op jit(solution)/shard_map/dot_general | solution.py:278
  259.3 2.5 add_convert_fusion
  261.9 2.5 collective-permute-start.26
  264.4 1.1 collective-permute-start.28
  266.4 3.2 collective-permute-start.33
  269.6 17.2 %collective-permute-done.26 = bf16[4,32,2048]{2,1,0:T(8,128)(2,1)S(1)} collective-permute-done((bf16[4,32,2048]{2,1,0:T(8,128)(2,1)S(1)}, bf16[4,32,2048]{2,1,0:T(8,128)(2,1)S(1)}, u32[]{:S(2)}, u32[]{:S(2)}) %collective-permute-start.26) | collective-permute-done | bytes 524320 | tf_op jit(solution)/shard_map/ppermute | solution.py:22
  286.8 1.8 collective-permute-start.34
  288.6 1.8 collective-permute-done.28
  291.4 3.2 collective-permute-start.30
  294.7 10.2 %collective-permute-done.34 = bf16[4,32,2048]{2,1,0:T(8,128)(2,1)S(1)} collective-permute-done((bf16[4,32,2048]{2,1,0:T(8,128)(2,1)S(1)}, bf16[4,32,2048]{2,1,0:T(8,128)(2,1)S(1)}, u32[]{:S(2)}, u32[]{:S(2)}) %collective-permute-start.34) | collective-permute-done | bytes 524320 | tf_op jit(solution)/shard_map/ppermute | solution.py:22
  305.3 3.9 %collective-permute-start.35 = (bf16[32,2048]{1,0:T(8,128)(2,1)S(1)}, bf16[32,2048]{1,0:T(8,128)(2,1)S(1)}, u32[]{:S(2)}, u32[]{:S(2)}) collective-permute-start(bf16[32,2048]{1,0:T(8,128)(2,1)S(1)} %get-tuple-element.48), channel_id=1, source_target_pairs={{0,96},{32,0},{64,32},{96,64},{1,97},{33,1},{65,33},{97,65},{2,98}... | collective-permute-start | bytes 393224 | tf_op jit(solution)/shard_map/ppermute | solution.py:22
  310.2 2.9 collective-permute-done.35
  313.1 2.7 collective-permute-done.36
  318.4 4.5 %all-to-all-start = ((bf16[32,4,1024]{2,0,1:T(8,128)(2,1)}), bf16[32,4,1024]{2,0,1:T(8,128)(2,1)S(1)}, u32[]{:S(2)}, u32[]{:S(2)}) async-start(bf16[32,4,1024]{2,0,1:T(8,128)(2,1)} %bitcast.215), calls=%async_computation.1 | async-start | bytes 524288 | tf_op jit(solution)/shard_map/all_to_all | solution.py:295
  323.7 5.9 %all-to-all-done = bf16[32,4,1024]{2,0,1:T(8,128)(2,1)S(1)} async-done(((bf16[32,4,1024]{2,0,1:T(8,128)(2,1)}), bf16[32,4,1024]{2,0,1:T(8,128)(2,1)S(1)}, u32[]{:S(2)}, u32[]{:S(2)}) %all-to-all-start) | async-done | bytes 262176 | tf_op jit(solution)/shard_map/all_to_all | solution.py:295
  (163 shorter events, 25.0 us)
Async XLA Ops:
  7.2 32.2 %copy-start = (bf16[4096,128]{1,0:T(8,128)(2,1)S(1)}, bf16[4096,128]{1,0:T(8,128)(2,1)}, u32[]{:S(2)}) copy-start(bf16[4096,128]{1,0:T(8,128)(2,1)} %param.16) | copy-start | bytes 3145732
  7.2 8.2 %copy-start.17 = (s32[1,4]{1,0:T(1,128)S(1)}, s32[1,4]{1,0:T(1,128)}, u32[]{:S(2)}) copy-start(s32[1,4]{1,0:T(1,128)} %param.24) | copy-start | bytes 52
  7.2 8.5 %copy-start.7 = (bf16[4096]{0:T(1024)(128)(2,1)S(1)}, bf16[4096]{0:T(1024)(128)(2,1)}, u32[]{:S(2)}) copy-start(bf16[4096]{0:T(1024)(128)(2,1)} %param.14) | copy-start | bytes 24580
  7.2 160.5 %reduce-scatter.2.cloned.1.call-start = ((), (), s32[]{:S(2)}) async-start(), calls=%async_computation.2 | async-start | bytes 2621440 | tf_op jit(solution)/shard_map/reduce_scatter | solution.py:258
  12.1 80.6 %collective-permute-start.16 = (bf16[1024,896]{1,0:T(8,128)(2,1)}, bf16[1024,896]{1,0:T(8,128)(2,1)}, u32[]{:S(2)}, u32[]{:S(2)}) collective-permute-start(bf16[1024,896]{1,0:T(8,128)(2,1)} %pad_maximum_fusion.3), channel_id=1, source_target_pairs={{0,1},{1,2},{2,3},{3,0},{4,5},{5,6},{6,7},{7,4},{8,9},{9,10},{10,1... | collective-permute-start | bytes 5505032 | tf_op jit(solution)/shard_map/ppermute | solution.py:161
  13.8 80.5 %collective-permute-start.18 = (bf16[1024,896]{1,0:T(8,128)(2,1)}, bf16[1024,896]{1,0:T(8,128)(2,1)}, u32[]{:S(2)}, u32[]{:S(2)}) collective-permute-start(bf16[1024,896]{1,0:T(8,128)(2,1)} %pad_maximum_fusion.3), channel_id=1, source_target_pairs={{0,3},{1,0},{2,1},{3,2},{4,7},{5,4},{6,5},{7,6},{8,11},{9,8},{10,9... | collective-permute-start | bytes 5505032 | tf_op jit(solution)/shard_map/ppermute | solution.py:162
  15.4 7.7 %copy-start.9 = (f32[64]{0:T(128)}, f32[64]{0:T(128)S(1)}, u32[]{:S(2)}) copy-start(f32[64]{0:T(128)S(1)} %multiply_power_fusion) | copy-start | bytes 772
  15.6 1.6 copy-start.14
  15.7 7.3 %copy-start.12 = (f32[128]{0:T(128)}, f32[128]{0:T(128)S(1)}, u32[]{:S(2)}) copy-start(f32[128]{0:T(128)S(1)} %subtract_convert_fusion.1) | copy-start | bytes 1540
  17.3 0.5 copy-start.18
  24.2 12.2 %collective-permute-start = (bf16[128,1,4,128]{3,0,2,1:T(8,128)(2,1)}, bf16[128,1,4,128]{3,0,2,1:T(8,128)(2,1)S(1)}, u32[]{:S(2)}, u32[]{:S(2)}) collective-permute-start(bf16[128,1,4,128]{3,0,2,1:T(8,128)(2,1)} %pad_maximum_fusion.11), channel_id=1, source_target_pairs={{0,4},{4,0},{1,5},{5,1},{2,6},{6,2},{3,7},{7,3},{8,12},{12,8},{9,1... | collective-permute-start | bytes 393224 | tf_op jit(solution)/shard_map/ppermute | solution.py:59
  26.5 4.2 %copy-start.10 = (f32[64]{0:T(128)S(1)}, f32[64]{0:T(128)}, u32[]{:S(2)}) copy-start(f32[64]{0:T(128)} %copy-done.9) | copy-start | bytes 772
  37.1 7.6 %copy-start.11 = (f32[64]{0:T(128)S(1)}, f32[64]{0:T(128)}, u32[]{:S(2)}) copy-start(f32[64]{0:T(128)} %copy-done.9) | copy-start | bytes 772
  37.2 7.6 %copy-start.13 = (f32[128]{0:T(128)S(1)}, f32[128]{0:T(128)}, u32[]{:S(2)}) copy-start(f32[128]{0:T(128)} %copy-done.12) | copy-start | bytes 1540
  37.2 9.5 %collective-permute-start.1 = (bf16[2,128,1,4,128]{4,1,3,2,0:T(8,128)(2,1)}, bf16[2,128,1,4,128]{4,1,3,2,0:T(8,128)(2,1)}, u32[]{:S(2)}, u32[]{:S(2)}) collective-permute-start(bf16[2,128,1,4,128]{4,1,3,2,0:T(8,128)(2,1)} %maximum_select_fusion.1), channel_id=1, source_target_pairs={{0,8},{8,0},{16,24},{24,16},{1,9},{9,1},{17,25},{25,17},{2,10},{10... | collective-permute-start | bytes 786440 | tf_op jit(solution)/shard_map/ppermute | solution.py:59
  41.2 6.8 %copy-start.4 = (bf16[2048,64]{1,0:T(8,128)(2,1)S(1)}, bf16[2048,64]{1,0:T(8,128)(2,1)}, u32[]{:S(2)}) copy-start(bf16[2048,64]{1,0:T(8,128)(2,1)} %get-tuple-element.37) | copy-start | bytes 786436
  73.8 2.2 copy-start.15
  73.9 14.7 %copy-start.2 = (bf16[128,4096]{1,0:T(8,128)(2,1)S(1)}, bf16[128,4096]{1,0:T(8,128)(2,1)}, u32[]{:S(2)}) copy-start(bf16[128,4096]{1,0:T(8,128)(2,1)} %param.13) | copy-start | bytes 3145732
  73.9 14.7 %copy-start.16 = (bf16[4096,128]{1,0:T(8,128)(2,1)S(1)}, bf16[4096,128]{1,0:T(8,128)(2,1)}, u32[]{:S(2)}) copy-start(bf16[4096,128]{1,0:T(8,128)(2,1)} %param.17) | copy-start | bytes 3145732
  74.0 14.7 %copy-start.19 = (f32[128]{0:T(128)S(1)}, f32[128]{0:T(128)}, u32[]{:S(2)}) copy-start(f32[128]{0:T(128)} %copy-done.18) | copy-start | bytes 1540
  74.2 14.0 %collective-permute-start.2 = (f32[1,4,2,128,130]{3,1,4,2,0:T(4,128)S(1)}, f32[1,4,2,128,130]{3,1,4,2,0:T(4,128)S(1)}, u32[]{:S(2)}, u32[]{:S(2)}) collective-permute-start(f32[1,4,2,128,130]{3,1,4,2,0:T(4,128)S(1)} %copy.88), channel_id=1, source_target_pairs={{0,8},{8,0},{16,24},{24,16},{1,9},{9,1},{17,25},{25,17},{2,10},{10... | collective-permute-start | bytes 1597448 | tf_op jit(solution)/shard_map/ppermute | solution.py:59
  88.4 2.2 copy-start.3
  88.5 1.6 collective-permute-start.3
  93.9 36.7 %collective-permute-start.17 = (bf16[512,896]{1,0:T(8,128)(2,1)S(1)}, bf16[512,896]{1,0:T(8,128)(2,1)S(1)}, u32[]{:S(2)}, u32[]{:S(2)}) collective-permute-start(bf16[512,896]{1,0:T(8,128)(2,1)S(1)} %slice.229), channel_id=1, source_target_pairs={{0,1},{1,2},{2,3},{3,0},{4,5},{5,6},{6,7},{7,4},{8,9},{9,10},{10,1... | collective-permute-start | bytes 2752520 | tf_op jit(solution)/shard_map/ppermute | solution.py:165
  95.5 39.4 %collective-permute-start.19 = (bf16[512,896]{1,0:T(8,128)(2,1)S(1)}, bf16[512,896]{1,0:T(8,128)(2,1)S(1)}, u32[]{:S(2)}, u32[]{:S(2)}) collective-permute-start(bf16[512,896]{1,0:T(8,128)(2,1)S(1)} %slice.230), channel_id=1, source_target_pairs={{0,3},{1,0},{2,1},{3,2},{4,7},{5,4},{6,5},{7,6},{8,11},{9,8},{10,9... | collective-permute-start | bytes 2752520 | tf_op jit(solution)/shard_map/ppermute | solution.py:170
  135.1 10.2 %copy-start.8 = (bf16[4096]{0:T(1024)(128)(2,1)S(1)}, bf16[4096]{0:T(1024)(128)(2,1)}, u32[]{:S(2)}) copy-start(bf16[4096]{0:T(1024)(128)(2,1)} %param.19) | copy-start | bytes 24580
  140.9 110.8 %collective-permute-start.24 = (bf16[4,1024,896]{2,1,0:T(8,128)(2,1)}, bf16[4,1024,896]{2,1,0:T(8,128)(2,1)}, u32[]{:S(2)}, u32[]{:S(2)}) collective-permute-start(bf16[4,1024,896]{2,1,0:T(8,128)(2,1)} %pad_maximum_fusion), channel_id=1, source_target_pairs={{0,4},{4,0},{1,5},{5,1},{2,6},{6,2},{3,7},{7,3},{8,12},{12,8},{9,1... | collective-permute-start | bytes 22020104 | tf_op jit(solution)/shard_map/ppermute | solution.py:59
  140.9 25.0 %collective-permute-start.20 = (bf16[448,1024]{1,0:T(8,128)(2,1)}, bf16[448,1024]{1,0:T(8,128)(2,1)}, u32[]{:S(2)}, u32[]{:S(2)}) collective-permute-start(bf16[448,1024]{1,0:T(8,128)(2,1)} %param.22), channel_id=1, source_target_pairs={{0,1},{1,2},{2,3},{3,0},{4,5},{5,6},{6,7},{7,4},{8,9},{9,10},{10,1... | collective-permute-start | bytes 2752520 | tf_op jit(solution)/shard_map/ppermute | solution.py:161
  140.9 33.0 %collective-permute-start.22 = (bf16[448,1024]{1,0:T(8,128)(2,1)}, bf16[448,1024]{1,0:T(8,128)(2,1)}, u32[]{:S(2)}, u32[]{:S(2)}) collective-permute-start(bf16[448,1024]{1,0:T(8,128)(2,1)} %param.22), channel_id=1, source_target_pairs={{0,3},{1,0},{2,1},{3,2},{4,7},{5,4},{6,5},{7,6},{8,11},{9,8},{10,9... | collective-permute-start | bytes 2752520 | tf_op jit(solution)/shard_map/ppermute | solution.py:162
  167.7 16.4 %collective-permute-start.21 = (bf16[224,1024]{1,0:T(8,128)(2,1)}, bf16[224,1024]{1,0:T(8,128)(2,1)S(1)}, u32[]{:S(2)}, u32[]{:S(2)}) collective-permute-start(bf16[224,1024]{1,0:T(8,128)(2,1)} %slice.233), channel_id=1, source_target_pairs={{0,1},{1,2},{2,3},{3,0},{4,5},{5,6},{6,7},{7,4},{8,9},{9,10},{10,1... | collective-permute-start | bytes 1376264 | tf_op jit(solution)/shard_map/ppermute | solution.py:165
  169.8 7.4 %collective-permute-start.10 = (bf16[32,2048]{1,0:T(8,128)(2,1)S(1)}, bf16[32,2048]{1,0:T(8,128)(2,1)S(1)}, u32[]{:S(2)}, u32[]{:S(2)}) collective-permute-start(bf16[32,2048]{1,0:T(8,128)(2,1)S(1)} %get-tuple-element.57), channel_id=1, source_target_pairs={{0,32},{32,64},{64,96},{96,0},{1,33},{33,65},{65,97},{97,1},{2,34}... | collective-permute-start | bytes 393224 | tf_op jit(solution)/shard_map/ppermute | solution.py:22
  171.2 9.2 %collective-permute-start.11 = (bf16[32,2048]{1,0:T(8,128)(2,1)S(1)}, bf16[32,2048]{1,0:T(8,128)(2,1)S(1)}, u32[]{:S(2)}, u32[]{:S(2)}) collective-permute-start(bf16[32,2048]{1,0:T(8,128)(2,1)S(1)} %get-tuple-element.57), channel_id=1, source_target_pairs={{0,64},{32,96},{64,0},{96,32},{1,65},{33,97},{65,1},{97,33},{2,66}... | collective-permute-start | bytes 393224 | tf_op jit(solution)/shard_map/ppermute | solution.py:22
  173.9 8.1 %collective-permute-start.12 = (bf16[32,2048]{1,0:T(8,128)(2,1)S(1)}, bf16[32,2048]{1,0:T(8,128)(2,1)S(1)}, u32[]{:S(2)}, u32[]{:S(2)}) collective-permute-start(bf16[32,2048]{1,0:T(8,128)(2,1)S(1)} %get-tuple-element.57), channel_id=1, source_target_pairs={{0,96},{32,0},{64,32},{96,64},{1,97},{33,1},{65,33},{97,65},{2,98}... | collective-permute-start | bytes 393224 | tf_op jit(solution)/shard_map/ppermute | solution.py:22
  177.2 12.3 %collective-permute-start.23 = (bf16[224,1024]{1,0:T(8,128)(2,1)}, bf16[224,1024]{1,0:T(8,128)(2,1)}, u32[]{:S(2)}, u32[]{:S(2)}) collective-permute-start(bf16[224,1024]{1,0:T(8,128)(2,1)} %slice.234), channel_id=1, source_target_pairs={{0,3},{1,0},{2,1},{3,2},{4,7},{5,4},{6,5},{7,6},{8,11},{9,8},{10,9... | collective-permute-start | bytes 1376264 | tf_op jit(solution)/shard_map/ppermute | solution.py:170
  180.4 12.6 %collective-permute-start.4 = (bf16[32,2048]{1,0:T(8,128)(2,1)}, bf16[32,2048]{1,0:T(8,128)(2,1)S(1)}, u32[]{:S(2)}, u32[]{:S(2)}) collective-permute-start(bf16[32,2048]{1,0:T(8,128)(2,1)} %get-tuple-element.58), channel_id=1, source_target_pairs={{0,8},{8,16},{16,24},{24,0},{1,9},{9,17},{17,25},{25,1},{2,10},{10... | collective-permute-start | bytes 393224 | tf_op jit(solution)/shard_map/ppermute | solution.py:22
  182.1 32.5 %collective-permute-start.13 = (bf16[4,32,2048]{2,1,0:T(8,128)(2,1)S(1)}, bf16[4,32,2048]{2,1,0:T(8,128)(2,1)S(1)}, u32[]{:S(2)}, u32[]{:S(2)}) collective-permute-start(bf16[4,32,2048]{2,1,0:T(8,128)(2,1)S(1)} %get-tuple-element.52), channel_id=1, source_target_pairs={{0,8},{8,16},{16,24},{24,0},{1,9},{9,17},{17,25},{25,1},{2,10},{10... | collective-permute-start | bytes 1572872 | tf_op jit(solution)/shard_map/ppermute | solution.py:22
  184.1 8.9 %copy-start.5 = (bf16[224,1024]{1,0:T(8,128)(2,1)}, bf16[224,1024]{1,0:T(8,128)(2,1)S(1)}, u32[]{:S(2)}) copy-start(bf16[224,1024]{1,0:T(8,128)(2,1)S(1)} %collective-permute-done.21) | copy-start | bytes 1376260
  184.1 32.6 %collective-permute-start.14 = (bf16[4,32,2048]{2,1,0:T(8,128)(2,1)S(1)}, bf16[4,32,2048]{2,1,0:T(8,128)(2,1)S(1)}, u32[]{:S(2)}, u32[]{:S(2)}) collective-permute-start(bf16[4,32,2048]{2,1,0:T(8,128)(2,1)S(1)} %get-tuple-element.52), channel_id=1, source_target_pairs={{0,16},{8,24},{16,0},{24,8},{1,17},{9,25},{17,1},{25,9},{2,18},{10... | collective-permute-start | bytes 1572872 | tf_op jit(solution)/shard_map/ppermute | solution.py:22
  189.5 23.6 %collective-permute-start.5 = (bf16[32,2048]{1,0:T(8,128)(2,1)}, bf16[32,2048]{1,0:T(8,128)(2,1)S(1)}, u32[]{:S(2)}, u32[]{:S(2)}) collective-permute-start(bf16[32,2048]{1,0:T(8,128)(2,1)} %get-tuple-element.58), channel_id=1, source_target_pairs={{0,16},{8,24},{16,0},{24,8},{1,17},{9,25},{17,1},{25,9},{2,18},{10... | collective-permute-start | bytes 393224 | tf_op jit(solution)/shard_map/ppermute | solution.py:22
  193.0 0.6 copy-start.6
  193.7 19.4 %collective-permute-start.6 = (bf16[32,2048]{1,0:T(8,128)(2,1)}, bf16[32,2048]{1,0:T(8,128)(2,1)S(1)}, u32[]{:S(2)}, u32[]{:S(2)}) collective-permute-start(bf16[32,2048]{1,0:T(8,128)(2,1)} %get-tuple-element.58), channel_id=1, source_target_pairs={{0,24},{8,0},{16,8},{24,16},{1,25},{9,1},{17,9},{25,17},{2,26},{10... | collective-permute-start | bytes 393224 | tf_op jit(solution)/shard_map/ppermute | solution.py:22
  213.1 11.6 %collective-permute-start.15 = (bf16[4,32,2048]{2,1,0:T(8,128)(2,1)S(1)}, bf16[4,32,2048]{2,1,0:T(8,128)(2,1)S(1)}, u32[]{:S(2)}, u32[]{:S(2)}) collective-permute-start(bf16[4,32,2048]{2,1,0:T(8,128)(2,1)S(1)} %get-tuple-element.52), channel_id=1, source_target_pairs={{0,24},{8,0},{16,8},{24,16},{1,25},{9,1},{17,9},{25,17},{2,26},{10... | collective-permute-start | bytes 1572872 | tf_op jit(solution)/shard_map/ppermute | solution.py:22
  214.1 24.2 %collective-permute-start.7 = (bf16[4,32,2048]{2,1,0:T(8,128)(2,1)S(1)}, bf16[4,32,2048]{2,1,0:T(8,128)(2,1)S(1)}, u32[]{:S(2)}, u32[]{:S(2)}) collective-permute-start(bf16[4,32,2048]{2,1,0:T(8,128)(2,1)S(1)} %get-tuple-element.54), channel_id=1, source_target_pairs={{0,32},{32,64},{64,96},{96,0},{1,33},{33,65},{65,97},{97,1},{2,34}... | collective-permute-start | bytes 1572872 | tf_op jit(solution)/shard_map/ppermute | solution.py:22
  214.6 23.6 %collective-permute-start.8 = (bf16[4,32,2048]{2,1,0:T(8,128)(2,1)S(1)}, bf16[4,32,2048]{2,1,0:T(8,128)(2,1)S(1)}, u32[]{:S(2)}, u32[]{:S(2)}) collective-permute-start(bf16[4,32,2048]{2,1,0:T(8,128)(2,1)S(1)} %get-tuple-element.54), channel_id=1, source_target_pairs={{0,64},{32,96},{64,0},{96,32},{1,65},{33,97},{65,1},{97,33},{2,66}... | collective-permute-start | bytes 1572872 | tf_op jit(solution)/shard_map/ppermute | solution.py:22
  216.7 22.2 %collective-permute-start.9 = (bf16[4,32,2048]{2,1,0:T(8,128)(2,1)S(1)}, bf16[4,32,2048]{2,1,0:T(8,128)(2,1)S(1)}, u32[]{:S(2)}, u32[]{:S(2)}) collective-permute-start(bf16[4,32,2048]{2,1,0:T(8,128)(2,1)S(1)} %get-tuple-element.54), channel_id=1, source_target_pairs={{0,96},{32,0},{64,32},{96,64},{1,97},{33,1},{65,33},{97,65},{2,98}... | collective-permute-start | bytes 1572872 | tf_op jit(solution)/shard_map/ppermute | solution.py:22
  224.8 34.5 %collective-permute-start.25 = (bf16[448,4096]{1,0:T(8,128)(2,1)S(1)}, bf16[448,4096]{1,0:T(8,128)(2,1)S(1)}, u32[]{:S(2)}, u32[]{:S(2)}) collective-permute-start(bf16[448,4096]{1,0:T(8,128)(2,1)S(1)} %bitcast.223), channel_id=1, source_target_pairs={{0,4},{4,0},{1,5},{5,1},{2,6},{6,2},{3,7},{7,3},{8,12},{12,8},{9,1... | collective-permute-start | bytes 11010056 | tf_op jit(solution)/shard_map/ppermute | solution.py:59
  261.9 24.9 %collective-permute-start.26 = (bf16[4,32,2048]{2,1,0:T(8,128)(2,1)S(1)}, bf16[4,32,2048]{2,1,0:T(8,128)(2,1)S(1)}, u32[]{:S(2)}, u32[]{:S(2)}) collective-permute-start(bf16[4,32,2048]{2,1,0:T(8,128)(2,1)S(1)} %get-tuple-element.27), channel_id=1, source_target_pairs={{0,96},{32,0},{64,32},{96,64},{1,97},{33,1},{65,33},{97,65},{2,98}... | collective-permute-start | bytes 1572872 | tf_op jit(solution)/shard_map/ppermute | solution.py:22
  264.4 24.2 %collective-permute-start.27 = (bf16[4,32,2048]{2,1,0:T(8,128)(2,1)S(1)}, bf16[4,32,2048]{2,1,0:T(8,128)(2,1)S(1)}, u32[]{:S(2)}, u32[]{:S(2)}) collective-permute-start(bf16[4,32,2048]{2,1,0:T(8,128)(2,1)S(1)} %get-tuple-element.29), channel_id=1, source_target_pairs={{0,64},{32,96},{64,0},{96,32},{1,65},{33,97},{65,1},{97,33},{2,66}... | collective-permute-start | bytes 1572872 | tf_op jit(solution)/shard_map/ppermute | solution.py:22
  264.4 26.0 %collective-permute-start.28 = (bf16[4,32,2048]{2,1,0:T(8,128)(2,1)S(1)}, bf16[4,32,2048]{2,1,0:T(8,128)(2,1)S(1)}, u32[]{:S(2)}, u32[]{:S(2)}) collective-permute-start(bf16[4,32,2048]{2,1,0:T(8,128)(2,1)S(1)} %get-tuple-element.28), channel_id=1, source_target_pairs={{0,32},{32,64},{64,96},{96,0},{1,33},{33,65},{65,97},{97,1},{2,34}... | collective-permute-start | bytes 1572872 | tf_op jit(solution)/shard_map/ppermute | solution.py:22
  265.8 28.9 %collective-permute-start.32 = (bf16[4,32,2048]{2,1,0:T(8,128)(2,1)S(1)}, bf16[4,32,2048]{2,1,0:T(8,128)(2,1)S(1)}, u32[]{:S(2)}, u32[]{:S(2)}) collective-permute-start(bf16[4,32,2048]{2,1,0:T(8,128)(2,1)S(1)} %get-tuple-element.34), channel_id=1, source_target_pairs={{0,24},{8,0},{16,8},{24,16},{1,25},{9,1},{17,9},{25,17},{2,26},{10... | collective-permute-start | bytes 1572872 | tf_op jit(solution)/shard_map/ppermute | solution.py:22
  266.4 28.2 %collective-permute-start.33 = (bf16[4,32,2048]{2,1,0:T(8,128)(2,1)S(1)}, bf16[4,32,2048]{2,1,0:T(8,128)(2,1)S(1)}, u32[]{:S(2)}, u32[]{:S(2)}) collective-permute-start(bf16[4,32,2048]{2,1,0:T(8,128)(2,1)S(1)} %get-tuple-element.36), channel_id=1, source_target_pairs={{0,16},{8,24},{16,0},{24,8},{1,17},{9,25},{17,1},{25,9},{2,18},{10... | collective-permute-start | bytes 1572872 | tf_op jit(solution)/shard_map/ppermute | solution.py:22
  286.8 18.1 %collective-permute-start.34 = (bf16[4,32,2048]{2,1,0:T(8,128)(2,1)S(1)}, bf16[4,32,2048]{2,1,0:T(8,128)(2,1)S(1)}, u32[]{:S(2)}, u32[]{:S(2)}) collective-permute-start(bf16[4,32,2048]{2,1,0:T(8,128)(2,1)S(1)} %get-tuple-element.35), channel_id=1, source_target_pairs={{0,8},{8,16},{16,24},{24,0},{1,9},{9,17},{17,25},{25,1},{2,10},{10... | collective-permute-start | bytes 1572872 | tf_op jit(solution)/shard_map/ppermute | solution.py:22
  290.8 18.4 %collective-permute-start.29 = (bf16[32,2048]{1,0:T(8,128)(2,1)S(1)}, bf16[32,2048]{1,0:T(8,128)(2,1)S(1)}, u32[]{:S(2)}, u32[]{:S(2)}) collective-permute-start(bf16[32,2048]{1,0:T(8,128)(2,1)S(1)} %get-tuple-element.45), channel_id=1, source_target_pairs={{0,24},{8,0},{16,8},{24,16},{1,25},{9,1},{17,9},{25,17},{2,26},{10... | collective-permute-start | bytes 393224 | tf_op jit(solution)/shard_map/ppermute | solution.py:22
  291.4 18.7 %collective-permute-start.30 = (bf16[32,2048]{1,0:T(8,128)(2,1)S(1)}, bf16[32,2048]{1,0:T(8,128)(2,1)S(1)}, u32[]{:S(2)}, u32[]{:S(2)}) collective-permute-start(bf16[32,2048]{1,0:T(8,128)(2,1)S(1)} %get-tuple-element.47), channel_id=1, source_target_pairs={{0,16},{8,24},{16,0},{24,8},{1,17},{9,25},{17,1},{25,9},{2,18},{10... | collective-permute-start | bytes 393224 | tf_op jit(solution)/shard_map/ppermute | solution.py:22
  294.7 15.5 %collective-permute-start.31 = (bf16[32,2048]{1,0:T(8,128)(2,1)S(1)}, bf16[32,2048]{1,0:T(8,128)(2,1)S(1)}, u32[]{:S(2)}, u32[]{:S(2)}) collective-permute-start(bf16[32,2048]{1,0:T(8,128)(2,1)S(1)} %get-tuple-element.46), channel_id=1, source_target_pairs={{0,8},{8,16},{16,24},{24,0},{1,9},{9,17},{17,25},{25,1},{2,10},{10... | collective-permute-start | bytes 393224 | tf_op jit(solution)/shard_map/ppermute | solution.py:22
  305.3 7.8 %collective-permute-start.35 = (bf16[32,2048]{1,0:T(8,128)(2,1)S(1)}, bf16[32,2048]{1,0:T(8,128)(2,1)S(1)}, u32[]{:S(2)}, u32[]{:S(2)}) collective-permute-start(bf16[32,2048]{1,0:T(8,128)(2,1)S(1)} %get-tuple-element.48), channel_id=1, source_target_pairs={{0,96},{32,0},{64,32},{96,64},{1,97},{33,1},{65,33},{97,65},{2,98}... | collective-permute-start | bytes 393224 | tf_op jit(solution)/shard_map/ppermute | solution.py:22
  309.2 6.6 %collective-permute-start.36 = (bf16[32,2048]{1,0:T(8,128)(2,1)S(1)}, bf16[32,2048]{1,0:T(8,128)(2,1)S(1)}, u32[]{:S(2)}, u32[]{:S(2)}) collective-permute-start(bf16[32,2048]{1,0:T(8,128)(2,1)S(1)} %get-tuple-element.50), channel_id=1, source_target_pairs={{0,64},{32,96},{64,0},{96,32},{1,65},{33,97},{65,1},{97,33},{2,66}... | collective-permute-start | bytes 393224 | tf_op jit(solution)/shard_map/ppermute | solution.py:22
  309.2 7.6 %collective-permute-start.37 = (bf16[32,2048]{1,0:T(8,128)(2,1)S(1)}, bf16[32,2048]{1,0:T(8,128)(2,1)S(1)}, u32[]{:S(2)}, u32[]{:S(2)}) collective-permute-start(bf16[32,2048]{1,0:T(8,128)(2,1)S(1)} %get-tuple-element.49), channel_id=1, source_target_pairs={{0,32},{32,64},{64,96},{96,0},{1,33},{33,65},{65,97},{97,1},{2,34}... | collective-permute-start | bytes 393224 | tf_op jit(solution)/shard_map/ppermute | solution.py:22
  316.8 13.5 %copy-start.1 = (bf16[4096,128]{1,0:T(8,128)(2,1)S(1)}, bf16[4096,128]{1,0:T(8,128)(2,1)}, u32[]{:S(2)}) copy-start(bf16[4096,128]{1,0:T(8,128)(2,1)} %param.16) | copy-start | bytes 3145732
  318.4 11.2 %all-to-all-start = ((bf16[32,4,1024]{2,0,1:T(8,128)(2,1)}), bf16[32,4,1024]{2,0,1:T(8,128)(2,1)S(1)}, u32[]{:S(2)}, u32[]{:S(2)}) async-start(bf16[32,4,1024]{2,0,1:T(8,128)(2,1)} %bitcast.215), calls=%async_computation.1 | async-start | bytes 524288 | tf_op jit(solution)/shard_map/all_to_all | solution.py:295
Sparse Core Ops, SparseCore 0:
  92.8 43.0 reduce-scatter.1

commit v6 on v5

--- a/solution.py
+++ b/solution.py
@@ -255,8 +255,12 @@
     )
 
     head_terms = jnp.dot(attended, w_out, preferred_element_type=jnp.float32)
-    head_rows = lax.psum_scatter(head_terms, "mlp", scatter_dimension=0, tiled=True)
     rows_here = slots_here // n_mlp
+    head_rows = lax.dynamic_slice_in_dim(head_terms, mlp_index * rows_here, rows_here, 0)
+    for shift in range(1, n_mlp):
+        target = (mlp_index + shift) % n_mlp
+        outgoing = lax.dynamic_slice_in_dim(head_terms, target * rows_here, rows_here, 0)
+        head_rows = head_rows + shifted(outgoing, "mlp", n_mlp, shift)
     row_start = mlp_index * rows_here
     hidden_rows = lax.dynamic_slice_in_dim(hidden_f, row_start, rows_here, 0)
     live_rows = lax.dynamic_slice_in_dim(live, row_start, rows_here, 0)

time: 343 us -> 333 us (0.971)
  between operations: 15.7 us -> 2.32 us
  other arithmetic: 41.7 us -> 46.9 us
  waiting for transfers between devices: 151 us -> 146 us
    ppermute x2, waiting for transfers between devices: 20.4 us -> 0.01 us  [layer(): lax.ppermute(own, 'mlp', [(i, (i + 1) % n_mlp) for i in range(n_mlp)])]
    ppermute x24 -> x27, waiting for transfers between devices: 71.5 us -> 91.9 us  [shifted(): lax.ppermute(value, axis, [(i, (i + shift) % size) for i in range(size)])]
    ppermute x2, waiting for transfers between devices: 31.5 us -> 19.1 us  [layer(): lax.ppermute((from_left[0][:half_gu], from_left[1][:half_wd]), 'mlp', [(i...]
    ppermute x2, waiting for transfers between devices: 0.01 us -> 11.8 us  [layer(): lax.ppermute(own, 'mlp', [(i, (i - 1) % n_mlp) for i in range(n_mlp)])]
    ppermute x24 -> x27, starting transfers between devices: 36.8 us -> 43.8 us  [shifted(): lax.ppermute(value, axis, [(i, (i + shift) % size) for i in range(size)])]
    ppermute x2, starting transfers between devices: 5.71 us -> 1.57 us  [layer(): lax.ppermute(own, 'mlp', [(i, (i - 1) % n_mlp) for i in range(n_mlp)])]
    unnamed x47 -> x51, local copies, waits for them, and re-layouts: 9.5 us -> 9.78 us
  transfers between devices with their start and end apart: 40 -> 42, of which waited for: 18 -> 19; matrix products, arithmetic and copies ran while one was open for 30% -> 32% of each run, Pallas kernels for 0% -> 0%
where the time goes in v6:
time: 333 us; the launch traced here: 327 us
  waiting for transfers between devices  146 us (44%)
  starting transfers between devices  61.9 us (19%)
  other arithmetic  46.9 us (14%)
  matrix products  43.3 us (13%)
  local copies, waits for them, and re-layouts  25.9 us (8%)
    ppermute x27, waiting for transfers between devices, shifted(): lax.ppermute(value, axis, [(i, (i + shift) % size) for i in range(size)])  91.9 us
    ppermute x27, starting transfers between devices, shifted(): lax.ppermute(value, axis, [(i, (i + shift) % size) for i in range(size)])  43.8 us
    ppermute x2, waiting for transfers between devices, layer(): lax.ppermute((from_left[0][:half_gu], from_left[1][:half_wd]), 'mlp', [(i...  19.1 us
    dot_general x2, matrix products, layer(): jnp.dot(tokens_ring, weights_here, preferred_element_type=jnp.float32)  15.2 us
    ppermute x6, waiting for transfers between devices, swap_with_partner(): lax.ppermute(value, axis, [(source, source ^ 1) for source in range(size)])  12.4 us
    ppermute x2, waiting for transfers between devices, layer(): lax.ppermute(own, 'mlp', [(i, (i - 1) % n_mlp) for i in range(n_mlp)])  11.8 us
    convert_element_type x1, other arithmetic, partial_attention(): weights.astype(jnp.bfloat16)  10.3 us
    unnamed x51, local copies, waits for them, and re-layouts  9.78 us
  transfers between devices with their start and end apart: 42, of which 19 were waited for; matrix products, arithmetic and copies ran while one was open for 32% of the time, Pallas kernels for 0%

profile of v6, /device:TPU:0, one launch (start us, length us, event | category | flops | bytes accessed | tf_op | source)
XLA Modules:
  0.0 326.9 jit_solution(969821785391801489)
XLA Ops:
  0.7 1.5 copy.96
  2.2 1.5 copy.97
  3.7 1.8 pad_maximum_fusion.3
  5.5 1.7 collective-permute-start.19
  7.2 1.5 collective-permute-start.21
  9.2 1.5 multiply_reduce_fusion
  11.2 4.0 %fusion.91 = f32[128,512]{1,0:T(8,128)} fusion(bf16[4096,512]{1,0:T(8,128)(2,1)} %param.15, f32[4096]{0:T(1024)S(1)} %convert_element_type.197, f32[128]{0:T(128)S(1)} %add_rsqrt_fusion.1, bf16[128,4096]{1,0:T(8,128)(2,1)} %param.13), kind=kOutput, calls=%fused_computation.216 | convolution fusion | flops 538968064 | bytes 5521920 | tf_op jit(solution)/shard_map/dot_general | solution.py:191
  20.3 4.1 %fusion.94 = (bf16[2048,1,128]{2,1,0:T(2,128)(2,1)}, bf16[2048,1,128]{2,1,0:T(2,128)(2,1)S(1)}) fusion(bf16[2048,2,128]{2,1,0:T(2,128)(2,1)} %param.23), kind=kLoop, calls=%fused_computation.217 | loop fusion | bytes 2097152 | tf_op jit(solution)/shard_map/slice | solution.py:217
  24.5 5.6 %fusion.46 = (bf16[2048,64]{1,0:T(8,128)(2,1)}, bf16[2048,64]{1,0:T(8,128)(2,1)}) fusion(f32[2048,1,128]{2,0,1:T(8,128)S(1)} %copy_convert_fusion, f32[64]{0:T(128)S(1)} %copy-done.12, f32[2048]{0:T(1024)S(1)} %add_convert_fusion.3), kind=kLoop, calls=%fused_computation.103 | loop fusion | flops 1179648 | bytes 1581312 | tf_op jit(solution)/shard_map/concatenate | solution.py:70
  30.9 2.4 collective-permute-start.1
  33.3 1.8 convolution_bitcast_fusion.1
  35.2 3.6 %copy.112 = bf16[2048,1,128]{0,2,1:T(8,128)(2,1)} copy(bf16[2048,1,128]{2,1,0:T(2,128)(2,1)} %get-tuple-element.42) | data formatting | bytes 1048576
  39.0 1.3 collective-permute-done.1
  40.3 1.3 maximum_select_fusion
  41.7 9.2 %bitcast_reduce_fusion = (f32[4,512]{1,0:T(4,128)S(1)}, f32[2048,512,4]{0,1,2:T(8,128)}) fusion(bf16[512,4,128]{2,0,1:T(8,128)(2,1)S(1)} %bitcast.225, bf16[2048,64]{1,0:T(8,128)(2,1)} %get-tuple-element.41, bf16[2048,64]{1,0:T(8,128)(2,1)S(1)} %copy-done.5), kind=kOutput, calls=%fused_computation.2 | convolution fusion | flops 1083176960 | bytes 17833984 | tf_op jit(solution)/shard_map/qkgd,nkd->kgqn/dot_general | solution.py:97
  51.0 10.3 %fusion.2 = (bf16[1,4,512,2048]{3,2,1,0:T(8,128)(2,1)}, f32[4,512]{1,0:T(4,128)S(1)}) fusion(f32[2048,512,4]{0,1,2:T(8,128)} %get-tuple-element.69, f32[4,512]{1,0:T(4,128)S(1)} %get-tuple-element.68), kind=kLoop, calls=%fused_computation.5 | loop fusion | flops 16775168 | bytes 25182208 | tf_op jit(solution)/shard_map/convert_element_type | solution.py:107
  61.3 6.3 %convolution_bitcast_fusion = f32[1,4,4,128,128]{3,4,2,1,0:T(8,128)S(1)} fusion(bf16[4,4,128,2048]{3,2,1,0:T(8,128)(2,1)} %bitcast.217, bf16[2048,1,128]{0,2,1:T(8,128)(2,1)} %copy.112), kind=kOutput, calls=%fused_computation.33 | convolution fusion | flops 1073741824 | bytes 9961472 | tf_op jit(solution)/shard_map/kgqn,nkd->kgqd/dot_general | solution.py:105
  69.8 1.7 collective-permute-start.2
  72.7 11.0 %collective-permute-done.2 = f32[1,4,2,128,130]{3,1,4,2,0:T(4,128)} collective-permute-done((f32[1,4,2,128,130]{3,1,4,2,0:T(4,128)}, f32[1,4,2,128,130]{3,1,4,2,0:T(4,128)}, u32[]{:S(2)}, u32[]{:S(2)}) %collective-permute-start.2) | collective-permute-done | bytes 532512 | tf_op jit(solution)/shard_map/ppermute | solution.py:59
  89.6 1.6 collective-permute-start.20
  92.5 1.7 collective-permute-start.22
  94.6 19.0 %collective-permute-done.20 = bf16[512,896]{1,0:T(8,128)(2,1)S(1)} collective-permute-done((bf16[512,896]{1,0:T(8,128)(2,1)S(1)}, bf16[512,896]{1,0:T(8,128)(2,1)S(1)}, u32[]{:S(2)}, u32[]{:S(2)}) %collective-permute-start.20) | collective-permute-done | bytes 917536 | tf_op jit(solution)/shard_map/ppermute | solution.py:165
  113.6 1.4 collective-permute-done.22
  115.2 6.2 %pad_maximum_fusion = bf16[4,1024,896]{2,1,0:T(8,128)(2,1)} fusion(bf16[1,1024,896]{2,1,0:T(8,128)(2,1)} %bitcast.69, bf16[1,1024,896]{2,1,0:T(8,128)(2,1)S(1)} %maximum_bitcast_fusion.2, bf16[1,1024,896]{2,1,0:T(8,128)(2,1)} %bitcast.67, bf16[1,1024,896]{2,1,0:T(8,128)(2,1)S(1)} %fusion.110), kind=kLoop, calls=%fused_computation.7 | loop fusion | flops 11010048 | bytes 14680064 | tf_op jit(solution)/shard_map/stack | solution.py:179
  123.3 1.4 collective-permute-start.4
  124.8 3.1 collective-permute-start.5
  129.0 1.5 convert_element_type.194
  131.7 7.6 %collective-permute-done.4 = f32[32,4096]{1,0:T(8,128)} collective-permute-done((f32[32,4096]{1,0:T(8,128)}, f32[32,4096]{1,0:T(8,128)}, u32[]{:S(2)}, u32[]{:S(2)}) %collective-permute-start.4) | collective-permute-done | bytes 524320 | tf_op jit(solution)/shard_map/ppermute | solution.py:22
  139.9 12.3 %collective-permute-done.5 = f32[32,4096]{1,0:T(8,128)} collective-permute-done((f32[32,4096]{1,0:T(8,128)}, f32[32,4096]{1,0:T(8,128)}, u32[]{:S(2)}, u32[]{:S(2)}) %collective-permute-start.5) | collective-permute-done | bytes 524320 | tf_op jit(solution)/shard_map/ppermute | solution.py:22
  152.2 1.7 fusion.31
  154.8 1.4 collective-permute-start.13
  156.3 2.7 collective-permute-start.14
  159.0 11.8 %collective-permute-done.25 = bf16[448,1024]{1,0:T(8,128)(2,1)S(1)} collective-permute-done((bf16[448,1024]{1,0:T(8,128)(2,1)}, bf16[448,1024]{1,0:T(8,128)(2,1)S(1)}, u32[]{:S(2)}, u32[]{:S(2)}) %collective-permute-start.25) | collective-permute-done | bytes 917536 | tf_op jit(solution)/shard_map/ppermute | solution.py:162
  170.8 2.7 collective-permute-start.15
  173.6 2.7 collective-permute-start.26
  176.3 1.6 collective-permute-start.7
  177.9 2.0 collective-permute-start.16
  179.9 1.8 collective-permute-start.17
  181.9 4.1 %collective-permute-done.26 = bf16[224,1024]{1,0:T(8,128)(2,1)S(1)} collective-permute-done((bf16[224,1024]{1,0:T(8,128)(2,1)S(1)}, bf16[224,1024]{1,0:T(8,128)(2,1)S(1)}, u32[]{:S(2)}, u32[]{:S(2)}) %collective-permute-start.26) | collective-permute-done | bytes 458784 | tf_op jit(solution)/shard_map/ppermute | solution.py:170
  186.0 3.5 %collective-permute-start.8 = (bf16[32,2048]{1,0:T(8,128)(2,1)}, bf16[32,2048]{1,0:T(8,128)(2,1)S(1)}, u32[]{:S(2)}, u32[]{:S(2)}) collective-permute-start(bf16[32,2048]{1,0:T(8,128)(2,1)} %get-tuple-element.61), channel_id=1, source_target_pairs={{0,16},{8,24},{16,0},{24,8},{1,17},{9,25},{17,1},{25,9},{2,18},{10... | collective-permute-start | bytes 393224 | tf_op jit(solution)/shard_map/ppermute | solution.py:22
  190.4 1.3 maximum_bitcast_fusion.3
  191.7 18.0 %collective-permute-done.8 = bf16[32,2048]{1,0:T(8,128)(2,1)S(1)} collective-permute-done((bf16[32,2048]{1,0:T(8,128)(2,1)}, bf16[32,2048]{1,0:T(8,128)(2,1)S(1)}, u32[]{:S(2)}, u32[]{:S(2)}) %collective-permute-start.8) | collective-permute-done | bytes 131104 | tf_op jit(solution)/shard_map/ppermute | solution.py:22
  210.8 2.3 collective-permute-start.11
  214.2 1.7 maximum_bitcast_fusion
  216.3 6.0 %collective-permute-done.18 = bf16[4,32,2048]{2,1,0:T(8,128)(2,1)S(1)} collective-permute-done((bf16[4,32,2048]{2,1,0:T(8,128)(2,1)S(1)}, bf16[4,32,2048]{2,1,0:T(8,128)(2,1)S(1)}, u32[]{:S(2)}, u32[]{:S(2)}) %collective-permute-start.18) | collective-permute-done | bytes 524320 | tf_op jit(solution)/shard_map/ppermute | solution.py:22
  222.5 1.5 maximum_bitcast_fusion.1
  224.2 11.6 %collective-permute-done.10 = bf16[4,32,2048]{2,1,0:T(8,128)(2,1)S(1)} collective-permute-done((bf16[4,32,2048]{2,1,0:T(8,128)(2,1)S(1)}, bf16[4,32,2048]{2,1,0:T(8,128)(2,1)S(1)}, u32[]{:S(2)}, u32[]{:S(2)}) %collective-permute-start.10) | collective-permute-done | bytes 524320 | tf_op jit(solution)/shard_map/ppermute | solution.py:22
  236.7 2.5 fusion.18
  239.2 7.6 %fusion.30 = f32[512,896]{1,0:T(8,128)S(1)} fusion(bf16[4096,896]{1,0:T(8,128)(2,1)} %bitcast.70, bf16[512,1024]{1,0:T(8,128)(2,1)S(1)} %get-tuple-element.33, bf16[512,1024]{1,0:T(8,128)(2,1)S(1)} %get-tuple-element.32, bf16[512,1024]{1,0:T(8,128)(2,1)S(1)} %get-tuple-element.31, bf16[512,1024]{1,0:T(8,128)(2,1)S(1)} %get-tuple-element.30), kind=kOutput, calls=%fused_computation.70 | convolution fusion | flops 3774873600 | bytes 13369344 | tf_op jit(solution)/shard_map/dot_general | solution.py:282
  246.8 2.4 convolution_convert_fusion.1
  249.2 7.6 %fusion.29 = f32[512,896]{1,0:T(8,128)S(1)} fusion(bf16[4096,896]{1,0:T(8,128)(2,1)} %bitcast.75, bf16[512,1024]{1,0:T(8,128)(2,1)S(1)} %get-tuple-element.33, bf16[512,1024]{1,0:T(8,128)(2,1)S(1)} %get-tuple-element.32, bf16[512,1024]{1,0:T(8,128)(2,1)S(1)} %get-tuple-element.31, bf16[512,1024]{1,0:T(8,128)(2,1)S(1)} %get-tuple-element.30), kind=kOutput, calls=%fused_computation.69 | convolution fusion | flops 3774873600 | bytes 13369344 | tf_op jit(solution)/shard_map/dot_general | solution.py:282
  256.8 2.5 add_convert_fusion
  259.4 2.5 collective-permute-start.29
  263.9 3.3 %collective-permute-start.36 = (bf16[4,32,2048]{2,1,0:T(8,128)(2,1)S(1)}, bf16[4,32,2048]{2,1,0:T(8,128)(2,1)S(1)}, u32[]{:S(2)}, u32[]{:S(2)}) collective-permute-start(bf16[4,32,2048]{2,1,0:T(8,128)(2,1)S(1)} %get-tuple-element.36), channel_id=1, source_target_pairs={{0,16},{8,24},{16,0},{24,8},{1,17},{9,25},{17,1},{25,9},{2,18},{10... | collective-permute-start | bytes 1572872 | tf_op jit(solution)/shard_map/ppermute | solution.py:22
  267.2 17.1 %collective-permute-done.29 = bf16[4,32,2048]{2,1,0:T(8,128)(2,1)S(1)} collective-permute-done((bf16[4,32,2048]{2,1,0:T(8,128)(2,1)S(1)}, bf16[4,32,2048]{2,1,0:T(8,128)(2,1)S(1)}, u32[]{:S(2)}, u32[]{:S(2)}) %collective-permute-start.29) | collective-permute-done | bytes 524320 | tf_op jit(solution)/shard_map/ppermute | solution.py:22
  284.3 1.7 collective-permute-start.37
  286.0 1.9 collective-permute-done.31
  288.9 3.3 %collective-permute-start.33 = (bf16[32,2048]{1,0:T(8,128)(2,1)S(1)}, bf16[32,2048]{1,0:T(8,128)(2,1)S(1)}, u32[]{:S(2)}, u32[]{:S(2)}) collective-permute-start(bf16[32,2048]{1,0:T(8,128)(2,1)S(1)} %get-tuple-element.50), channel_id=1, source_target_pairs={{0,16},{8,24},{16,0},{24,8},{1,17},{9,25},{17,1},{25,9},{2,18},{10... | collective-permute-start | bytes 393224 | tf_op jit(solution)/shard_map/ppermute | solution.py:22
  292.2 10.1 %collective-permute-done.37 = bf16[4,32,2048]{2,1,0:T(8,128)(2,1)S(1)} collective-permute-done((bf16[4,32,2048]{2,1,0:T(8,128)(2,1)S(1)}, bf16[4,32,2048]{2,1,0:T(8,128)(2,1)S(1)}, u32[]{:S(2)}, u32[]{:S(2)}) %collective-permute-start.37) | collective-permute-done | bytes 524320 | tf_op jit(solution)/shard_map/ppermute | solution.py:22
  302.7 3.9 %collective-permute-start.38 = (bf16[32,2048]{1,0:T(8,128)(2,1)S(1)}, bf16[32,2048]{1,0:T(8,128)(2,1)S(1)}, u32[]{:S(2)}, u32[]{:S(2)}) collective-permute-start(bf16[32,2048]{1,0:T(8,128)(2,1)S(1)} %get-tuple-element.51), channel_id=1, source_target_pairs={{0,96},{32,0},{64,32},{96,64},{1,97},{33,1},{65,33},{97,65},{2,98}... | collective-permute-start | bytes 393224 | tf_op jit(solution)/shard_map/ppermute | solution.py:22
  307.6 2.9 collective-permute-done.38
  310.5 2.7 collective-permute-done.39
  315.8 3.4 %all-to-all-start = ((bf16[32,4,1024]{2,0,1:T(8,128)(2,1)}), bf16[32,4,1024]{2,0,1:T(8,128)(2,1)S(1)}, u32[]{:S(2)}, u32[]{:S(2)}) async-start(bf16[32,4,1024]{2,0,1:T(8,128)(2,1)} %bitcast.215), calls=%async_computation | async-start | bytes 524288 | tf_op jit(solution)/shard_map/all_to_all | solution.py:299
  320.0 5.9 %all-to-all-done = bf16[32,4,1024]{2,0,1:T(8,128)(2,1)S(1)} async-done(((bf16[32,4,1024]{2,0,1:T(8,128)(2,1)}), bf16[32,4,1024]{2,0,1:T(8,128)(2,1)S(1)}, u32[]{:S(2)}, u32[]{:S(2)}) %all-to-all-start) | async-done | bytes 262176 | tf_op jit(solution)/shard_map/all_to_all | solution.py:299
  (171 shorter events, 36.6 us)
Async XLA Ops:
  0.6 32.7 %copy-start = (bf16[4096,128]{1,0:T(8,128)(2,1)S(1)}, bf16[4096,128]{1,0:T(8,128)(2,1)}, u32[]{:S(2)}) copy-start(bf16[4096,128]{1,0:T(8,128)(2,1)} %param.16) | copy-start | bytes 3145732
  0.6 8.1 %copy-start.19 = (s32[1,4]{1,0:T(1,128)S(1)}, s32[1,4]{1,0:T(1,128)}, u32[]{:S(2)}) copy-start(s32[1,4]{1,0:T(1,128)} %param.24) | copy-start | bytes 52
  0.7 8.5 %copy-start.9 = (bf16[4096]{0:T(1024)(128)(2,1)S(1)}, bf16[4096]{0:T(1024)(128)(2,1)}, u32[]{:S(2)}) copy-start(bf16[4096]{0:T(1024)(128)(2,1)} %param.14) | copy-start | bytes 24580
  5.5 82.8 %collective-permute-start.19 = (bf16[1024,896]{1,0:T(8,128)(2,1)}, bf16[1024,896]{1,0:T(8,128)(2,1)}, u32[]{:S(2)}, u32[]{:S(2)}) collective-permute-start(bf16[1024,896]{1,0:T(8,128)(2,1)} %pad_maximum_fusion.3), channel_id=1, source_target_pairs={{0,1},{1,2},{2,3},{3,0},{4,5},{5,6},{6,7},{7,4},{8,9},{9,10},{10,1... | collective-permute-start | bytes 5505032 | tf_op jit(solution)/shard_map/ppermute | solution.py:161
  7.2 84.0 %collective-permute-start.21 = (bf16[1024,896]{1,0:T(8,128)(2,1)}, bf16[1024,896]{1,0:T(8,128)(2,1)}, u32[]{:S(2)}, u32[]{:S(2)}) collective-permute-start(bf16[1024,896]{1,0:T(8,128)(2,1)} %pad_maximum_fusion.3), channel_id=1, source_target_pairs={{0,3},{1,0},{2,1},{3,2},{4,7},{5,4},{6,5},{7,6},{8,11},{9,8},{10,9... | collective-permute-start | bytes 5505032 | tf_op jit(solution)/shard_map/ppermute | solution.py:162
  8.8 7.7 %copy-start.11 = (f32[64]{0:T(128)}, f32[64]{0:T(128)S(1)}, u32[]{:S(2)}) copy-start(f32[64]{0:T(128)S(1)} %multiply_power_fusion) | copy-start | bytes 772
  9.0 1.6 copy-start.16
  9.1 7.3 %copy-start.14 = (f32[128]{0:T(128)}, f32[128]{0:T(128)S(1)}, u32[]{:S(2)}) copy-start(f32[128]{0:T(128)S(1)} %subtract_convert_fusion.1) | copy-start | bytes 1540
  10.7 0.5 copy-start.20
  17.6 12.6 %collective-permute-start = (bf16[128,1,4,128]{3,0,2,1:T(8,128)(2,1)}, bf16[128,1,4,128]{3,0,2,1:T(8,128)(2,1)S(1)}, u32[]{:S(2)}, u32[]{:S(2)}) collective-permute-start(bf16[128,1,4,128]{3,0,2,1:T(8,128)(2,1)} %pad_maximum_fusion.11), channel_id=1, source_target_pairs={{0,4},{4,0},{1,5},{5,1},{2,6},{6,2},{3,7},{7,3},{8,12},{12,8},{9,1... | collective-permute-start | bytes 393224 | tf_op jit(solution)/shard_map/ppermute | solution.py:59
  17.6 113.1 %collective-permute-start.23 = (bf16[448,1024]{1,0:T(8,128)(2,1)}, bf16[448,1024]{1,0:T(8,128)(2,1)}, u32[]{:S(2)}, u32[]{:S(2)}) collective-permute-start(bf16[448,1024]{1,0:T(8,128)(2,1)} %param.22), channel_id=1, source_target_pairs={{0,1},{1,2},{2,3},{3,0},{4,5},{5,6},{6,7},{7,4},{8,9},{9,10},{10,1... | collective-permute-start | bytes 2752520 | tf_op jit(solution)/shard_map/ppermute | solution.py:161
  20.3 4.2 %copy-start.12 = (f32[64]{0:T(128)S(1)}, f32[64]{0:T(128)}, u32[]{:S(2)}) copy-start(f32[64]{0:T(128)} %copy-done.11) | copy-start | bytes 772
  30.9 7.9 %copy-start.13 = (f32[64]{0:T(128)S(1)}, f32[64]{0:T(128)}, u32[]{:S(2)}) copy-start(f32[64]{0:T(128)} %copy-done.11) | copy-start | bytes 772
  30.9 7.9 %copy-start.15 = (f32[128]{0:T(128)S(1)}, f32[128]{0:T(128)}, u32[]{:S(2)}) copy-start(f32[128]{0:T(128)} %copy-done.14) | copy-start | bytes 1540
  30.9 9.4 %collective-permute-start.1 = (bf16[2,128,1,4,128]{4,1,3,2,0:T(8,128)(2,1)}, bf16[2,128,1,4,128]{4,1,3,2,0:T(8,128)(2,1)}, u32[]{:S(2)}, u32[]{:S(2)}) collective-permute-start(bf16[2,128,1,4,128]{4,1,3,2,0:T(8,128)(2,1)} %maximum_select_fusion.1), channel_id=1, source_target_pairs={{0,8},{8,0},{16,24},{24,16},{1,9},{9,1},{17,25},{25,17},{2,10},{10... | collective-permute-start | bytes 786440 | tf_op jit(solution)/shard_map/ppermute | solution.py:59
  35.2 6.5 %copy-start.5 = (bf16[2048,64]{1,0:T(8,128)(2,1)S(1)}, bf16[2048,64]{1,0:T(8,128)(2,1)}, u32[]{:S(2)}) copy-start(bf16[2048,64]{1,0:T(8,128)(2,1)} %get-tuple-element.40) | copy-start | bytes 786436
  67.7 3.9 %copy-start.17 = (s32[128]{0:T(128)S(1)}, s32[128]{0:T(128)}, u32[]{:S(2)}) copy-start(s32[128]{0:T(128)} %copy-done.16) | copy-start | bytes 1540
  67.8 1.0 copy-start.2
  69.8 13.9 %collective-permute-start.2 = (f32[1,4,2,128,130]{3,1,4,2,0:T(4,128)}, f32[1,4,2,128,130]{3,1,4,2,0:T(4,128)}, u32[]{:S(2)}, u32[]{:S(2)}) collective-permute-start(f32[1,4,2,128,130]{3,1,4,2,0:T(4,128)} %copy.88), channel_id=1, source_target_pairs={{0,8},{8,0},{16,24},{24,16},{1,9},{9,1},{17,25},{25,17},{2,10},{10... | collective-permute-start | bytes 1597448 | tf_op jit(solution)/shard_map/ppermute | solution.py:59
  72.1 15.6 %copy-start.3 = (bf16[128,4096]{1,0:T(8,128)(2,1)S(1)}, bf16[128,4096]{1,0:T(8,128)(2,1)}, u32[]{:S(2)}) copy-start(bf16[128,4096]{1,0:T(8,128)(2,1)} %param.13) | copy-start | bytes 3145732
  72.1 15.6 %copy-start.18 = (bf16[4096,128]{1,0:T(8,128)(2,1)S(1)}, bf16[4096,128]{1,0:T(8,128)(2,1)}, u32[]{:S(2)}) copy-start(bf16[4096,128]{1,0:T(8,128)(2,1)} %param.17) | copy-start | bytes 3145732
  72.1 15.6 %copy-start.21 = (f32[128]{0:T(128)S(1)}, f32[128]{0:T(128)}, u32[]{:S(2)}) copy-start(f32[128]{0:T(128)} %copy-done.20) | copy-start | bytes 1540
  87.5 6.7 %collective-permute-start.3 = (f32[1,4,1,128,130]{3,4,2,1,0:T(8,128)S(1)}, f32[1,4,1,128,130]{3,4,2,1,0:T(8,128)S(1)}, u32[]{:S(2)}, u32[]{:S(2)}) collective-permute-start(f32[1,4,1,128,130]{3,4,2,1,0:T(8,128)S(1)} %constant_dynamic-slice_fusion.5), channel_id=1, source_target_pairs={{0,4},{4,0},{1,5},{5,1},{2,6},{6,2},{3,7},{7,3},{8,12},{12,8},{9,1... | collective-permute-start | bytes 798728 | tf_op jit(solution)/shard_map/ppermute | solution.py:59
  89.6 24.0 %collective-permute-start.20 = (bf16[512,896]{1,0:T(8,128)(2,1)S(1)}, bf16[512,896]{1,0:T(8,128)(2,1)S(1)}, u32[]{:S(2)}, u32[]{:S(2)}) collective-permute-start(bf16[512,896]{1,0:T(8,128)(2,1)S(1)} %slice.229), channel_id=1, source_target_pairs={{0,1},{1,2},{2,3},{3,0},{4,5},{5,6},{6,7},{7,4},{8,9},{9,10},{10,1... | collective-permute-start | bytes 2752520 | tf_op jit(solution)/shard_map/ppermute | solution.py:165
  92.5 22.5 %collective-permute-start.22 = (bf16[512,896]{1,0:T(8,128)(2,1)S(1)}, bf16[512,896]{1,0:T(8,128)(2,1)S(1)}, u32[]{:S(2)}, u32[]{:S(2)}) collective-permute-start(bf16[512,896]{1,0:T(8,128)(2,1)S(1)} %slice.230), channel_id=1, source_target_pairs={{0,3},{1,0},{2,1},{3,2},{4,7},{5,4},{6,5},{7,6},{8,11},{9,8},{10,9... | collective-permute-start | bytes 2752520 | tf_op jit(solution)/shard_map/ppermute | solution.py:170
  115.2 6.2 %copy-start.4 = (bf16[512,4096]{1,0:T(8,128)(2,1)S(1)}, bf16[512,4096]{1,0:T(8,128)(2,1)}, u32[]{:S(2)}) copy-start(bf16[512,4096]{1,0:T(8,128)(2,1)} %param.18) | copy-start | bytes 12582916
  121.4 127.8 %collective-permute-start.27 = (bf16[4,1024,896]{2,1,0:T(8,128)(2,1)}, bf16[4,1024,896]{2,1,0:T(8,128)(2,1)}, u32[]{:S(2)}, u32[]{:S(2)}) collective-permute-start(bf16[4,1024,896]{2,1,0:T(8,128)(2,1)} %pad_maximum_fusion), channel_id=1, source_target_pairs={{0,4},{4,0},{1,5},{5,1},{2,6},{6,2},{3,7},{7,3},{8,12},{12,8},{9,1... | collective-permute-start | bytes 22020104 | tf_op jit(solution)/shard_map/ppermute | solution.py:59
  122.1 8.4 %copy-start.10 = (bf16[4096]{0:T(1024)(128)(2,1)S(1)}, bf16[4096]{0:T(1024)(128)(2,1)}, u32[]{:S(2)}) copy-start(bf16[4096]{0:T(1024)(128)(2,1)} %param.19) | copy-start | bytes 24580
  123.3 16.0 %collective-permute-start.4 = (f32[32,4096]{1,0:T(8,128)}, f32[32,4096]{1,0:T(8,128)}, u32[]{:S(2)}, u32[]{:S(2)}) collective-permute-start(f32[32,4096]{1,0:T(8,128)} %get-tuple-element.37), channel_id=1, source_target_pairs={{0,1},{1,2},{2,3},{3,0},{4,5},{5,6},{6,7},{7,4},{8,9},{9,10},{10,1... | collective-permute-start | bytes 1572872 | tf_op jit(solution)/shard_map/ppermute | solution.py:22
  124.8 27.5 %collective-permute-start.5 = (f32[32,4096]{1,0:T(8,128)}, f32[32,4096]{1,0:T(8,128)}, u32[]{:S(2)}, u32[]{:S(2)}) collective-permute-start(f32[32,4096]{1,0:T(8,128)} %get-tuple-element.39), channel_id=1, source_target_pairs={{0,2},{1,3},{2,0},{3,1},{4,6},{5,7},{6,4},{7,5},{8,10},{9,11},{10,... | collective-permute-start | bytes 1572872 | tf_op jit(solution)/shard_map/ppermute | solution.py:22
  127.8 24.4 %collective-permute-start.6 = (f32[32,4096]{1,0:T(8,128)}, f32[32,4096]{1,0:T(8,128)}, u32[]{:S(2)}, u32[]{:S(2)}) collective-permute-start(f32[32,4096]{1,0:T(8,128)} %get-tuple-element.38), channel_id=1, source_target_pairs={{0,3},{1,0},{2,1},{3,2},{4,7},{5,4},{6,5},{7,6},{8,11},{9,8},{10,9... | collective-permute-start | bytes 1572872 | tf_op jit(solution)/shard_map/ppermute | solution.py:22
  130.7 40.1 %collective-permute-start.25 = (bf16[448,1024]{1,0:T(8,128)(2,1)}, bf16[448,1024]{1,0:T(8,128)(2,1)S(1)}, u32[]{:S(2)}, u32[]{:S(2)}) collective-permute-start(bf16[448,1024]{1,0:T(8,128)(2,1)} %param.22), channel_id=1, source_target_pairs={{0,3},{1,0},{2,1},{3,2},{4,7},{5,4},{6,5},{7,6},{8,11},{9,8},{10,9... | collective-permute-start | bytes 2752520 | tf_op jit(solution)/shard_map/ppermute | solution.py:162
  139.3 40.6 %collective-permute-start.24 = (bf16[224,1024]{1,0:T(8,128)(2,1)S(1)}, bf16[224,1024]{1,0:T(8,128)(2,1)}, u32[]{:S(2)}, u32[]{:S(2)}) collective-permute-start(bf16[224,1024]{1,0:T(8,128)(2,1)S(1)} %slice.233), channel_id=1, source_target_pairs={{0,1},{1,2},{2,3},{3,0},{4,5},{5,6},{6,7},{7,4},{8,9},{9,10},{10,1... | collective-permute-start | bytes 1376264 | tf_op jit(solution)/shard_map/ppermute | solution.py:165
  154.8 18.7 %collective-permute-start.13 = (bf16[32,2048]{1,0:T(8,128)(2,1)S(1)}, bf16[32,2048]{1,0:T(8,128)(2,1)S(1)}, u32[]{:S(2)}, u32[]{:S(2)}) collective-permute-start(bf16[32,2048]{1,0:T(8,128)(2,1)S(1)} %get-tuple-element.60), channel_id=1, source_target_pairs={{0,32},{32,64},{64,96},{96,0},{1,33},{33,65},{65,97},{97,1},{2,34}... | collective-permute-start | bytes 393224 | tf_op jit(solution)/shard_map/ppermute | solution.py:22
  156.3 20.0 %collective-permute-start.14 = (bf16[32,2048]{1,0:T(8,128)(2,1)S(1)}, bf16[32,2048]{1,0:T(8,128)(2,1)S(1)}, u32[]{:S(2)}, u32[]{:S(2)}) collective-permute-start(bf16[32,2048]{1,0:T(8,128)(2,1)S(1)} %get-tuple-element.60), channel_id=1, source_target_pairs={{0,64},{32,96},{64,0},{96,32},{1,65},{33,97},{65,1},{97,33},{2,66}... | collective-permute-start | bytes 393224 | tf_op jit(solution)/shard_map/ppermute | solution.py:22
  170.8 18.7 %copy-start.6 = (bf16[448,1024]{1,0:T(8,128)(2,1)}, bf16[448,1024]{1,0:T(8,128)(2,1)S(1)}, u32[]{:S(2)}) copy-start(bf16[448,1024]{1,0:T(8,128)(2,1)S(1)} %collective-permute-done.25) | copy-start | bytes 2752516
  170.8 7.0 %collective-permute-start.15 = (bf16[32,2048]{1,0:T(8,128)(2,1)S(1)}, bf16[32,2048]{1,0:T(8,128)(2,1)S(1)}, u32[]{:S(2)}, u32[]{:S(2)}) collective-permute-start(bf16[32,2048]{1,0:T(8,128)(2,1)S(1)} %get-tuple-element.60), channel_id=1, source_target_pairs={{0,96},{32,0},{64,32},{96,64},{1,97},{33,1},{65,33},{97,65},{2,98}... | collective-permute-start | bytes 393224 | tf_op jit(solution)/shard_map/ppermute | solution.py:22
  173.6 12.4 %collective-permute-start.26 = (bf16[224,1024]{1,0:T(8,128)(2,1)S(1)}, bf16[224,1024]{1,0:T(8,128)(2,1)S(1)}, u32[]{:S(2)}, u32[]{:S(2)}) collective-permute-start(bf16[224,1024]{1,0:T(8,128)(2,1)S(1)} %slice.234), channel_id=1, source_target_pairs={{0,3},{1,0},{2,1},{3,2},{4,7},{5,4},{6,5},{7,6},{8,11},{9,8},{10,9... | collective-permute-start | bytes 1376264 | tf_op jit(solution)/shard_map/ppermute | solution.py:170
  176.3 13.2 %collective-permute-start.7 = (bf16[32,2048]{1,0:T(8,128)(2,1)}, bf16[32,2048]{1,0:T(8,128)(2,1)}, u32[]{:S(2)}, u32[]{:S(2)}) collective-permute-start(bf16[32,2048]{1,0:T(8,128)(2,1)} %get-tuple-element.61), channel_id=1, source_target_pairs={{0,8},{8,16},{16,24},{24,0},{1,9},{9,17},{17,25},{25,1},{2,10},{10... | collective-permute-start | bytes 393224 | tf_op jit(solution)/shard_map/ppermute | solution.py:22
  177.9 32.9 %collective-permute-start.16 = (bf16[4,32,2048]{2,1,0:T(8,128)(2,1)S(1)}, bf16[4,32,2048]{2,1,0:T(8,128)(2,1)}, u32[]{:S(2)}, u32[]{:S(2)}) collective-permute-start(bf16[4,32,2048]{2,1,0:T(8,128)(2,1)S(1)} %get-tuple-element.55), channel_id=1, source_target_pairs={{0,8},{8,16},{16,24},{24,0},{1,9},{9,17},{17,25},{25,1},{2,10},{10... | collective-permute-start | bytes 1572872 | tf_op jit(solution)/shard_map/ppermute | solution.py:22
  179.9 33.2 %collective-permute-start.17 = (bf16[4,32,2048]{2,1,0:T(8,128)(2,1)S(1)}, bf16[4,32,2048]{2,1,0:T(8,128)(2,1)}, u32[]{:S(2)}, u32[]{:S(2)}) collective-permute-start(bf16[4,32,2048]{2,1,0:T(8,128)(2,1)S(1)} %get-tuple-element.55), channel_id=1, source_target_pairs={{0,16},{8,24},{16,0},{24,8},{1,17},{9,25},{17,1},{25,9},{2,18},{10... | collective-permute-start | bytes 1572872 | tf_op jit(solution)/shard_map/ppermute | solution.py:22
  186.0 3.5 %copy-start.8 = (bf16[224,1024]{1,0:T(8,128)(2,1)}, bf16[224,1024]{1,0:T(8,128)(2,1)S(1)}, u32[]{:S(2)}) copy-start(bf16[224,1024]{1,0:T(8,128)(2,1)S(1)} %collective-permute-done.26) | copy-start | bytes 1376260
  186.0 23.8 %collective-permute-start.8 = (bf16[32,2048]{1,0:T(8,128)(2,1)}, bf16[32,2048]{1,0:T(8,128)(2,1)S(1)}, u32[]{:S(2)}, u32[]{:S(2)}) collective-permute-start(bf16[32,2048]{1,0:T(8,128)(2,1)} %get-tuple-element.61), channel_id=1, source_target_pairs={{0,16},{8,24},{16,0},{24,8},{1,17},{9,25},{17,1},{25,9},{2,18},{10... | collective-permute-start | bytes 393224 | tf_op jit(solution)/shard_map/ppermute | solution.py:22
  189.5 20.3 %collective-permute-start.9 = (bf16[32,2048]{1,0:T(8,128)(2,1)}, bf16[32,2048]{1,0:T(8,128)(2,1)S(1)}, u32[]{:S(2)}, u32[]{:S(2)}) collective-permute-start(bf16[32,2048]{1,0:T(8,128)(2,1)} %get-tuple-element.61), channel_id=1, source_target_pairs={{0,24},{8,0},{16,8},{24,16},{1,25},{9,1},{17,9},{25,17},{2,26},{10... | collective-permute-start | bytes 393224 | tf_op jit(solution)/shard_map/ppermute | solution.py:22
  190.4 23.9 %copy-start.7 = (bf16[448,1024]{1,0:T(8,128)(2,1)S(1)}, bf16[448,1024]{1,0:T(8,128)(2,1)}, u32[]{:S(2)}) copy-start(bf16[448,1024]{1,0:T(8,128)(2,1)} %copy-done.6) | copy-start | bytes 2752516
  209.7 12.5 %collective-permute-start.18 = (bf16[4,32,2048]{2,1,0:T(8,128)(2,1)S(1)}, bf16[4,32,2048]{2,1,0:T(8,128)(2,1)S(1)}, u32[]{:S(2)}, u32[]{:S(2)}) collective-permute-start(bf16[4,32,2048]{2,1,0:T(8,128)(2,1)S(1)} %get-tuple-element.55), channel_id=1, source_target_pairs={{0,24},{8,0},{16,8},{24,16},{1,25},{9,1},{17,9},{25,17},{2,26},{10... | collective-permute-start | bytes 1572872 | tf_op jit(solution)/shard_map/ppermute | solution.py:22
  210.7 25.1 %collective-permute-start.10 = (bf16[4,32,2048]{2,1,0:T(8,128)(2,1)S(1)}, bf16[4,32,2048]{2,1,0:T(8,128)(2,1)S(1)}, u32[]{:S(2)}, u32[]{:S(2)}) collective-permute-start(bf16[4,32,2048]{2,1,0:T(8,128)(2,1)S(1)} %get-tuple-element.57), channel_id=1, source_target_pairs={{0,32},{32,64},{64,96},{96,0},{1,33},{33,65},{65,97},{97,1},{2,34}... | collective-permute-start | bytes 1572872 | tf_op jit(solution)/shard_map/ppermute | solution.py:22
  210.8 25.0 %collective-permute-start.11 = (bf16[4,32,2048]{2,1,0:T(8,128)(2,1)S(1)}, bf16[4,32,2048]{2,1,0:T(8,128)(2,1)S(1)}, u32[]{:S(2)}, u32[]{:S(2)}) collective-permute-start(bf16[4,32,2048]{2,1,0:T(8,128)(2,1)S(1)} %get-tuple-element.57), channel_id=1, source_target_pairs={{0,64},{32,96},{64,0},{96,32},{1,65},{33,97},{65,1},{97,33},{2,66}... | collective-permute-start | bytes 1572872 | tf_op jit(solution)/shard_map/ppermute | solution.py:22
  213.1 23.3 %collective-permute-start.12 = (bf16[4,32,2048]{2,1,0:T(8,128)(2,1)S(1)}, bf16[4,32,2048]{2,1,0:T(8,128)(2,1)S(1)}, u32[]{:S(2)}, u32[]{:S(2)}) collective-permute-start(bf16[4,32,2048]{2,1,0:T(8,128)(2,1)S(1)} %get-tuple-element.57), channel_id=1, source_target_pairs={{0,96},{32,0},{64,32},{96,64},{1,97},{33,1},{65,33},{97,65},{2,98}... | collective-permute-start | bytes 1572872 | tf_op jit(solution)/shard_map/ppermute | solution.py:22
  222.3 34.5 %collective-permute-start.28 = (bf16[448,4096]{1,0:T(8,128)(2,1)S(1)}, bf16[448,4096]{1,0:T(8,128)(2,1)S(1)}, u32[]{:S(2)}, u32[]{:S(2)}) collective-permute-start(bf16[448,4096]{1,0:T(8,128)(2,1)S(1)} %bitcast.223), channel_id=1, source_target_pairs={{0,4},{4,0},{1,5},{5,1},{2,6},{6,2},{3,7},{7,3},{8,12},{12,8},{9,1... | collective-permute-start | bytes 11010056 | tf_op jit(solution)/shard_map/ppermute | solution.py:59
  259.4 24.9 %collective-permute-start.29 = (bf16[4,32,2048]{2,1,0:T(8,128)(2,1)S(1)}, bf16[4,32,2048]{2,1,0:T(8,128)(2,1)S(1)}, u32[]{:S(2)}, u32[]{:S(2)}) collective-permute-start(bf16[4,32,2048]{2,1,0:T(8,128)(2,1)S(1)} %get-tuple-element.27), channel_id=1, source_target_pairs={{0,96},{32,0},{64,32},{96,64},{1,97},{33,1},{65,33},{97,65},{2,98}... | collective-permute-start | bytes 1572872 | tf_op jit(solution)/shard_map/ppermute | solution.py:22
  261.9 24.1 %collective-permute-start.30 = (bf16[4,32,2048]{2,1,0:T(8,128)(2,1)S(1)}, bf16[4,32,2048]{2,1,0:T(8,128)(2,1)S(1)}, u32[]{:S(2)}, u32[]{:S(2)}) collective-permute-start(bf16[4,32,2048]{2,1,0:T(8,128)(2,1)S(1)} %get-tuple-element.29), channel_id=1, source_target_pairs={{0,64},{32,96},{64,0},{96,32},{1,65},{33,97},{65,1},{97,33},{2,66}... | collective-permute-start | bytes 1572872 | tf_op jit(solution)/shard_map/ppermute | solution.py:22
  261.9 26.0 %collective-permute-start.31 = (bf16[4,32,2048]{2,1,0:T(8,128)(2,1)S(1)}, bf16[4,32,2048]{2,1,0:T(8,128)(2,1)S(1)}, u32[]{:S(2)}, u32[]{:S(2)}) collective-permute-start(bf16[4,32,2048]{2,1,0:T(8,128)(2,1)S(1)} %get-tuple-element.28), channel_id=1, source_target_pairs={{0,32},{32,64},{64,96},{96,0},{1,33},{33,65},{65,97},{97,1},{2,34}... | collective-permute-start | bytes 1572872 | tf_op jit(solution)/shard_map/ppermute | solution.py:22
  263.3 28.8 %collective-permute-start.35 = (bf16[4,32,2048]{2,1,0:T(8,128)(2,1)S(1)}, bf16[4,32,2048]{2,1,0:T(8,128)(2,1)S(1)}, u32[]{:S(2)}, u32[]{:S(2)}) collective-permute-start(bf16[4,32,2048]{2,1,0:T(8,128)(2,1)S(1)} %get-tuple-element.34), channel_id=1, source_target_pairs={{0,24},{8,0},{16,8},{24,16},{1,25},{9,1},{17,9},{25,17},{2,26},{10... | collective-permute-start | bytes 1572872 | tf_op jit(solution)/shard_map/ppermute | solution.py:22
  263.9 28.3 %collective-permute-start.36 = (bf16[4,32,2048]{2,1,0:T(8,128)(2,1)S(1)}, bf16[4,32,2048]{2,1,0:T(8,128)(2,1)S(1)}, u32[]{:S(2)}, u32[]{:S(2)}) collective-permute-start(bf16[4,32,2048]{2,1,0:T(8,128)(2,1)S(1)} %get-tuple-element.36), channel_id=1, source_target_pairs={{0,16},{8,24},{16,0},{24,8},{1,17},{9,25},{17,1},{25,9},{2,18},{10... | collective-permute-start | bytes 1572872 | tf_op jit(solution)/shard_map/ppermute | solution.py:22
  284.3 18.0 %collective-permute-start.37 = (bf16[4,32,2048]{2,1,0:T(8,128)(2,1)S(1)}, bf16[4,32,2048]{2,1,0:T(8,128)(2,1)S(1)}, u32[]{:S(2)}, u32[]{:S(2)}) collective-permute-start(bf16[4,32,2048]{2,1,0:T(8,128)(2,1)S(1)} %get-tuple-element.35), channel_id=1, source_target_pairs={{0,8},{8,16},{16,24},{24,0},{1,9},{9,17},{17,25},{25,1},{2,10},{10... | collective-permute-start | bytes 1572872 | tf_op jit(solution)/shard_map/ppermute | solution.py:22
  288.3 18.3 %collective-permute-start.32 = (bf16[32,2048]{1,0:T(8,128)(2,1)S(1)}, bf16[32,2048]{1,0:T(8,128)(2,1)S(1)}, u32[]{:S(2)}, u32[]{:S(2)}) collective-permute-start(bf16[32,2048]{1,0:T(8,128)(2,1)S(1)} %get-tuple-element.48), channel_id=1, source_target_pairs={{0,24},{8,0},{16,8},{24,16},{1,25},{9,1},{17,9},{25,17},{2,26},{10... | collective-permute-start | bytes 393224 | tf_op jit(solution)/shard_map/ppermute | solution.py:22
  288.9 18.7 %collective-permute-start.33 = (bf16[32,2048]{1,0:T(8,128)(2,1)S(1)}, bf16[32,2048]{1,0:T(8,128)(2,1)S(1)}, u32[]{:S(2)}, u32[]{:S(2)}) collective-permute-start(bf16[32,2048]{1,0:T(8,128)(2,1)S(1)} %get-tuple-element.50), channel_id=1, source_target_pairs={{0,16},{8,24},{16,0},{24,8},{1,17},{9,25},{17,1},{25,9},{2,18},{10... | collective-permute-start | bytes 393224 | tf_op jit(solution)/shard_map/ppermute | solution.py:22
  292.2 15.4 %collective-permute-start.34 = (bf16[32,2048]{1,0:T(8,128)(2,1)S(1)}, bf16[32,2048]{1,0:T(8,128)(2,1)S(1)}, u32[]{:S(2)}, u32[]{:S(2)}) collective-permute-start(bf16[32,2048]{1,0:T(8,128)(2,1)S(1)} %get-tuple-element.49), channel_id=1, source_target_pairs={{0,8},{8,16},{16,24},{24,0},{1,9},{9,17},{17,25},{25,1},{2,10},{10... | collective-permute-start | bytes 393224 | tf_op jit(solution)/shard_map/ppermute | solution.py:22
  302.7 7.8 %collective-permute-start.38 = (bf16[32,2048]{1,0:T(8,128)(2,1)S(1)}, bf16[32,2048]{1,0:T(8,128)(2,1)S(1)}, u32[]{:S(2)}, u32[]{:S(2)}) collective-permute-start(bf16[32,2048]{1,0:T(8,128)(2,1)S(1)} %get-tuple-element.51), channel_id=1, source_target_pairs={{0,96},{32,0},{64,32},{96,64},{1,97},{33,1},{65,33},{97,65},{2,98}... | collective-permute-start | bytes 393224 | tf_op jit(solution)/shard_map/ppermute | solution.py:22
  306.6 6.6 %collective-permute-start.39 = (bf16[32,2048]{1,0:T(8,128)(2,1)S(1)}, bf16[32,2048]{1,0:T(8,128)(2,1)S(1)}, u32[]{:S(2)}, u32[]{:S(2)}) collective-permute-start(bf16[32,2048]{1,0:T(8,128)(2,1)S(1)} %get-tuple-element.53), channel_id=1, source_target_pairs={{0,64},{32,96},{64,0},{96,32},{1,65},{33,97},{65,1},{97,33},{2,66}... | collective-permute-start | bytes 393224 | tf_op jit(solution)/shard_map/ppermute | solution.py:22
  306.6 7.6 %collective-permute-start.40 = (bf16[32,2048]{1,0:T(8,128)(2,1)S(1)}, bf16[32,2048]{1,0:T(8,128)(2,1)S(1)}, u32[]{:S(2)}, u32[]{:S(2)}) collective-permute-start(bf16[32,2048]{1,0:T(8,128)(2,1)S(1)} %get-tuple-element.52), channel_id=1, source_target_pairs={{0,32},{32,64},{64,96},{96,0},{1,33},{33,65},{65,97},{97,1},{2,34}... | collective-permute-start | bytes 393224 | tf_op jit(solution)/shard_map/ppermute | solution.py:22
  314.2 12.4 %copy-start.1 = (bf16[4096,128]{1,0:T(8,128)(2,1)S(1)}, bf16[4096,128]{1,0:T(8,128)(2,1)}, u32[]{:S(2)}) copy-start(bf16[4096,128]{1,0:T(8,128)(2,1)} %param.16) | copy-start | bytes 3145732
  315.8 10.1 %all-to-all-start = ((bf16[32,4,1024]{2,0,1:T(8,128)(2,1)}), bf16[32,4,1024]{2,0,1:T(8,128)(2,1)S(1)}, u32[]{:S(2)}, u32[]{:S(2)}) async-start(bf16[32,4,1024]{2,0,1:T(8,128)(2,1)} %bitcast.215), calls=%async_computation | async-start | bytes 524288 | tf_op jit(solution)/shard_map/all_to_all | solution.py:299

commit v7 on v6

--- a/solution.py
+++ b/solution.py
@@ -158,8 +158,12 @@
     mlp_index = lax.axis_index("mlp")
 
     own = (jnp.concatenate([w_gate, w_up], axis=1), w_down)
-    from_left = lax.ppermute(own, "mlp", [(i, (i + 1) % n_mlp) for i in range(n_mlp)])
-    from_right = lax.ppermute(own, "mlp", [(i, (i - 1) % n_mlp) for i in range(n_mlp)])
+    left_gu = shifted(own[0], "mlp", n_mlp, 1)
+    right_gu = shifted(own[0], "mlp", n_mlp, -1)
+    left_wd = shifted(own[1], "mlp", n_mlp, 1)
+    right_wd = shifted(own[1], "mlp", n_mlp, -1)
+    from_left = (left_gu, left_wd)
+    from_right = (right_gu, right_wd)
     half_gu = width_part // 2
     half_wd = unit_count // 2
     relay_a = lax.ppermute(
@@ -237,7 +241,8 @@
     states = states.reshape(kv_heads, group, runs, slots_here, head_dim + 2)
     keep = lax.dynamic_slice_in_dim(states, z_bit * 2, 2, 2)
     send = lax.dynamic_slice_in_dim(states, (1 - z_bit) * 2, 2, 2)
-    states = combine_states(keep, swap_with_partner(send, "az", n_az))
+    from_z = swap_with_partner(send, "az", n_az)
+    states = combine_states(keep, from_z)
     keep = lax.dynamic_slice_in_dim(states, rc_index, 1, 2)
     send = lax.dynamic_slice_in_dim(states, 1 - rc_index, 1, 2)
     prefix_state = combine_states(keep, swap_with_partner(send, "rc", n_rc))[:, :, 0]

time: 333 us -> 333 us (level)
    ppermute x27 -> x31, waiting for transfers between devices: 91.9 us -> 104 us  [shifted(): lax.ppermute(value, axis, [(i, (i + shift) % size) for i in range(size)])]
    ppermute x4 -> x0, waiting for transfers between devices: 11.8 us -> none  [the longest x2 11.8 us: layer(): lax.ppermute(own, 'mlp', [(i, (i - 1) % n_mlp) for i in range(n_mlp)])]
    ppermute x4 -> x0, starting transfers between devices: 3.73 us -> none  [the longest x2 2.17 us: layer(): lax.ppermute(own, 'mlp', [(i, (i + 1) % n_mlp) for i in range(n_mlp)])]
    ppermute x27 -> x31, starting transfers between devices: 43.8 us -> 47.5 us  [shifted(): lax.ppermute(value, axis, [(i, (i + shift) % size) for i in range(size)])]
where the time goes in v7:
time: 333 us; the launch traced here: 327 us
  waiting for transfers between devices  146 us (44%)
  starting transfers between devices  61.9 us (19%)
  other arithmetic  46.9 us (14%)
  matrix products  43.3 us (13%)
  local copies, waits for them, and re-layouts  25.9 us (8%)
    ppermute x31, waiting for transfers between devices, shifted(): lax.ppermute(value, axis, [(i, (i + shift) % size) for i in range(size)])  104 us
    ppermute x31, starting transfers between devices, shifted(): lax.ppermute(value, axis, [(i, (i + shift) % size) for i in range(size)])  47.5 us
    ppermute x2, waiting for transfers between devices, layer(): lax.ppermute((from_left[0][:half_gu], from_left[1][:half_wd]), 'mlp', [(i...  19.1 us
    dot_general x2, matrix products, layer(): jnp.dot(tokens_ring, weights_here, preferred_element_type=jnp.float32)  15.2 us
    ppermute x6, waiting for transfers between devices, swap_with_partner(): lax.ppermute(value, axis, [(source, source ^ 1) for source in range(size)])  12.4 us
    convert_element_type x1, other arithmetic, partial_attention(): weights.astype(jnp.bfloat16)  10.3 us
    unnamed x51, local copies, waits for them, and re-layouts  9.78 us
    dot_general x2, matrix products, partial_attention(): jnp.einsum('qkgd,nkd->kgqn', grouped_queries, key_block, preferred_elemen...  9.53 us
  transfers between devices with their start and end apart: 42, of which 19 were waited for; matrix products, arithmetic and copies ran while one was open for 32% of the time, Pallas kernels for 0%

profile of v7, /device:TPU:0, one launch (start us, length us, event | category | flops | bytes accessed | tf_op | source)
XLA Modules:
  0.0 326.9 jit_solution(969821785391801489)
XLA Ops:
  0.7 1.5 copy.96
  2.2 1.5 copy.97
  3.7 1.8 pad_maximum_fusion.3
  5.5 1.7 collective-permute-start.19
  7.2 1.5 collective-permute-start.21
  9.2 1.5 multiply_reduce_fusion
  11.2 4.0 %fusion.91 = f32[128,512]{1,0:T(8,128)} fusion(bf16[4096,512]{1,0:T(8,128)(2,1)} %param.15, f32[4096]{0:T(1024)S(1)} %convert_element_type.197, f32[128]{0:T(128)S(1)} %add_rsqrt_fusion.1, bf16[128,4096]{1,0:T(8,128)(2,1)} %param.13), kind=kOutput, calls=%fused_computation.216 | convolution fusion | flops 538968064 | bytes 5521920 | tf_op jit(solution)/shard_map/dot_general | solution.py:195
  20.3 4.1 %fusion.94 = (bf16[2048,1,128]{2,1,0:T(2,128)(2,1)}, bf16[2048,1,128]{2,1,0:T(2,128)(2,1)S(1)}) fusion(bf16[2048,2,128]{2,1,0:T(2,128)(2,1)} %param.23), kind=kLoop, calls=%fused_computation.217 | loop fusion | bytes 2097152 | tf_op jit(solution)/shard_map/slice | solution.py:221
  24.5 5.6 %fusion.46 = (bf16[2048,64]{1,0:T(8,128)(2,1)}, bf16[2048,64]{1,0:T(8,128)(2,1)}) fusion(f32[2048,1,128]{2,0,1:T(8,128)S(1)} %copy_convert_fusion, f32[64]{0:T(128)S(1)} %copy-done.12, f32[2048]{0:T(1024)S(1)} %add_convert_fusion.3), kind=kLoop, calls=%fused_computation.103 | loop fusion | flops 1179648 | bytes 1581312 | tf_op jit(solution)/shard_map/concatenate | solution.py:70
  30.9 2.4 collective-permute-start.1
  33.3 1.8 convolution_bitcast_fusion.1
  35.2 3.6 %copy.112 = bf16[2048,1,128]{0,2,1:T(8,128)(2,1)} copy(bf16[2048,1,128]{2,1,0:T(2,128)(2,1)} %get-tuple-element.42) | data formatting | bytes 1048576
  39.0 1.3 collective-permute-done.1
  40.3 1.3 maximum_select_fusion
  41.7 9.2 %bitcast_reduce_fusion = (f32[4,512]{1,0:T(4,128)S(1)}, f32[2048,512,4]{0,1,2:T(8,128)}) fusion(bf16[512,4,128]{2,0,1:T(8,128)(2,1)S(1)} %bitcast.225, bf16[2048,64]{1,0:T(8,128)(2,1)} %get-tuple-element.41, bf16[2048,64]{1,0:T(8,128)(2,1)S(1)} %copy-done.5), kind=kOutput, calls=%fused_computation.2 | convolution fusion | flops 1083176960 | bytes 17833984 | tf_op jit(solution)/shard_map/qkgd,nkd->kgqn/dot_general | solution.py:97
  51.0 10.3 %fusion.2 = (bf16[1,4,512,2048]{3,2,1,0:T(8,128)(2,1)}, f32[4,512]{1,0:T(4,128)S(1)}) fusion(f32[2048,512,4]{0,1,2:T(8,128)} %get-tuple-element.69, f32[4,512]{1,0:T(4,128)S(1)} %get-tuple-element.68), kind=kLoop, calls=%fused_computation.5 | loop fusion | flops 16775168 | bytes 25182208 | tf_op jit(solution)/shard_map/convert_element_type | solution.py:107
  61.3 6.3 %convolution_bitcast_fusion = f32[1,4,4,128,128]{3,4,2,1,0:T(8,128)S(1)} fusion(bf16[4,4,128,2048]{3,2,1,0:T(8,128)(2,1)} %bitcast.217, bf16[2048,1,128]{0,2,1:T(8,128)(2,1)} %copy.112), kind=kOutput, calls=%fused_computation.33 | convolution fusion | flops 1073741824 | bytes 9961472 | tf_op jit(solution)/shard_map/kgqn,nkd->kgqd/dot_general | solution.py:105
  69.8 1.7 collective-permute-start.2
  72.7 11.0 %collective-permute-done.2 = f32[1,4,2,128,130]{3,1,4,2,0:T(4,128)} collective-permute-done((f32[1,4,2,128,130]{3,1,4,2,0:T(4,128)}, f32[1,4,2,128,130]{3,1,4,2,0:T(4,128)}, u32[]{:S(2)}, u32[]{:S(2)}) %collective-permute-start.2) | collective-permute-done | bytes 532512 | tf_op jit(solution)/shard_map/ppermute | solution.py:59
  89.6 1.6 collective-permute-start.20
  92.5 1.7 collective-permute-start.22
  94.6 19.0 %collective-permute-done.20 = bf16[512,896]{1,0:T(8,128)(2,1)S(1)} collective-permute-done((bf16[512,896]{1,0:T(8,128)(2,1)S(1)}, bf16[512,896]{1,0:T(8,128)(2,1)S(1)}, u32[]{:S(2)}, u32[]{:S(2)}) %collective-permute-start.20) | collective-permute-done | bytes 917536 | tf_op jit(solution)/shard_map/ppermute | solution.py:169
  113.6 1.4 collective-permute-done.22
  115.2 6.2 %pad_maximum_fusion = bf16[4,1024,896]{2,1,0:T(8,128)(2,1)} fusion(bf16[1,1024,896]{2,1,0:T(8,128)(2,1)} %bitcast.69, bf16[1,1024,896]{2,1,0:T(8,128)(2,1)S(1)} %maximum_bitcast_fusion.2, bf16[1,1024,896]{2,1,0:T(8,128)(2,1)} %bitcast.67, bf16[1,1024,896]{2,1,0:T(8,128)(2,1)S(1)} %fusion.110), kind=kLoop, calls=%fused_computation.7 | loop fusion | flops 11010048 | bytes 14680064 | tf_op jit(solution)/shard_map/stack | solution.py:183
  123.3 1.4 collective-permute-start.4
  124.8 3.1 collective-permute-start.5
  129.0 1.5 convert_element_type.194
  131.7 7.6 %collective-permute-done.4 = f32[32,4096]{1,0:T(8,128)} collective-permute-done((f32[32,4096]{1,0:T(8,128)}, f32[32,4096]{1,0:T(8,128)}, u32[]{:S(2)}, u32[]{:S(2)}) %collective-permute-start.4) | collective-permute-done | bytes 524320 | tf_op jit(solution)/shard_map/ppermute | solution.py:22
  139.9 12.3 %collective-permute-done.5 = f32[32,4096]{1,0:T(8,128)} collective-permute-done((f32[32,4096]{1,0:T(8,128)}, f32[32,4096]{1,0:T(8,128)}, u32[]{:S(2)}, u32[]{:S(2)}) %collective-permute-start.5) | collective-permute-done | bytes 524320 | tf_op jit(solution)/shard_map/ppermute | solution.py:22
  152.2 1.7 fusion.31
  154.8 1.4 collective-permute-start.13
  156.3 2.7 collective-permute-start.14
  159.0 11.8 %collective-permute-done.25 = bf16[448,1024]{1,0:T(8,128)(2,1)S(1)} collective-permute-done((bf16[448,1024]{1,0:T(8,128)(2,1)}, bf16[448,1024]{1,0:T(8,128)(2,1)S(1)}, u32[]{:S(2)}, u32[]{:S(2)}) %collective-permute-start.25) | collective-permute-done | bytes 917536 | tf_op jit(solution)/shard_map/ppermute | solution.py:22
  170.8 2.7 collective-permute-start.15
  173.6 2.7 collective-permute-start.26
  176.3 1.6 collective-permute-start.7
  177.9 2.0 collective-permute-start.16
  179.9 1.8 collective-permute-start.17
  181.9 4.1 %collective-permute-done.26 = bf16[224,1024]{1,0:T(8,128)(2,1)S(1)} collective-permute-done((bf16[224,1024]{1,0:T(8,128)(2,1)S(1)}, bf16[224,1024]{1,0:T(8,128)(2,1)S(1)}, u32[]{:S(2)}, u32[]{:S(2)}) %collective-permute-start.26) | collective-permute-done | bytes 458784 | tf_op jit(solution)/shard_map/ppermute | solution.py:174
  186.0 3.5 %collective-permute-start.8 = (bf16[32,2048]{1,0:T(8,128)(2,1)}, bf16[32,2048]{1,0:T(8,128)(2,1)S(1)}, u32[]{:S(2)}, u32[]{:S(2)}) collective-permute-start(bf16[32,2048]{1,0:T(8,128)(2,1)} %get-tuple-element.61), channel_id=1, source_target_pairs={{0,16},{8,24},{16,0},{24,8},{1,17},{9,25},{17,1},{25,9},{2,18},{10... | collective-permute-start | bytes 393224 | tf_op jit(solution)/shard_map/ppermute | solution.py:22
  190.4 1.3 maximum_bitcast_fusion.3
  191.7 18.0 %collective-permute-done.8 = bf16[32,2048]{1,0:T(8,128)(2,1)S(1)} collective-permute-done((bf16[32,2048]{1,0:T(8,128)(2,1)}, bf16[32,2048]{1,0:T(8,128)(2,1)S(1)}, u32[]{:S(2)}, u32[]{:S(2)}) %collective-permute-start.8) | collective-permute-done | bytes 131104 | tf_op jit(solution)/shard_map/ppermute | solution.py:22
  210.8 2.3 collective-permute-start.11
  214.2 1.7 maximum_bitcast_fusion
  216.3 6.0 %collective-permute-done.18 = bf16[4,32,2048]{2,1,0:T(8,128)(2,1)S(1)} collective-permute-done((bf16[4,32,2048]{2,1,0:T(8,128)(2,1)S(1)}, bf16[4,32,2048]{2,1,0:T(8,128)(2,1)S(1)}, u32[]{:S(2)}, u32[]{:S(2)}) %collective-permute-start.18) | collective-permute-done | bytes 524320 | tf_op jit(solution)/shard_map/ppermute | solution.py:22
  222.5 1.5 maximum_bitcast_fusion.1
  224.2 11.6 %collective-permute-done.10 = bf16[4,32,2048]{2,1,0:T(8,128)(2,1)S(1)} collective-permute-done((bf16[4,32,2048]{2,1,0:T(8,128)(2,1)S(1)}, bf16[4,32,2048]{2,1,0:T(8,128)(2,1)S(1)}, u32[]{:S(2)}, u32[]{:S(2)}) %collective-permute-start.10) | collective-permute-done | bytes 524320 | tf_op jit(solution)/shard_map/ppermute | solution.py:22
  236.7 2.5 fusion.18
  239.2 7.6 %fusion.30 = f32[512,896]{1,0:T(8,128)S(1)} fusion(bf16[4096,896]{1,0:T(8,128)(2,1)} %bitcast.70, bf16[512,1024]{1,0:T(8,128)(2,1)S(1)} %get-tuple-element.33, bf16[512,1024]{1,0:T(8,128)(2,1)S(1)} %get-tuple-element.32, bf16[512,1024]{1,0:T(8,128)(2,1)S(1)} %get-tuple-element.31, bf16[512,1024]{1,0:T(8,128)(2,1)S(1)} %get-tuple-element.30), kind=kOutput, calls=%fused_computation.70 | convolution fusion | flops 3774873600 | bytes 13369344 | tf_op jit(solution)/shard_map/dot_general | solution.py:287
  246.8 2.4 convolution_convert_fusion.1
  249.2 7.6 %fusion.29 = f32[512,896]{1,0:T(8,128)S(1)} fusion(bf16[4096,896]{1,0:T(8,128)(2,1)} %bitcast.75, bf16[512,1024]{1,0:T(8,128)(2,1)S(1)} %get-tuple-element.33, bf16[512,1024]{1,0:T(8,128)(2,1)S(1)} %get-tuple-element.32, bf16[512,1024]{1,0:T(8,128)(2,1)S(1)} %get-tuple-element.31, bf16[512,1024]{1,0:T(8,128)(2,1)S(1)} %get-tuple-element.30), kind=kOutput, calls=%fused_computation.69 | convolution fusion | flops 3774873600 | bytes 13369344 | tf_op jit(solution)/shard_map/dot_general | solution.py:287
  256.8 2.5 add_convert_fusion
  259.4 2.5 collective-permute-start.29
  263.9 3.3 %collective-permute-start.36 = (bf16[4,32,2048]{2,1,0:T(8,128)(2,1)S(1)}, bf16[4,32,2048]{2,1,0:T(8,128)(2,1)S(1)}, u32[]{:S(2)}, u32[]{:S(2)}) collective-permute-start(bf16[4,32,2048]{2,1,0:T(8,128)(2,1)S(1)} %get-tuple-element.36), channel_id=1, source_target_pairs={{0,16},{8,24},{16,0},{24,8},{1,17},{9,25},{17,1},{25,9},{2,18},{10... | collective-permute-start | bytes 1572872 | tf_op jit(solution)/shard_map/ppermute | solution.py:22
  267.2 17.1 %collective-permute-done.29 = bf16[4,32,2048]{2,1,0:T(8,128)(2,1)S(1)} collective-permute-done((bf16[4,32,2048]{2,1,0:T(8,128)(2,1)S(1)}, bf16[4,32,2048]{2,1,0:T(8,128)(2,1)S(1)}, u32[]{:S(2)}, u32[]{:S(2)}) %collective-permute-start.29) | collective-permute-done | bytes 524320 | tf_op jit(solution)/shard_map/ppermute | solution.py:22
  284.3 1.7 collective-permute-start.37
  286.0 1.9 collective-permute-done.31
  288.9 3.3 %collective-permute-start.33 = (bf16[32,2048]{1,0:T(8,128)(2,1)S(1)}, bf16[32,2048]{1,0:T(8,128)(2,1)S(1)}, u32[]{:S(2)}, u32[]{:S(2)}) collective-permute-start(bf16[32,2048]{1,0:T(8,128)(2,1)S(1)} %get-tuple-element.50), channel_id=1, source_target_pairs={{0,16},{8,24},{16,0},{24,8},{1,17},{9,25},{17,1},{25,9},{2,18},{10... | collective-permute-start | bytes 393224 | tf_op jit(solution)/shard_map/ppermute | solution.py:22
  292.2 10.1 %collective-permute-done.37 = bf16[4,32,2048]{2,1,0:T(8,128)(2,1)S(1)} collective-permute-done((bf16[4,32,2048]{2,1,0:T(8,128)(2,1)S(1)}, bf16[4,32,2048]{2,1,0:T(8,128)(2,1)S(1)}, u32[]{:S(2)}, u32[]{:S(2)}) %collective-permute-start.37) | collective-permute-done | bytes 524320 | tf_op jit(solution)/shard_map/ppermute | solution.py:22
  302.7 3.9 %collective-permute-start.38 = (bf16[32,2048]{1,0:T(8,128)(2,1)S(1)}, bf16[32,2048]{1,0:T(8,128)(2,1)S(1)}, u32[]{:S(2)}, u32[]{:S(2)}) collective-permute-start(bf16[32,2048]{1,0:T(8,128)(2,1)S(1)} %get-tuple-element.51), channel_id=1, source_target_pairs={{0,96},{32,0},{64,32},{96,64},{1,97},{33,1},{65,33},{97,65},{2,98}... | collective-permute-start | bytes 393224 | tf_op jit(solution)/shard_map/ppermute | solution.py:22
  307.6 2.9 collective-permute-done.38
  310.5 2.7 collective-permute-done.39
  315.8 3.4 %all-to-all-start = ((bf16[32,4,1024]{2,0,1:T(8,128)(2,1)}), bf16[32,4,1024]{2,0,1:T(8,128)(2,1)S(1)}, u32[]{:S(2)}, u32[]{:S(2)}) async-start(bf16[32,4,1024]{2,0,1:T(8,128)(2,1)} %bitcast.215), calls=%async_computation | async-start | bytes 524288 | tf_op jit(solution)/shard_map/all_to_all | solution.py:304
  320.0 5.9 %all-to-all-done = bf16[32,4,1024]{2,0,1:T(8,128)(2,1)S(1)} async-done(((bf16[32,4,1024]{2,0,1:T(8,128)(2,1)}), bf16[32,4,1024]{2,0,1:T(8,128)(2,1)S(1)}, u32[]{:S(2)}, u32[]{:S(2)}) %all-to-all-start) | async-done | bytes 262176 | tf_op jit(solution)/shard_map/all_to_all | solution.py:304
  (171 shorter events, 36.6 us)
Async XLA Ops:
  0.6 32.7 %copy-start = (bf16[4096,128]{1,0:T(8,128)(2,1)S(1)}, bf16[4096,128]{1,0:T(8,128)(2,1)}, u32[]{:S(2)}) copy-start(bf16[4096,128]{1,0:T(8,128)(2,1)} %param.16) | copy-start | bytes 3145732
  0.6 8.1 %copy-start.19 = (s32[1,4]{1,0:T(1,128)S(1)}, s32[1,4]{1,0:T(1,128)}, u32[]{:S(2)}) copy-start(s32[1,4]{1,0:T(1,128)} %param.24) | copy-start | bytes 52
  0.7 8.5 %copy-start.9 = (bf16[4096]{0:T(1024)(128)(2,1)S(1)}, bf16[4096]{0:T(1024)(128)(2,1)}, u32[]{:S(2)}) copy-start(bf16[4096]{0:T(1024)(128)(2,1)} %param.14) | copy-start | bytes 24580
  5.5 82.8 %collective-permute-start.19 = (bf16[1024,896]{1,0:T(8,128)(2,1)}, bf16[1024,896]{1,0:T(8,128)(2,1)}, u32[]{:S(2)}, u32[]{:S(2)}) collective-permute-start(bf16[1024,896]{1,0:T(8,128)(2,1)} %pad_maximum_fusion.3), channel_id=1, source_target_pairs={{0,1},{1,2},{2,3},{3,0},{4,5},{5,6},{6,7},{7,4},{8,9},{9,10},{10,1... | collective-permute-start | bytes 5505032 | tf_op jit(solution)/shard_map/ppermute | solution.py:22
  7.2 84.0 %collective-permute-start.21 = (bf16[1024,896]{1,0:T(8,128)(2,1)}, bf16[1024,896]{1,0:T(8,128)(2,1)}, u32[]{:S(2)}, u32[]{:S(2)}) collective-permute-start(bf16[1024,896]{1,0:T(8,128)(2,1)} %pad_maximum_fusion.3), channel_id=1, source_target_pairs={{0,3},{1,0},{2,1},{3,2},{4,7},{5,4},{6,5},{7,6},{8,11},{9,8},{10,9... | collective-permute-start | bytes 5505032 | tf_op jit(solution)/shard_map/ppermute | solution.py:22
  8.8 7.7 %copy-start.11 = (f32[64]{0:T(128)}, f32[64]{0:T(128)S(1)}, u32[]{:S(2)}) copy-start(f32[64]{0:T(128)S(1)} %multiply_power_fusion) | copy-start | bytes 772
  9.0 1.6 copy-start.16
  9.1 7.3 %copy-start.14 = (f32[128]{0:T(128)}, f32[128]{0:T(128)S(1)}, u32[]{:S(2)}) copy-start(f32[128]{0:T(128)S(1)} %subtract_convert_fusion.1) | copy-start | bytes 1540
  10.7 0.5 copy-start.20
  17.6 12.6 %collective-permute-start = (bf16[128,1,4,128]{3,0,2,1:T(8,128)(2,1)}, bf16[128,1,4,128]{3,0,2,1:T(8,128)(2,1)S(1)}, u32[]{:S(2)}, u32[]{:S(2)}) collective-permute-start(bf16[128,1,4,128]{3,0,2,1:T(8,128)(2,1)} %pad_maximum_fusion.11), channel_id=1, source_target_pairs={{0,4},{4,0},{1,5},{5,1},{2,6},{6,2},{3,7},{7,3},{8,12},{12,8},{9,1... | collective-permute-start | bytes 393224 | tf_op jit(solution)/shard_map/ppermute | solution.py:59
  17.6 113.1 %collective-permute-start.23 = (bf16[448,1024]{1,0:T(8,128)(2,1)}, bf16[448,1024]{1,0:T(8,128)(2,1)}, u32[]{:S(2)}, u32[]{:S(2)}) collective-permute-start(bf16[448,1024]{1,0:T(8,128)(2,1)} %param.22), channel_id=1, source_target_pairs={{0,1},{1,2},{2,3},{3,0},{4,5},{5,6},{6,7},{7,4},{8,9},{9,10},{10,1... | collective-permute-start | bytes 2752520 | tf_op jit(solution)/shard_map/ppermute | solution.py:22
  20.3 4.2 %copy-start.12 = (f32[64]{0:T(128)S(1)}, f32[64]{0:T(128)}, u32[]{:S(2)}) copy-start(f32[64]{0:T(128)} %copy-done.11) | copy-start | bytes 772
  30.9 7.9 %copy-start.13 = (f32[64]{0:T(128)S(1)}, f32[64]{0:T(128)}, u32[]{:S(2)}) copy-start(f32[64]{0:T(128)} %copy-done.11) | copy-start | bytes 772
  30.9 7.9 %copy-start.15 = (f32[128]{0:T(128)S(1)}, f32[128]{0:T(128)}, u32[]{:S(2)}) copy-start(f32[128]{0:T(128)} %copy-done.14) | copy-start | bytes 1540
  30.9 9.4 %collective-permute-start.1 = (bf16[2,128,1,4,128]{4,1,3,2,0:T(8,128)(2,1)}, bf16[2,128,1,4,128]{4,1,3,2,0:T(8,128)(2,1)}, u32[]{:S(2)}, u32[]{:S(2)}) collective-permute-start(bf16[2,128,1,4,128]{4,1,3,2,0:T(8,128)(2,1)} %maximum_select_fusion.1), channel_id=1, source_target_pairs={{0,8},{8,0},{16,24},{24,16},{1,9},{9,1},{17,25},{25,17},{2,10},{10... | collective-permute-start | bytes 786440 | tf_op jit(solution)/shard_map/ppermute | solution.py:59
  35.2 6.5 %copy-start.5 = (bf16[2048,64]{1,0:T(8,128)(2,1)S(1)}, bf16[2048,64]{1,0:T(8,128)(2,1)}, u32[]{:S(2)}) copy-start(bf16[2048,64]{1,0:T(8,128)(2,1)} %get-tuple-element.40) | copy-start | bytes 786436
  67.7 3.9 %copy-start.17 = (s32[128]{0:T(128)S(1)}, s32[128]{0:T(128)}, u32[]{:S(2)}) copy-start(s32[128]{0:T(128)} %copy-done.16) | copy-start | bytes 1540
  67.8 1.0 copy-start.2
  69.8 13.9 %collective-permute-start.2 = (f32[1,4,2,128,130]{3,1,4,2,0:T(4,128)}, f32[1,4,2,128,130]{3,1,4,2,0:T(4,128)}, u32[]{:S(2)}, u32[]{:S(2)}) collective-permute-start(f32[1,4,2,128,130]{3,1,4,2,0:T(4,128)} %copy.88), channel_id=1, source_target_pairs={{0,8},{8,0},{16,24},{24,16},{1,9},{9,1},{17,25},{25,17},{2,10},{10... | collective-permute-start | bytes 1597448 | tf_op jit(solution)/shard_map/ppermute | solution.py:59
  72.1 15.6 %copy-start.3 = (bf16[128,4096]{1,0:T(8,128)(2,1)S(1)}, bf16[128,4096]{1,0:T(8,128)(2,1)}, u32[]{:S(2)}) copy-start(bf16[128,4096]{1,0:T(8,128)(2,1)} %param.13) | copy-start | bytes 3145732
  72.1 15.6 %copy-start.18 = (bf16[4096,128]{1,0:T(8,128)(2,1)S(1)}, bf16[4096,128]{1,0:T(8,128)(2,1)}, u32[]{:S(2)}) copy-start(bf16[4096,128]{1,0:T(8,128)(2,1)} %param.17) | copy-start | bytes 3145732
  72.1 15.6 %copy-start.21 = (f32[128]{0:T(128)S(1)}, f32[128]{0:T(128)}, u32[]{:S(2)}) copy-start(f32[128]{0:T(128)} %copy-done.20) | copy-start | bytes 1540
  87.5 6.7 %collective-permute-start.3 = (f32[1,4,1,128,130]{3,4,2,1,0:T(8,128)S(1)}, f32[1,4,1,128,130]{3,4,2,1,0:T(8,128)S(1)}, u32[]{:S(2)}, u32[]{:S(2)}) collective-permute-start(f32[1,4,1,128,130]{3,4,2,1,0:T(8,128)S(1)} %constant_dynamic-slice_fusion.5), channel_id=1, source_target_pairs={{0,4},{4,0},{1,5},{5,1},{2,6},{6,2},{3,7},{7,3},{8,12},{12,8},{9,1... | collective-permute-start | bytes 798728 | tf_op jit(solution)/shard_map/ppermute | solution.py:59
  89.6 24.0 %collective-permute-start.20 = (bf16[512,896]{1,0:T(8,128)(2,1)S(1)}, bf16[512,896]{1,0:T(8,128)(2,1)S(1)}, u32[]{:S(2)}, u32[]{:S(2)}) collective-permute-start(bf16[512,896]{1,0:T(8,128)(2,1)S(1)} %slice.229), channel_id=1, source_target_pairs={{0,1},{1,2},{2,3},{3,0},{4,5},{5,6},{6,7},{7,4},{8,9},{9,10},{10,1... | collective-permute-start | bytes 2752520 | tf_op jit(solution)/shard_map/ppermute | solution.py:169
  92.5 22.5 %collective-permute-start.22 = (bf16[512,896]{1,0:T(8,128)(2,1)S(1)}, bf16[512,896]{1,0:T(8,128)(2,1)S(1)}, u32[]{:S(2)}, u32[]{:S(2)}) collective-permute-start(bf16[512,896]{1,0:T(8,128)(2,1)S(1)} %slice.230), channel_id=1, source_target_pairs={{0,3},{1,0},{2,1},{3,2},{4,7},{5,4},{6,5},{7,6},{8,11},{9,8},{10,9... | collective-permute-start | bytes 2752520 | tf_op jit(solution)/shard_map/ppermute | solution.py:174
  115.2 6.2 %copy-start.4 = (bf16[512,4096]{1,0:T(8,128)(2,1)S(1)}, bf16[512,4096]{1,0:T(8,128)(2,1)}, u32[]{:S(2)}) copy-start(bf16[512,4096]{1,0:T(8,128)(2,1)} %param.18) | copy-start | bytes 12582916
  121.4 127.8 %collective-permute-start.27 = (bf16[4,1024,896]{2,1,0:T(8,128)(2,1)}, bf16[4,1024,896]{2,1,0:T(8,128)(2,1)}, u32[]{:S(2)}, u32[]{:S(2)}) collective-permute-start(bf16[4,1024,896]{2,1,0:T(8,128)(2,1)} %pad_maximum_fusion), channel_id=1, source_target_pairs={{0,4},{4,0},{1,5},{5,1},{2,6},{6,2},{3,7},{7,3},{8,12},{12,8},{9,1... | collective-permute-start | bytes 22020104 | tf_op jit(solution)/shard_map/ppermute | solution.py:59
  122.1 8.4 %copy-start.10 = (bf16[4096]{0:T(1024)(128)(2,1)S(1)}, bf16[4096]{0:T(1024)(128)(2,1)}, u32[]{:S(2)}) copy-start(bf16[4096]{0:T(1024)(128)(2,1)} %param.19) | copy-start | bytes 24580
  123.3 16.0 %collective-permute-start.4 = (f32[32,4096]{1,0:T(8,128)}, f32[32,4096]{1,0:T(8,128)}, u32[]{:S(2)}, u32[]{:S(2)}) collective-permute-start(f32[32,4096]{1,0:T(8,128)} %get-tuple-element.37), channel_id=1, source_target_pairs={{0,1},{1,2},{2,3},{3,0},{4,5},{5,6},{6,7},{7,4},{8,9},{9,10},{10,1... | collective-permute-start | bytes 1572872 | tf_op jit(solution)/shard_map/ppermute | solution.py:22
  124.8 27.5 %collective-permute-start.5 = (f32[32,4096]{1,0:T(8,128)}, f32[32,4096]{1,0:T(8,128)}, u32[]{:S(2)}, u32[]{:S(2)}) collective-permute-start(f32[32,4096]{1,0:T(8,128)} %get-tuple-element.39), channel_id=1, source_target_pairs={{0,2},{1,3},{2,0},{3,1},{4,6},{5,7},{6,4},{7,5},{8,10},{9,11},{10,... | collective-permute-start | bytes 1572872 | tf_op jit(solution)/shard_map/ppermute | solution.py:22
  127.8 24.4 %collective-permute-start.6 = (f32[32,4096]{1,0:T(8,128)}, f32[32,4096]{1,0:T(8,128)}, u32[]{:S(2)}, u32[]{:S(2)}) collective-permute-start(f32[32,4096]{1,0:T(8,128)} %get-tuple-element.38), channel_id=1, source_target_pairs={{0,3},{1,0},{2,1},{3,2},{4,7},{5,4},{6,5},{7,6},{8,11},{9,8},{10,9... | collective-permute-start | bytes 1572872 | tf_op jit(solution)/shard_map/ppermute | solution.py:22
  130.7 40.1 %collective-permute-start.25 = (bf16[448,1024]{1,0:T(8,128)(2,1)}, bf16[448,1024]{1,0:T(8,128)(2,1)S(1)}, u32[]{:S(2)}, u32[]{:S(2)}) collective-permute-start(bf16[448,1024]{1,0:T(8,128)(2,1)} %param.22), channel_id=1, source_target_pairs={{0,3},{1,0},{2,1},{3,2},{4,7},{5,4},{6,5},{7,6},{8,11},{9,8},{10,9... | collective-permute-start | bytes 2752520 | tf_op jit(solution)/shard_map/ppermute | solution.py:22
  139.3 40.6 %collective-permute-start.24 = (bf16[224,1024]{1,0:T(8,128)(2,1)S(1)}, bf16[224,1024]{1,0:T(8,128)(2,1)}, u32[]{:S(2)}, u32[]{:S(2)}) collective-permute-start(bf16[224,1024]{1,0:T(8,128)(2,1)S(1)} %slice.233), channel_id=1, source_target_pairs={{0,1},{1,2},{2,3},{3,0},{4,5},{5,6},{6,7},{7,4},{8,9},{9,10},{10,1... | collective-permute-start | bytes 1376264 | tf_op jit(solution)/shard_map/ppermute | solution.py:169
  154.8 18.7 %collective-permute-start.13 = (bf16[32,2048]{1,0:T(8,128)(2,1)S(1)}, bf16[32,2048]{1,0:T(8,128)(2,1)S(1)}, u32[]{:S(2)}, u32[]{:S(2)}) collective-permute-start(bf16[32,2048]{1,0:T(8,128)(2,1)S(1)} %get-tuple-element.60), channel_id=1, source_target_pairs={{0,32},{32,64},{64,96},{96,0},{1,33},{33,65},{65,97},{97,1},{2,34}... | collective-permute-start | bytes 393224 | tf_op jit(solution)/shard_map/ppermute | solution.py:22
  156.3 20.0 %collective-permute-start.14 = (bf16[32,2048]{1,0:T(8,128)(2,1)S(1)}, bf16[32,2048]{1,0:T(8,128)(2,1)S(1)}, u32[]{:S(2)}, u32[]{:S(2)}) collective-permute-start(bf16[32,2048]{1,0:T(8,128)(2,1)S(1)} %get-tuple-element.60), channel_id=1, source_target_pairs={{0,64},{32,96},{64,0},{96,32},{1,65},{33,97},{65,1},{97,33},{2,66}... | collective-permute-start | bytes 393224 | tf_op jit(solution)/shard_map/ppermute | solution.py:22
  170.8 18.7 %copy-start.6 = (bf16[448,1024]{1,0:T(8,128)(2,1)}, bf16[448,1024]{1,0:T(8,128)(2,1)S(1)}, u32[]{:S(2)}) copy-start(bf16[448,1024]{1,0:T(8,128)(2,1)S(1)} %collective-permute-done.25) | copy-start | bytes 2752516
  170.8 7.0 %collective-permute-start.15 = (bf16[32,2048]{1,0:T(8,128)(2,1)S(1)}, bf16[32,2048]{1,0:T(8,128)(2,1)S(1)}, u32[]{:S(2)}, u32[]{:S(2)}) collective-permute-start(bf16[32,2048]{1,0:T(8,128)(2,1)S(1)} %get-tuple-element.60), channel_id=1, source_target_pairs={{0,96},{32,0},{64,32},{96,64},{1,97},{33,1},{65,33},{97,65},{2,98}... | collective-permute-start | bytes 393224 | tf_op jit(solution)/shard_map/ppermute | solution.py:22
  173.6 12.4 %collective-permute-start.26 = (bf16[224,1024]{1,0:T(8,128)(2,1)S(1)}, bf16[224,1024]{1,0:T(8,128)(2,1)S(1)}, u32[]{:S(2)}, u32[]{:S(2)}) collective-permute-start(bf16[224,1024]{1,0:T(8,128)(2,1)S(1)} %slice.234), channel_id=1, source_target_pairs={{0,3},{1,0},{2,1},{3,2},{4,7},{5,4},{6,5},{7,6},{8,11},{9,8},{10,9... | collective-permute-start | bytes 1376264 | tf_op jit(solution)/shard_map/ppermute | solution.py:174
  176.3 13.2 %collective-permute-start.7 = (bf16[32,2048]{1,0:T(8,128)(2,1)}, bf16[32,2048]{1,0:T(8,128)(2,1)}, u32[]{:S(2)}, u32[]{:S(2)}) collective-permute-start(bf16[32,2048]{1,0:T(8,128)(2,1)} %get-tuple-element.61), channel_id=1, source_target_pairs={{0,8},{8,16},{16,24},{24,0},{1,9},{9,17},{17,25},{25,1},{2,10},{10... | collective-permute-start | bytes 393224 | tf_op jit(solution)/shard_map/ppermute | solution.py:22
  177.9 32.9 %collective-permute-start.16 = (bf16[4,32,2048]{2,1,0:T(8,128)(2,1)S(1)}, bf16[4,32,2048]{2,1,0:T(8,128)(2,1)}, u32[]{:S(2)}, u32[]{:S(2)}) collective-permute-start(bf16[4,32,2048]{2,1,0:T(8,128)(2,1)S(1)} %get-tuple-element.55), channel_id=1, source_target_pairs={{0,8},{8,16},{16,24},{24,0},{1,9},{9,17},{17,25},{25,1},{2,10},{10... | collective-permute-start | bytes 1572872 | tf_op jit(solution)/shard_map/ppermute | solution.py:22
  179.9 33.2 %collective-permute-start.17 = (bf16[4,32,2048]{2,1,0:T(8,128)(2,1)S(1)}, bf16[4,32,2048]{2,1,0:T(8,128)(2,1)}, u32[]{:S(2)}, u32[]{:S(2)}) collective-permute-start(bf16[4,32,2048]{2,1,0:T(8,128)(2,1)S(1)} %get-tuple-element.55), channel_id=1, source_target_pairs={{0,16},{8,24},{16,0},{24,8},{1,17},{9,25},{17,1},{25,9},{2,18},{10... | collective-permute-start | bytes 1572872 | tf_op jit(solution)/shard_map/ppermute | solution.py:22
  186.0 3.5 %copy-start.8 = (bf16[224,1024]{1,0:T(8,128)(2,1)}, bf16[224,1024]{1,0:T(8,128)(2,1)S(1)}, u32[]{:S(2)}) copy-start(bf16[224,1024]{1,0:T(8,128)(2,1)S(1)} %collective-permute-done.26) | copy-start | bytes 1376260
  186.0 23.8 %collective-permute-start.8 = (bf16[32,2048]{1,0:T(8,128)(2,1)}, bf16[32,2048]{1,0:T(8,128)(2,1)S(1)}, u32[]{:S(2)}, u32[]{:S(2)}) collective-permute-start(bf16[32,2048]{1,0:T(8,128)(2,1)} %get-tuple-element.61), channel_id=1, source_target_pairs={{0,16},{8,24},{16,0},{24,8},{1,17},{9,25},{17,1},{25,9},{2,18},{10... | collective-permute-start | bytes 393224 | tf_op jit(solution)/shard_map/ppermute | solution.py:22
  189.5 20.3 %collective-permute-start.9 = (bf16[32,2048]{1,0:T(8,128)(2,1)}, bf16[32,2048]{1,0:T(8,128)(2,1)S(1)}, u32[]{:S(2)}, u32[]{:S(2)}) collective-permute-start(bf16[32,2048]{1,0:T(8,128)(2,1)} %get-tuple-element.61), channel_id=1, source_target_pairs={{0,24},{8,0},{16,8},{24,16},{1,25},{9,1},{17,9},{25,17},{2,26},{10... | collective-permute-start | bytes 393224 | tf_op jit(solution)/shard_map/ppermute | solution.py:22
  190.4 23.9 %copy-start.7 = (bf16[448,1024]{1,0:T(8,128)(2,1)S(1)}, bf16[448,1024]{1,0:T(8,128)(2,1)}, u32[]{:S(2)}) copy-start(bf16[448,1024]{1,0:T(8,128)(2,1)} %copy-done.6) | copy-start | bytes 2752516
  209.7 12.5 %collective-permute-start.18 = (bf16[4,32,2048]{2,1,0:T(8,128)(2,1)S(1)}, bf16[4,32,2048]{2,1,0:T(8,128)(2,1)S(1)}, u32[]{:S(2)}, u32[]{:S(2)}) collective-permute-start(bf16[4,32,2048]{2,1,0:T(8,128)(2,1)S(1)} %get-tuple-element.55), channel_id=1, source_target_pairs={{0,24},{8,0},{16,8},{24,16},{1,25},{9,1},{17,9},{25,17},{2,26},{10... | collective-permute-start | bytes 1572872 | tf_op jit(solution)/shard_map/ppermute | solution.py:22
  210.7 25.1 %collective-permute-start.10 = (bf16[4,32,2048]{2,1,0:T(8,128)(2,1)S(1)}, bf16[4,32,2048]{2,1,0:T(8,128)(2,1)S(1)}, u32[]{:S(2)}, u32[]{:S(2)}) collective-permute-start(bf16[4,32,2048]{2,1,0:T(8,128)(2,1)S(1)} %get-tuple-element.57), channel_id=1, source_target_pairs={{0,32},{32,64},{64,96},{96,0},{1,33},{33,65},{65,97},{97,1},{2,34}... | collective-permute-start | bytes 1572872 | tf_op jit(solution)/shard_map/ppermute | solution.py:22
  210.8 25.0 %collective-permute-start.11 = (bf16[4,32,2048]{2,1,0:T(8,128)(2,1)S(1)}, bf16[4,32,2048]{2,1,0:T(8,128)(2,1)S(1)}, u32[]{:S(2)}, u32[]{:S(2)}) collective-permute-start(bf16[4,32,2048]{2,1,0:T(8,128)(2,1)S(1)} %get-tuple-element.57), channel_id=1, source_target_pairs={{0,64},{32,96},{64,0},{96,32},{1,65},{33,97},{65,1},{97,33},{2,66}... | collective-permute-start | bytes 1572872 | tf_op jit(solution)/shard_map/ppermute | solution.py:22
  213.1 23.3 %collective-permute-start.12 = (bf16[4,32,2048]{2,1,0:T(8,128)(2,1)S(1)}, bf16[4,32,2048]{2,1,0:T(8,128)(2,1)S(1)}, u32[]{:S(2)}, u32[]{:S(2)}) collective-permute-start(bf16[4,32,2048]{2,1,0:T(8,128)(2,1)S(1)} %get-tuple-element.57), channel_id=1, source_target_pairs={{0,96},{32,0},{64,32},{96,64},{1,97},{33,1},{65,33},{97,65},{2,98}... | collective-permute-start | bytes 1572872 | tf_op jit(solution)/shard_map/ppermute | solution.py:22
  222.3 34.5 %collective-permute-start.28 = (bf16[448,4096]{1,0:T(8,128)(2,1)S(1)}, bf16[448,4096]{1,0:T(8,128)(2,1)S(1)}, u32[]{:S(2)}, u32[]{:S(2)}) collective-permute-start(bf16[448,4096]{1,0:T(8,128)(2,1)S(1)} %bitcast.223), channel_id=1, source_target_pairs={{0,4},{4,0},{1,5},{5,1},{2,6},{6,2},{3,7},{7,3},{8,12},{12,8},{9,1... | collective-permute-start | bytes 11010056 | tf_op jit(solution)/shard_map/ppermute | solution.py:59
  259.4 24.9 %collective-permute-start.29 = (bf16[4,32,2048]{2,1,0:T(8,128)(2,1)S(1)}, bf16[4,32,2048]{2,1,0:T(8,128)(2,1)S(1)}, u32[]{:S(2)}, u32[]{:S(2)}) collective-permute-start(bf16[4,32,2048]{2,1,0:T(8,128)(2,1)S(1)} %get-tuple-element.27), channel_id=1, source_target_pairs={{0,96},{32,0},{64,32},{96,64},{1,97},{33,1},{65,33},{97,65},{2,98}... | collective-permute-start | bytes 1572872 | tf_op jit(solution)/shard_map/ppermute | solution.py:22
  261.9 24.1 %collective-permute-start.30 = (bf16[4,32,2048]{2,1,0:T(8,128)(2,1)S(1)}, bf16[4,32,2048]{2,1,0:T(8,128)(2,1)S(1)}, u32[]{:S(2)}, u32[]{:S(2)}) collective-permute-start(bf16[4,32,2048]{2,1,0:T(8,128)(2,1)S(1)} %get-tuple-element.29), channel_id=1, source_target_pairs={{0,64},{32,96},{64,0},{96,32},{1,65},{33,97},{65,1},{97,33},{2,66}... | collective-permute-start | bytes 1572872 | tf_op jit(solution)/shard_map/ppermute | solution.py:22
  261.9 26.0 %collective-permute-start.31 = (bf16[4,32,2048]{2,1,0:T(8,128)(2,1)S(1)}, bf16[4,32,2048]{2,1,0:T(8,128)(2,1)S(1)}, u32[]{:S(2)}, u32[]{:S(2)}) collective-permute-start(bf16[4,32,2048]{2,1,0:T(8,128)(2,1)S(1)} %get-tuple-element.28), channel_id=1, source_target_pairs={{0,32},{32,64},{64,96},{96,0},{1,33},{33,65},{65,97},{97,1},{2,34}... | collective-permute-start | bytes 1572872 | tf_op jit(solution)/shard_map/ppermute | solution.py:22
  263.3 28.8 %collective-permute-start.35 = (bf16[4,32,2048]{2,1,0:T(8,128)(2,1)S(1)}, bf16[4,32,2048]{2,1,0:T(8,128)(2,1)S(1)}, u32[]{:S(2)}, u32[]{:S(2)}) collective-permute-start(bf16[4,32,2048]{2,1,0:T(8,128)(2,1)S(1)} %get-tuple-element.34), channel_id=1, source_target_pairs={{0,24},{8,0},{16,8},{24,16},{1,25},{9,1},{17,9},{25,17},{2,26},{10... | collective-permute-start | bytes 1572872 | tf_op jit(solution)/shard_map/ppermute | solution.py:22
  263.9 28.3 %collective-permute-start.36 = (bf16[4,32,2048]{2,1,0:T(8,128)(2,1)S(1)}, bf16[4,32,2048]{2,1,0:T(8,128)(2,1)S(1)}, u32[]{:S(2)}, u32[]{:S(2)}) collective-permute-start(bf16[4,32,2048]{2,1,0:T(8,128)(2,1)S(1)} %get-tuple-element.36), channel_id=1, source_target_pairs={{0,16},{8,24},{16,0},{24,8},{1,17},{9,25},{17,1},{25,9},{2,18},{10... | collective-permute-start | bytes 1572872 | tf_op jit(solution)/shard_map/ppermute | solution.py:22
  284.3 18.0 %collective-permute-start.37 = (bf16[4,32,2048]{2,1,0:T(8,128)(2,1)S(1)}, bf16[4,32,2048]{2,1,0:T(8,128)(2,1)S(1)}, u32[]{:S(2)}, u32[]{:S(2)}) collective-permute-start(bf16[4,32,2048]{2,1,0:T(8,128)(2,1)S(1)} %get-tuple-element.35), channel_id=1, source_target_pairs={{0,8},{8,16},{16,24},{24,0},{1,9},{9,17},{17,25},{25,1},{2,10},{10... | collective-permute-start | bytes 1572872 | tf_op jit(solution)/shard_map/ppermute | solution.py:22
  288.3 18.3 %collective-permute-start.32 = (bf16[32,2048]{1,0:T(8,128)(2,1)S(1)}, bf16[32,2048]{1,0:T(8,128)(2,1)S(1)}, u32[]{:S(2)}, u32[]{:S(2)}) collective-permute-start(bf16[32,2048]{1,0:T(8,128)(2,1)S(1)} %get-tuple-element.48), channel_id=1, source_target_pairs={{0,24},{8,0},{16,8},{24,16},{1,25},{9,1},{17,9},{25,17},{2,26},{10... | collective-permute-start | bytes 393224 | tf_op jit(solution)/shard_map/ppermute | solution.py:22
  288.9 18.7 %collective-permute-start.33 = (bf16[32,2048]{1,0:T(8,128)(2,1)S(1)}, bf16[32,2048]{1,0:T(8,128)(2,1)S(1)}, u32[]{:S(2)}, u32[]{:S(2)}) collective-permute-start(bf16[32,2048]{1,0:T(8,128)(2,1)S(1)} %get-tuple-element.50), channel_id=1, source_target_pairs={{0,16},{8,24},{16,0},{24,8},{1,17},{9,25},{17,1},{25,9},{2,18},{10... | collective-permute-start | bytes 393224 | tf_op jit(solution)/shard_map/ppermute | solution.py:22
  292.2 15.4 %collective-permute-start.34 = (bf16[32,2048]{1,0:T(8,128)(2,1)S(1)}, bf16[32,2048]{1,0:T(8,128)(2,1)S(1)}, u32[]{:S(2)}, u32[]{:S(2)}) collective-permute-start(bf16[32,2048]{1,0:T(8,128)(2,1)S(1)} %get-tuple-element.49), channel_id=1, source_target_pairs={{0,8},{8,16},{16,24},{24,0},{1,9},{9,17},{17,25},{25,1},{2,10},{10... | collective-permute-start | bytes 393224 | tf_op jit(solution)/shard_map/ppermute | solution.py:22
  302.7 7.8 %collective-permute-start.38 = (bf16[32,2048]{1,0:T(8,128)(2,1)S(1)}, bf16[32,2048]{1,0:T(8,128)(2,1)S(1)}, u32[]{:S(2)}, u32[]{:S(2)}) collective-permute-start(bf16[32,2048]{1,0:T(8,128)(2,1)S(1)} %get-tuple-element.51), channel_id=1, source_target_pairs={{0,96},{32,0},{64,32},{96,64},{1,97},{33,1},{65,33},{97,65},{2,98}... | collective-permute-start | bytes 393224 | tf_op jit(solution)/shard_map/ppermute | solution.py:22
  306.6 6.6 %collective-permute-start.39 = (bf16[32,2048]{1,0:T(8,128)(2,1)S(1)}, bf16[32,2048]{1,0:T(8,128)(2,1)S(1)}, u32[]{:S(2)}, u32[]{:S(2)}) collective-permute-start(bf16[32,2048]{1,0:T(8,128)(2,1)S(1)} %get-tuple-element.53), channel_id=1, source_target_pairs={{0,64},{32,96},{64,0},{96,32},{1,65},{33,97},{65,1},{97,33},{2,66}... | collective-permute-start | bytes 393224 | tf_op jit(solution)/shard_map/ppermute | solution.py:22
  306.6 7.6 %collective-permute-start.40 = (bf16[32,2048]{1,0:T(8,128)(2,1)S(1)}, bf16[32,2048]{1,0:T(8,128)(2,1)S(1)}, u32[]{:S(2)}, u32[]{:S(2)}) collective-permute-start(bf16[32,2048]{1,0:T(8,128)(2,1)S(1)} %get-tuple-element.52), channel_id=1, source_target_pairs={{0,32},{32,64},{64,96},{96,0},{1,33},{33,65},{65,97},{97,1},{2,34}... | collective-permute-start | bytes 393224 | tf_op jit(solution)/shard_map/ppermute | solution.py:22
  314.2 12.4 %copy-start.1 = (bf16[4096,128]{1,0:T(8,128)(2,1)S(1)}, bf16[4096,128]{1,0:T(8,128)(2,1)}, u32[]{:S(2)}) copy-start(bf16[4096,128]{1,0:T(8,128)(2,1)} %param.16) | copy-start | bytes 3145732
  315.8 10.1 %all-to-all-start = ((bf16[32,4,1024]{2,0,1:T(8,128)(2,1)}), bf16[32,4,1024]{2,0,1:T(8,128)(2,1)S(1)}, u32[]{:S(2)}, u32[]{:S(2)}) async-start(bf16[32,4,1024]{2,0,1:T(8,128)(2,1)} %bitcast.215), calls=%async_computation | async-start | bytes 524288 | tf_op jit(solution)/shard_map/all_to_all | solution.py:304

commit v8 on v6

--- a/solution.py
+++ b/solution.py
@@ -260,7 +260,8 @@
     for shift in range(1, n_mlp):
         target = (mlp_index + shift) % n_mlp
         outgoing = lax.dynamic_slice_in_dim(head_terms, target * rows_here, rows_here, 0)
-        head_rows = head_rows + shifted(outgoing, "mlp", n_mlp, shift)
+        incoming = shifted(outgoing.astype(jnp.bfloat16), "mlp", n_mlp, shift)
+        head_rows = head_rows + incoming.astype(jnp.float32)
     row_start = mlp_index * rows_here
     hidden_rows = lax.dynamic_slice_in_dim(hidden_f, row_start, rows_here, 0)
     live_rows = lax.dynamic_slice_in_dim(live, row_start, rows_here, 0)
@@ -296,7 +297,14 @@
     out_rows = jnp.where(
         live_rows[:, None], residual.astype(jnp.float32) + down, 0.0
     ).astype(jnp.bfloat16)
-    hidden_out = lax.all_to_all(out_rows, "mlp", 1, 0, tiled=True)
+    arrived = [lax.dynamic_slice_in_dim(out_rows, mlp_index * width_part, width_part, 1)]
+    for shift in range(1, n_mlp):
+        target = (mlp_index + shift) % n_mlp
+        outgoing = lax.dynamic_slice_in_dim(out_rows, target * width_part, width_part, 1)
+        arrived.append(shifted(outgoing, "mlp", n_mlp, shift))
+    arrived = jnp.stack(arrived)
+    shift_of = jnp.stack([(mlp_index - j) % n_mlp for j in range(n_mlp)])
+    hidden_out = jnp.take(arrived, shift_of, axis=0).reshape(slots_here, width_part)
 
     stacked_kv = jnp.stack(
         [

time: 333 us -> 318 us (0.955)
  waiting for transfers between devices: 146 us -> 133 us
    ppermute x27 -> x30, waiting for transfers between devices: 91.9 us -> 83.5 us  [shifted(): lax.ppermute(value, axis, [(i, (i + shift) % size) for i in range(size)])]
    all_to_all x1 -> x0, waiting for transfers between devices: 5.86 us -> none  [layer(): hidden_out = lax.all_to_all(out_rows, 'mlp', 1, 0, tiled=True)]
    all_to_all x1 -> x0, starting transfers between devices: 3.41 us -> none  [layer(): hidden_out = lax.all_to_all(out_rows, 'mlp', 1, 0, tiled=True)]
    ppermute x27 -> x30, starting transfers between devices: 43.8 us -> 47.1 us  [shifted(): lax.ppermute(value, axis, [(i, (i + shift) % size) for i in range(size)])]
    unnamed x51 -> x46, local copies, waits for them, and re-layouts: 9.78 us -> 7.9 us
  transfers between devices with their start and end apart: 42 -> 44, of which waited for: 19 -> 20; matrix products, arithmetic and copies ran while one was open for 32% -> 33% of each run, Pallas kernels for 0% -> 0%
where the time goes in v8:
time: 318 us; the launch traced here: 312 us
  waiting for transfers between devices  133 us (42%)
  starting transfers between devices  61.7 us (19%)
  other arithmetic  47.5 us (15%)
  matrix products  44.6 us (14%)
  local copies, waits for them, and re-layouts  23.8 us (7%)
    ppermute x30, waiting for transfers between devices, shifted(): lax.ppermute(value, axis, [(i, (i + shift) % size) for i in range(size)])  83.5 us
    ppermute x30, starting transfers between devices, shifted(): lax.ppermute(value, axis, [(i, (i + shift) % size) for i in range(size)])  47.1 us
    ppermute x2, waiting for transfers between devices, layer(): lax.ppermute((from_left[0][:half_gu], from_left[1][:half_wd]), 'mlp', [(i...  19.2 us
    dot_general x2, matrix products, layer(): jnp.dot(tokens_ring, weights_here, preferred_element_type=jnp.float32)  15.2 us
    ppermute x6, waiting for transfers between devices, swap_with_partner(): lax.ppermute(value, axis, [(source, source ^ 1) for source in range(size)])  12.3 us
    ppermute x2, waiting for transfers between devices, layer(): lax.ppermute(own, 'mlp', [(i, (i - 1) % n_mlp) for i in range(n_mlp)])  12 us
    convert_element_type x1, other arithmetic, partial_attention(): weights.astype(jnp.bfloat16)  10.3 us
    dot_general x2, matrix products, partial_attention(): jnp.einsum('qkgd,nkd->kgqn', grouped_queries, key_block, preferred_elemen...  9.69 us
  transfers between devices with their start and end apart: 44, of which 20 were waited for; matrix products, arithmetic and copies ran while one was open for 33% of the time, Pallas kernels for 0%

profile of v8, /device:TPU:0, one launch (start us, length us, event | category | flops | bytes accessed | tf_op | source)
XLA Modules:
  0.0 312.5 jit_solution(16673783746416852564)
XLA Ops:
  0.7 1.5 copy.92
  2.2 1.5 copy.93
  3.7 1.8 pad_maximum_fusion.3
  5.5 1.7 collective-permute-start.19
  7.2 1.5 collective-permute-start.21
  9.2 1.5 multiply_reduce_fusion
  11.3 4.0 %fusion.91 = f32[128,512]{1,0:T(8,128)} fusion(bf16[4096,512]{1,0:T(8,128)(2,1)} %param.15, f32[4096]{0:T(1024)S(1)} %convert_element_type.215, f32[128]{0:T(128)S(1)} %add_rsqrt_fusion.1, bf16[128,4096]{1,0:T(8,128)(2,1)} %param.13), kind=kOutput, calls=%fused_computation.222 | convolution fusion | flops 538968064 | bytes 5521920 | tf_op jit(solution)/shard_map/dot_general | solution.py:191
  20.3 4.1 %fusion.94 = (bf16[2048,1,128]{2,1,0:T(2,128)(2,1)}, bf16[2048,1,128]{2,1,0:T(2,128)(2,1)S(1)}) fusion(bf16[2048,2,128]{2,1,0:T(2,128)(2,1)} %param.23), kind=kLoop, calls=%fused_computation.223 | loop fusion | bytes 2097152 | tf_op jit(solution)/shard_map/slice | solution.py:217
  24.5 5.6 %fusion.46 = (bf16[2048,64]{1,0:T(8,128)(2,1)}, bf16[2048,64]{1,0:T(8,128)(2,1)}) fusion(f32[2048,1,128]{2,0,1:T(8,128)S(1)} %copy_convert_fusion, f32[64]{0:T(128)S(1)} %copy-done.11, f32[2048]{0:T(1024)S(1)} %add_convert_fusion.3), kind=kLoop, calls=%fused_computation.107 | loop fusion | flops 1179648 | bytes 1581312 | tf_op jit(solution)/shard_map/concatenate | solution.py:70
  30.9 2.1 collective-permute-start.1
  33.0 1.8 convolution_bitcast_fusion.1
  34.9 2.3 copy.107
  37.5 2.6 collective-permute-done.1
  40.0 1.3 maximum_select_fusion
  41.4 9.4 %bitcast_reduce_fusion = (f32[4,512]{1,0:T(4,128)S(1)}, f32[2048,512,4]{0,1,2:T(8,128)}) fusion(bf16[512,4,128]{2,0,1:T(8,128)(2,1)S(1)} %bitcast.225, bf16[2048,64]{1,0:T(8,128)(2,1)} %get-tuple-element.41, bf16[2048,64]{1,0:T(8,128)(2,1)} %get-tuple-element.40), kind=kOutput, calls=%fused_computation.3 | convolution fusion | flops 1083176960 | bytes 17833984 | tf_op jit(solution)/shard_map/qkgd,nkd->kgqn/dot_general | solution.py:97
  50.8 10.3 %fusion.2 = (bf16[1,4,512,2048]{3,2,1,0:T(8,128)(2,1)}, f32[4,512]{1,0:T(4,128)S(1)}) fusion(f32[2048,512,4]{0,1,2:T(8,128)} %get-tuple-element.73, f32[4,512]{1,0:T(4,128)S(1)} %get-tuple-element.72), kind=kLoop, calls=%fused_computation.6 | loop fusion | flops 16775168 | bytes 25182208 | tf_op jit(solution)/shard_map/convert_element_type | solution.py:107
  61.1 6.3 %convolution_bitcast_fusion = f32[1,4,4,128,128]{3,4,2,1,0:T(8,128)S(1)} fusion(bf16[4,4,128,2048]{3,2,1,0:T(8,128)(2,1)} %bitcast.217, bf16[2048,1,128]{0,2,1:T(8,128)(2,1)S(1)} %copy.107), kind=kOutput, calls=%fused_computation.34 | convolution fusion | flops 1073741824 | bytes 9961472 | tf_op jit(solution)/shard_map/kgqn,nkd->kgqd/dot_general | solution.py:105
  69.6 1.7 collective-permute-start.2
  71.8 1.8 convolution_convert_fusion.2
  73.7 9.8 %collective-permute-done.2 = f32[1,4,2,128,130]{3,1,4,2,0:T(4,128)} collective-permute-done((f32[1,4,2,128,130]{3,1,4,2,0:T(4,128)}, f32[1,4,2,128,130]{3,1,4,2,0:T(4,128)}, u32[]{:S(2)}, u32[]{:S(2)}) %collective-permute-start.2) | collective-permute-done | bytes 532512 | tf_op jit(solution)/shard_map/ppermute | solution.py:59
  89.2 1.6 collective-permute-start.20
  92.2 1.7 collective-permute-start.22
  94.1 19.2 %collective-permute-done.20 = bf16[512,896]{1,0:T(8,128)(2,1)S(1)} collective-permute-done((bf16[512,896]{1,0:T(8,128)(2,1)S(1)}, bf16[512,896]{1,0:T(8,128)(2,1)S(1)}, u32[]{:S(2)}, u32[]{:S(2)}) %collective-permute-start.20) | collective-permute-done | bytes 917536 | tf_op jit(solution)/shard_map/ppermute | solution.py:165
  113.3 1.4 collective-permute-done.22
  114.9 6.2 %pad_maximum_fusion = bf16[4,1024,896]{2,1,0:T(8,128)(2,1)} fusion(bf16[1,1024,896]{2,1,0:T(8,128)(2,1)} %bitcast.69, bf16[1,1024,896]{2,1,0:T(8,128)(2,1)S(1)} %maximum_bitcast_fusion.2, bf16[1,1024,896]{2,1,0:T(8,128)(2,1)} %bitcast.67, bf16[1,1024,896]{2,1,0:T(8,128)(2,1)S(1)} %fusion.110), kind=kLoop, calls=%fused_computation.8 | loop fusion | flops 11010048 | bytes 14680064 | tf_op jit(solution)/shard_map/stack | solution.py:179
  123.0 1.5 collective-permute-start.4
  124.4 3.1 collective-permute-start.5
  128.7 1.5 convert_element_type.212
  131.4 2.0 collective-permute-done.4
  133.9 6.7 %collective-permute-done.5 = bf16[32,4096]{1,0:T(8,128)(2,1)} collective-permute-done((bf16[32,4096]{1,0:T(8,128)(2,1)}, bf16[32,4096]{1,0:T(8,128)(2,1)}, u32[]{:S(2)}, u32[]{:S(2)}) %collective-permute-start.5) | collective-permute-done | bytes 262176 | tf_op jit(solution)/shard_map/ppermute | solution.py:22
  140.6 1.6 fusion.31
  143.1 1.5 collective-permute-start.13
  144.5 2.7 collective-permute-start.14
  147.3 12.0 %collective-permute-done.25 = bf16[448,1024]{1,0:T(8,128)(2,1)S(1)} collective-permute-done((bf16[448,1024]{1,0:T(8,128)(2,1)}, bf16[448,1024]{1,0:T(8,128)(2,1)S(1)}, u32[]{:S(2)}, u32[]{:S(2)}) %collective-permute-start.25) | collective-permute-done | bytes 917536 | tf_op jit(solution)/shard_map/ppermute | solution.py:162
  159.2 2.7 collective-permute-start.15
  162.0 2.7 collective-permute-start.26
  164.7 1.6 collective-permute-start.7
  166.4 2.0 collective-permute-start.16
  168.4 1.8 collective-permute-start.17
  170.3 4.1 %collective-permute-done.26 = bf16[224,1024]{1,0:T(8,128)(2,1)S(1)} collective-permute-done((bf16[224,1024]{1,0:T(8,128)(2,1)S(1)}, bf16[224,1024]{1,0:T(8,128)(2,1)S(1)}, u32[]{:S(2)}, u32[]{:S(2)}) %collective-permute-start.26) | collective-permute-done | bytes 458784 | tf_op jit(solution)/shard_map/ppermute | solution.py:170
  174.4 3.5 %collective-permute-start.8 = (bf16[32,2048]{1,0:T(8,128)(2,1)}, bf16[32,2048]{1,0:T(8,128)(2,1)S(1)}, u32[]{:S(2)}, u32[]{:S(2)}) collective-permute-start(bf16[32,2048]{1,0:T(8,128)(2,1)} %get-tuple-element.65), channel_id=1, source_target_pairs={{0,16},{8,24},{16,0},{24,8},{1,17},{9,25},{17,1},{25,9},{2,18},{10... | collective-permute-start | bytes 393224 | tf_op jit(solution)/shard_map/ppermute | solution.py:22
  180.2 18.0 %collective-permute-done.8 = bf16[32,2048]{1,0:T(8,128)(2,1)S(1)} collective-permute-done((bf16[32,2048]{1,0:T(8,128)(2,1)}, bf16[32,2048]{1,0:T(8,128)(2,1)S(1)}, u32[]{:S(2)}, u32[]{:S(2)}) %collective-permute-start.8) | collective-permute-done | bytes 131104 | tf_op jit(solution)/shard_map/ppermute | solution.py:22
  199.3 2.3 collective-permute-start.11
  202.7 1.7 maximum_bitcast_fusion
  204.8 5.9 %collective-permute-done.18 = bf16[4,32,2048]{2,1,0:T(8,128)(2,1)S(1)} collective-permute-done((bf16[4,32,2048]{2,1,0:T(8,128)(2,1)S(1)}, bf16[4,32,2048]{2,1,0:T(8,128)(2,1)S(1)}, u32[]{:S(2)}, u32[]{:S(2)}) %collective-permute-start.18) | collective-permute-done | bytes 524320 | tf_op jit(solution)/shard_map/ppermute | solution.py:22
  211.1 1.5 maximum_bitcast_fusion.1
  212.8 11.4 %collective-permute-done.10 = bf16[4,32,2048]{2,1,0:T(8,128)(2,1)S(1)} collective-permute-done((bf16[4,32,2048]{2,1,0:T(8,128)(2,1)S(1)}, bf16[4,32,2048]{2,1,0:T(8,128)(2,1)S(1)}, u32[]{:S(2)}, u32[]{:S(2)}) %collective-permute-start.10) | collective-permute-done | bytes 524320 | tf_op jit(solution)/shard_map/ppermute | solution.py:22
  225.1 2.5 fusion.18
  227.6 7.6 %fusion.30 = f32[512,896]{1,0:T(8,128)S(1)} fusion(bf16[4096,896]{1,0:T(8,128)(2,1)} %bitcast.70, bf16[512,1024]{1,0:T(8,128)(2,1)S(1)} %get-tuple-element.33, bf16[512,1024]{1,0:T(8,128)(2,1)S(1)} %get-tuple-element.32, bf16[512,1024]{1,0:T(8,128)(2,1)S(1)} %get-tuple-element.31, bf16[512,1024]{1,0:T(8,128)(2,1)S(1)} %get-tuple-element.30), kind=kOutput, calls=%fused_computation.71 | convolution fusion | flops 3774873600 | bytes 13369344 | tf_op jit(solution)/shard_map/dot_general | solution.py:283
  235.2 2.4 convolution_convert_fusion.1
  237.7 7.6 %fusion.29 = f32[512,896]{1,0:T(8,128)S(1)} fusion(bf16[4096,896]{1,0:T(8,128)(2,1)} %bitcast.75, bf16[512,1024]{1,0:T(8,128)(2,1)S(1)} %get-tuple-element.33, bf16[512,1024]{1,0:T(8,128)(2,1)S(1)} %get-tuple-element.32, bf16[512,1024]{1,0:T(8,128)(2,1)S(1)} %get-tuple-element.31, bf16[512,1024]{1,0:T(8,128)(2,1)S(1)} %get-tuple-element.30), kind=kOutput, calls=%fused_computation.70 | convolution fusion | flops 3774873600 | bytes 13369344 | tf_op jit(solution)/shard_map/dot_general | solution.py:283
  245.3 2.5 add_convert_fusion
  247.9 2.5 collective-permute-start.29
  252.3 3.3 %collective-permute-start.36 = (bf16[4,32,2048]{2,1,0:T(8,128)(2,1)S(1)}, bf16[4,32,2048]{2,1,0:T(8,128)(2,1)S(1)}, u32[]{:S(2)}, u32[]{:S(2)}) collective-permute-start(bf16[4,32,2048]{2,1,0:T(8,128)(2,1)S(1)} %get-tuple-element.36), channel_id=1, source_target_pairs={{0,16},{8,24},{16,0},{24,8},{1,17},{9,25},{17,1},{25,9},{2,18},{10... | collective-permute-start | bytes 1572872 | tf_op jit(solution)/shard_map/ppermute | solution.py:22
  255.6 17.1 %collective-permute-done.29 = bf16[4,32,2048]{2,1,0:T(8,128)(2,1)S(1)} collective-permute-done((bf16[4,32,2048]{2,1,0:T(8,128)(2,1)S(1)}, bf16[4,32,2048]{2,1,0:T(8,128)(2,1)S(1)}, u32[]{:S(2)}, u32[]{:S(2)}) %collective-permute-start.29) | collective-permute-done | bytes 524320 | tf_op jit(solution)/shard_map/ppermute | solution.py:22
  272.7 1.7 collective-permute-start.37
  274.5 1.8 collective-permute-done.31
  277.2 3.3 %collective-permute-start.33 = (bf16[32,2048]{1,0:T(8,128)(2,1)S(1)}, bf16[32,2048]{1,0:T(8,128)(2,1)S(1)}, u32[]{:S(2)}, u32[]{:S(2)}) collective-permute-start(bf16[32,2048]{1,0:T(8,128)(2,1)S(1)} %get-tuple-element.50), channel_id=1, source_target_pairs={{0,16},{8,24},{16,0},{24,8},{1,17},{9,25},{17,1},{25,9},{2,18},{10... | collective-permute-start | bytes 393224 | tf_op jit(solution)/shard_map/ppermute | solution.py:22
  280.5 10.2 %collective-permute-done.37 = bf16[4,32,2048]{2,1,0:T(8,128)(2,1)S(1)} collective-permute-done((bf16[4,32,2048]{2,1,0:T(8,128)(2,1)S(1)}, bf16[4,32,2048]{2,1,0:T(8,128)(2,1)S(1)}, u32[]{:S(2)}, u32[]{:S(2)}) %collective-permute-start.37) | collective-permute-done | bytes 524320 | tf_op jit(solution)/shard_map/ppermute | solution.py:22
  291.2 3.9 %collective-permute-start.38 = (bf16[32,2048]{1,0:T(8,128)(2,1)S(1)}, bf16[32,2048]{1,0:T(8,128)(2,1)S(1)}, u32[]{:S(2)}, u32[]{:S(2)}) collective-permute-start(bf16[32,2048]{1,0:T(8,128)(2,1)S(1)} %get-tuple-element.51), channel_id=1, source_target_pairs={{0,96},{32,0},{64,32},{96,64},{1,97},{33,1},{65,33},{97,65},{2,98}... | collective-permute-start | bytes 393224 | tf_op jit(solution)/shard_map/ppermute | solution.py:22
  296.1 2.9 collective-permute-done.38
  299.0 2.7 collective-permute-done.39
  303.7 2.9 collective-permute-start.42
  307.9 2.0 collective-permute-done.41
  (175 shorter events, 38.8 us)
Async XLA Ops:
  0.6 32.4 %copy-start = (bf16[4096,128]{1,0:T(8,128)(2,1)S(1)}, bf16[4096,128]{1,0:T(8,128)(2,1)}, u32[]{:S(2)}) copy-start(bf16[4096,128]{1,0:T(8,128)(2,1)} %param.16) | copy-start | bytes 3145732
  0.6 8.1 %copy-start.17 = (s32[1,4]{1,0:T(1,128)S(1)}, s32[1,4]{1,0:T(1,128)}, u32[]{:S(2)}) copy-start(s32[1,4]{1,0:T(1,128)} %param.24) | copy-start | bytes 52
  0.7 8.5 %copy-start.8 = (bf16[4096]{0:T(1024)(128)(2,1)S(1)}, bf16[4096]{0:T(1024)(128)(2,1)}, u32[]{:S(2)}) copy-start(bf16[4096]{0:T(1024)(128)(2,1)} %param.14) | copy-start | bytes 24580
  5.5 82.5 %collective-permute-start.19 = (bf16[1024,896]{1,0:T(8,128)(2,1)}, bf16[1024,896]{1,0:T(8,128)(2,1)}, u32[]{:S(2)}, u32[]{:S(2)}) collective-permute-start(bf16[1024,896]{1,0:T(8,128)(2,1)} %pad_maximum_fusion.3), channel_id=1, source_target_pairs={{0,1},{1,2},{2,3},{3,0},{4,5},{5,6},{6,7},{7,4},{8,9},{9,10},{10,1... | collective-permute-start | bytes 5505032 | tf_op jit(solution)/shard_map/ppermute | solution.py:161
  7.2 83.7 %collective-permute-start.21 = (bf16[1024,896]{1,0:T(8,128)(2,1)}, bf16[1024,896]{1,0:T(8,128)(2,1)}, u32[]{:S(2)}, u32[]{:S(2)}) collective-permute-start(bf16[1024,896]{1,0:T(8,128)(2,1)} %pad_maximum_fusion.3), channel_id=1, source_target_pairs={{0,3},{1,0},{2,1},{3,2},{4,7},{5,4},{6,5},{7,6},{8,11},{9,8},{10,9... | collective-permute-start | bytes 5505032 | tf_op jit(solution)/shard_map/ppermute | solution.py:162
  8.8 7.7 %copy-start.10 = (f32[64]{0:T(128)}, f32[64]{0:T(128)S(1)}, u32[]{:S(2)}) copy-start(f32[64]{0:T(128)S(1)} %multiply_power_fusion) | copy-start | bytes 772
  9.0 1.6 copy-start.15
  9.1 7.4 %copy-start.13 = (f32[128]{0:T(128)}, f32[128]{0:T(128)S(1)}, u32[]{:S(2)}) copy-start(f32[128]{0:T(128)S(1)} %subtract_convert_fusion.1) | copy-start | bytes 1540
  10.7 0.6 copy-start.18
  17.7 12.5 %collective-permute-start = (bf16[128,1,4,128]{3,0,2,1:T(8,128)(2,1)}, bf16[128,1,4,128]{3,0,2,1:T(8,128)(2,1)S(1)}, u32[]{:S(2)}, u32[]{:S(2)}) collective-permute-start(bf16[128,1,4,128]{3,0,2,1:T(8,128)(2,1)} %pad_maximum_fusion.12), channel_id=1, source_target_pairs={{0,4},{4,0},{1,5},{5,1},{2,6},{6,2},{3,7},{7,3},{8,12},{12,8},{9,1... | collective-permute-start | bytes 393224 | tf_op jit(solution)/shard_map/ppermute | solution.py:59
  17.7 112.7 %collective-permute-start.23 = (bf16[448,1024]{1,0:T(8,128)(2,1)}, bf16[448,1024]{1,0:T(8,128)(2,1)}, u32[]{:S(2)}, u32[]{:S(2)}) collective-permute-start(bf16[448,1024]{1,0:T(8,128)(2,1)} %param.22), channel_id=1, source_target_pairs={{0,1},{1,2},{2,3},{3,0},{4,5},{5,6},{6,7},{7,4},{8,9},{9,10},{10,1... | collective-permute-start | bytes 2752520 | tf_op jit(solution)/shard_map/ppermute | solution.py:161
  20.3 4.2 %copy-start.11 = (f32[64]{0:T(128)S(1)}, f32[64]{0:T(128)}, u32[]{:S(2)}) copy-start(f32[64]{0:T(128)} %copy-done.10) | copy-start | bytes 772
  30.9 6.3 %copy-start.12 = (f32[64]{0:T(128)S(1)}, f32[64]{0:T(128)}, u32[]{:S(2)}) copy-start(f32[64]{0:T(128)} %copy-done.10) | copy-start | bytes 772
  30.9 6.3 %copy-start.14 = (f32[128]{0:T(128)S(1)}, f32[128]{0:T(128)}, u32[]{:S(2)}) copy-start(f32[128]{0:T(128)} %copy-done.13) | copy-start | bytes 1540
  30.9 9.1 %collective-permute-start.1 = (bf16[2,128,1,4,128]{4,1,3,2,0:T(8,128)(2,1)}, bf16[2,128,1,4,128]{4,1,3,2,0:T(8,128)(2,1)}, u32[]{:S(2)}, u32[]{:S(2)}) collective-permute-start(bf16[2,128,1,4,128]{4,1,3,2,0:T(8,128)(2,1)} %maximum_select_fusion.1), channel_id=1, source_target_pairs={{0,8},{8,0},{16,24},{24,16},{1,9},{9,1},{17,25},{25,17},{2,10},{10... | collective-permute-start | bytes 786440 | tf_op jit(solution)/shard_map/ppermute | solution.py:59
  67.4 3.9 %copy-start.16 = (s32[128]{0:T(128)S(1)}, s32[128]{0:T(128)}, u32[]{:S(2)}) copy-start(s32[128]{0:T(128)} %copy-done.15) | copy-start | bytes 1540
  67.4 4.4 %copy-start.3 = (bf16[128,4096]{1,0:T(8,128)(2,1)S(1)}, bf16[128,4096]{1,0:T(8,128)(2,1)}, u32[]{:S(2)}) copy-start(bf16[128,4096]{1,0:T(8,128)(2,1)} %param.13) | copy-start | bytes 3145732
  67.4 4.4 %copy-start.19 = (f32[128]{0:T(128)S(1)}, f32[128]{0:T(128)}, u32[]{:S(2)}) copy-start(f32[128]{0:T(128)} %copy-done.18) | copy-start | bytes 1540
  67.5 1.0 copy-start.2
  69.6 13.9 %collective-permute-start.2 = (f32[1,4,2,128,130]{3,1,4,2,0:T(4,128)}, f32[1,4,2,128,130]{3,1,4,2,0:T(4,128)}, u32[]{:S(2)}, u32[]{:S(2)}) collective-permute-start(f32[1,4,2,128,130]{3,1,4,2,0:T(4,128)} %copy.84), channel_id=1, source_target_pairs={{0,8},{8,0},{16,24},{24,16},{1,9},{9,1},{17,25},{25,17},{2,10},{10... | collective-permute-start | bytes 1597448 | tf_op jit(solution)/shard_map/ppermute | solution.py:59
  87.3 6.6 %collective-permute-start.3 = (f32[1,4,1,128,130]{3,4,2,1,0:T(8,128)S(1)}, f32[1,4,1,128,130]{3,4,2,1,0:T(8,128)S(1)}, u32[]{:S(2)}, u32[]{:S(2)}) collective-permute-start(f32[1,4,1,128,130]{3,4,2,1,0:T(8,128)S(1)} %constant_dynamic-slice_fusion.5), channel_id=1, source_target_pairs={{0,4},{4,0},{1,5},{5,1},{2,6},{6,2},{3,7},{7,3},{8,12},{12,8},{9,1... | collective-permute-start | bytes 798728 | tf_op jit(solution)/shard_map/ppermute | solution.py:59
  89.2 24.0 %collective-permute-start.20 = (bf16[512,896]{1,0:T(8,128)(2,1)S(1)}, bf16[512,896]{1,0:T(8,128)(2,1)S(1)}, u32[]{:S(2)}, u32[]{:S(2)}) collective-permute-start(bf16[512,896]{1,0:T(8,128)(2,1)S(1)} %slice.231), channel_id=1, source_target_pairs={{0,1},{1,2},{2,3},{3,0},{4,5},{5,6},{6,7},{7,4},{8,9},{9,10},{10,1... | collective-permute-start | bytes 2752520 | tf_op jit(solution)/shard_map/ppermute | solution.py:165
  92.2 22.5 %collective-permute-start.22 = (bf16[512,896]{1,0:T(8,128)(2,1)S(1)}, bf16[512,896]{1,0:T(8,128)(2,1)S(1)}, u32[]{:S(2)}, u32[]{:S(2)}) collective-permute-start(bf16[512,896]{1,0:T(8,128)(2,1)S(1)} %slice.232), channel_id=1, source_target_pairs={{0,3},{1,0},{2,1},{3,2},{4,7},{5,4},{6,5},{7,6},{8,11},{9,8},{10,9... | collective-permute-start | bytes 2752520 | tf_op jit(solution)/shard_map/ppermute | solution.py:170
  114.8 6.4 %copy-start.4 = (bf16[512,4096]{1,0:T(8,128)(2,1)S(1)}, bf16[512,4096]{1,0:T(8,128)(2,1)}, u32[]{:S(2)}) copy-start(bf16[512,4096]{1,0:T(8,128)(2,1)} %param.18) | copy-start | bytes 12582916
  121.1 116.6 %collective-permute-start.27 = (bf16[4,1024,896]{2,1,0:T(8,128)(2,1)}, bf16[4,1024,896]{2,1,0:T(8,128)(2,1)}, u32[]{:S(2)}, u32[]{:S(2)}) collective-permute-start(bf16[4,1024,896]{2,1,0:T(8,128)(2,1)} %pad_maximum_fusion), channel_id=1, source_target_pairs={{0,4},{4,0},{1,5},{5,1},{2,6},{6,2},{3,7},{7,3},{8,12},{12,8},{9,1... | collective-permute-start | bytes 22020104 | tf_op jit(solution)/shard_map/ppermute | solution.py:59
  122.0 8.2 %copy-start.9 = (bf16[4096]{0:T(1024)(128)(2,1)S(1)}, bf16[4096]{0:T(1024)(128)(2,1)}, u32[]{:S(2)}) copy-start(bf16[4096]{0:T(1024)(128)(2,1)} %param.19) | copy-start | bytes 24580
  123.0 10.4 %collective-permute-start.4 = (bf16[32,4096]{1,0:T(8,128)(2,1)}, bf16[32,4096]{1,0:T(8,128)(2,1)}, u32[]{:S(2)}, u32[]{:S(2)}) collective-permute-start(bf16[32,4096]{1,0:T(8,128)(2,1)} %get-tuple-element.37), channel_id=1, source_target_pairs={{0,1},{1,2},{2,3},{3,0},{4,5},{5,6},{6,7},{7,4},{8,9},{9,10},{10,1... | collective-permute-start | bytes 786440 | tf_op jit(solution)/shard_map/ppermute | solution.py:22
  124.4 16.2 %collective-permute-start.5 = (bf16[32,4096]{1,0:T(8,128)(2,1)}, bf16[32,4096]{1,0:T(8,128)(2,1)}, u32[]{:S(2)}, u32[]{:S(2)}) collective-permute-start(bf16[32,4096]{1,0:T(8,128)(2,1)} %get-tuple-element.39), channel_id=1, source_target_pairs={{0,2},{1,3},{2,0},{3,1},{4,6},{5,7},{6,4},{7,5},{8,10},{9,11},{10,... | collective-permute-start | bytes 786440 | tf_op jit(solution)/shard_map/ppermute | solution.py:22
  127.5 13.1 %collective-permute-start.6 = (bf16[32,4096]{1,0:T(8,128)(2,1)S(1)}, bf16[32,4096]{1,0:T(8,128)(2,1)}, u32[]{:S(2)}, u32[]{:S(2)}) collective-permute-start(bf16[32,4096]{1,0:T(8,128)(2,1)S(1)} %get-tuple-element.38), channel_id=1, source_target_pairs={{0,3},{1,0},{2,1},{3,2},{4,7},{5,4},{6,5},{7,6},{8,11},{9,8},{10,9... | collective-permute-start | bytes 786440 | tf_op jit(solution)/shard_map/ppermute | solution.py:22
  130.3 28.9 %collective-permute-start.25 = (bf16[448,1024]{1,0:T(8,128)(2,1)}, bf16[448,1024]{1,0:T(8,128)(2,1)S(1)}, u32[]{:S(2)}, u32[]{:S(2)}) collective-permute-start(bf16[448,1024]{1,0:T(8,128)(2,1)} %param.22), channel_id=1, source_target_pairs={{0,3},{1,0},{2,1},{3,2},{4,7},{5,4},{6,5},{7,6},{8,11},{9,8},{10,9... | collective-permute-start | bytes 2752520 | tf_op jit(solution)/shard_map/ppermute | solution.py:162
  133.4 35.0 %collective-permute-start.24 = (bf16[224,1024]{1,0:T(8,128)(2,1)S(1)}, bf16[224,1024]{1,0:T(8,128)(2,1)}, u32[]{:S(2)}, u32[]{:S(2)}) collective-permute-start(bf16[224,1024]{1,0:T(8,128)(2,1)S(1)} %slice.235), channel_id=1, source_target_pairs={{0,1},{1,2},{2,3},{3,0},{4,5},{5,6},{6,7},{7,4},{8,9},{9,10},{10,1... | collective-permute-start | bytes 1376264 | tf_op jit(solution)/shard_map/ppermute | solution.py:165
  143.1 18.9 %collective-permute-start.13 = (bf16[32,2048]{1,0:T(8,128)(2,1)S(1)}, bf16[32,2048]{1,0:T(8,128)(2,1)S(1)}, u32[]{:S(2)}, u32[]{:S(2)}) collective-permute-start(bf16[32,2048]{1,0:T(8,128)(2,1)S(1)} %get-tuple-element.64), channel_id=1, source_target_pairs={{0,32},{32,64},{64,96},{96,0},{1,33},{33,65},{65,97},{97,1},{2,34}... | collective-permute-start | bytes 393224 | tf_op jit(solution)/shard_map/ppermute | solution.py:22
  144.5 20.2 %collective-permute-start.14 = (bf16[32,2048]{1,0:T(8,128)(2,1)S(1)}, bf16[32,2048]{1,0:T(8,128)(2,1)S(1)}, u32[]{:S(2)}, u32[]{:S(2)}) collective-permute-start(bf16[32,2048]{1,0:T(8,128)(2,1)S(1)} %get-tuple-element.64), channel_id=1, source_target_pairs={{0,64},{32,96},{64,0},{96,32},{1,65},{33,97},{65,1},{97,33},{2,66}... | collective-permute-start | bytes 393224 | tf_op jit(solution)/shard_map/ppermute | solution.py:22
  159.2 18.7 %copy-start.5 = (bf16[448,1024]{1,0:T(8,128)(2,1)}, bf16[448,1024]{1,0:T(8,128)(2,1)S(1)}, u32[]{:S(2)}) copy-start(bf16[448,1024]{1,0:T(8,128)(2,1)S(1)} %collective-permute-done.25) | copy-start | bytes 2752516
  159.2 7.0 %collective-permute-start.15 = (bf16[32,2048]{1,0:T(8,128)(2,1)S(1)}, bf16[32,2048]{1,0:T(8,128)(2,1)S(1)}, u32[]{:S(2)}, u32[]{:S(2)}) collective-permute-start(bf16[32,2048]{1,0:T(8,128)(2,1)S(1)} %get-tuple-element.64), channel_id=1, source_target_pairs={{0,96},{32,0},{64,32},{96,64},{1,97},{33,1},{65,33},{97,65},{2,98}... | collective-permute-start | bytes 393224 | tf_op jit(solution)/shard_map/ppermute | solution.py:22
  162.0 12.4 %collective-permute-start.26 = (bf16[224,1024]{1,0:T(8,128)(2,1)S(1)}, bf16[224,1024]{1,0:T(8,128)(2,1)S(1)}, u32[]{:S(2)}, u32[]{:S(2)}) collective-permute-start(bf16[224,1024]{1,0:T(8,128)(2,1)S(1)} %slice.236), channel_id=1, source_target_pairs={{0,3},{1,0},{2,1},{3,2},{4,7},{5,4},{6,5},{7,6},{8,11},{9,8},{10,9... | collective-permute-start | bytes 1376264 | tf_op jit(solution)/shard_map/ppermute | solution.py:170
  164.7 13.2 %collective-permute-start.7 = (bf16[32,2048]{1,0:T(8,128)(2,1)}, bf16[32,2048]{1,0:T(8,128)(2,1)}, u32[]{:S(2)}, u32[]{:S(2)}) collective-permute-start(bf16[32,2048]{1,0:T(8,128)(2,1)} %get-tuple-element.65), channel_id=1, source_target_pairs={{0,8},{8,16},{16,24},{24,0},{1,9},{9,17},{17,25},{25,1},{2,10},{10... | collective-permute-start | bytes 393224 | tf_op jit(solution)/shard_map/ppermute | solution.py:22
  166.4 32.9 %collective-permute-start.16 = (bf16[4,32,2048]{2,1,0:T(8,128)(2,1)S(1)}, bf16[4,32,2048]{2,1,0:T(8,128)(2,1)}, u32[]{:S(2)}, u32[]{:S(2)}) collective-permute-start(bf16[4,32,2048]{2,1,0:T(8,128)(2,1)S(1)} %get-tuple-element.55), channel_id=1, source_target_pairs={{0,8},{8,16},{16,24},{24,0},{1,9},{9,17},{17,25},{25,1},{2,10},{10... | collective-permute-start | bytes 1572872 | tf_op jit(solution)/shard_map/ppermute | solution.py:22
  168.4 33.2 %collective-permute-start.17 = (bf16[4,32,2048]{2,1,0:T(8,128)(2,1)S(1)}, bf16[4,32,2048]{2,1,0:T(8,128)(2,1)}, u32[]{:S(2)}, u32[]{:S(2)}) collective-permute-start(bf16[4,32,2048]{2,1,0:T(8,128)(2,1)S(1)} %get-tuple-element.55), channel_id=1, source_target_pairs={{0,16},{8,24},{16,0},{24,8},{1,17},{9,25},{17,1},{25,9},{2,18},{10... | collective-permute-start | bytes 1572872 | tf_op jit(solution)/shard_map/ppermute | solution.py:22
  174.4 3.5 %copy-start.7 = (bf16[224,1024]{1,0:T(8,128)(2,1)}, bf16[224,1024]{1,0:T(8,128)(2,1)S(1)}, u32[]{:S(2)}) copy-start(bf16[224,1024]{1,0:T(8,128)(2,1)S(1)} %collective-permute-done.26) | copy-start | bytes 1376260
  174.4 23.8 %collective-permute-start.8 = (bf16[32,2048]{1,0:T(8,128)(2,1)}, bf16[32,2048]{1,0:T(8,128)(2,1)S(1)}, u32[]{:S(2)}, u32[]{:S(2)}) collective-permute-start(bf16[32,2048]{1,0:T(8,128)(2,1)} %get-tuple-element.65), channel_id=1, source_target_pairs={{0,16},{8,24},{16,0},{24,8},{1,17},{9,25},{17,1},{25,9},{2,18},{10... | collective-permute-start | bytes 393224 | tf_op jit(solution)/shard_map/ppermute | solution.py:22
  177.9 20.3 %collective-permute-start.9 = (bf16[32,2048]{1,0:T(8,128)(2,1)}, bf16[32,2048]{1,0:T(8,128)(2,1)S(1)}, u32[]{:S(2)}, u32[]{:S(2)}) collective-permute-start(bf16[32,2048]{1,0:T(8,128)(2,1)} %get-tuple-element.65), channel_id=1, source_target_pairs={{0,24},{8,0},{16,8},{24,16},{1,25},{9,1},{17,9},{25,17},{2,26},{10... | collective-permute-start | bytes 393224 | tf_op jit(solution)/shard_map/ppermute | solution.py:22
  178.9 23.8 %copy-start.6 = (bf16[448,1024]{1,0:T(8,128)(2,1)S(1)}, bf16[448,1024]{1,0:T(8,128)(2,1)}, u32[]{:S(2)}) copy-start(bf16[448,1024]{1,0:T(8,128)(2,1)} %copy-done.5) | copy-start | bytes 2752516
  198.2 12.5 %collective-permute-start.18 = (bf16[4,32,2048]{2,1,0:T(8,128)(2,1)S(1)}, bf16[4,32,2048]{2,1,0:T(8,128)(2,1)S(1)}, u32[]{:S(2)}, u32[]{:S(2)}) collective-permute-start(bf16[4,32,2048]{2,1,0:T(8,128)(2,1)S(1)} %get-tuple-element.55), channel_id=1, source_target_pairs={{0,24},{8,0},{16,8},{24,16},{1,25},{9,1},{17,9},{25,17},{2,26},{10... | collective-permute-start | bytes 1572872 | tf_op jit(solution)/shard_map/ppermute | solution.py:22
  199.2 25.1 %collective-permute-start.10 = (bf16[4,32,2048]{2,1,0:T(8,128)(2,1)S(1)}, bf16[4,32,2048]{2,1,0:T(8,128)(2,1)S(1)}, u32[]{:S(2)}, u32[]{:S(2)}) collective-permute-start(bf16[4,32,2048]{2,1,0:T(8,128)(2,1)S(1)} %get-tuple-element.57), channel_id=1, source_target_pairs={{0,32},{32,64},{64,96},{96,0},{1,33},{33,65},{65,97},{97,1},{2,34}... | collective-permute-start | bytes 1572872 | tf_op jit(solution)/shard_map/ppermute | solution.py:22
  199.3 25.0 %collective-permute-start.11 = (bf16[4,32,2048]{2,1,0:T(8,128)(2,1)S(1)}, bf16[4,32,2048]{2,1,0:T(8,128)(2,1)S(1)}, u32[]{:S(2)}, u32[]{:S(2)}) collective-permute-start(bf16[4,32,2048]{2,1,0:T(8,128)(2,1)S(1)} %get-tuple-element.57), channel_id=1, source_target_pairs={{0,64},{32,96},{64,0},{96,32},{1,65},{33,97},{65,1},{97,33},{2,66}... | collective-permute-start | bytes 1572872 | tf_op jit(solution)/shard_map/ppermute | solution.py:22
  201.6 23.3 %collective-permute-start.12 = (bf16[4,32,2048]{2,1,0:T(8,128)(2,1)S(1)}, bf16[4,32,2048]{2,1,0:T(8,128)(2,1)S(1)}, u32[]{:S(2)}, u32[]{:S(2)}) collective-permute-start(bf16[4,32,2048]{2,1,0:T(8,128)(2,1)S(1)} %get-tuple-element.57), channel_id=1, source_target_pairs={{0,96},{32,0},{64,32},{96,64},{1,97},{33,1},{65,33},{97,65},{2,98}... | collective-permute-start | bytes 1572872 | tf_op jit(solution)/shard_map/ppermute | solution.py:22
  210.7 34.6 %collective-permute-start.28 = (bf16[448,4096]{1,0:T(8,128)(2,1)S(1)}, bf16[448,4096]{1,0:T(8,128)(2,1)S(1)}, u32[]{:S(2)}, u32[]{:S(2)}) collective-permute-start(bf16[448,4096]{1,0:T(8,128)(2,1)S(1)} %bitcast.223), channel_id=1, source_target_pairs={{0,4},{4,0},{1,5},{5,1},{2,6},{6,2},{3,7},{7,3},{8,12},{12,8},{9,1... | collective-permute-start | bytes 11010056 | tf_op jit(solution)/shard_map/ppermute | solution.py:59
  247.9 24.9 %collective-permute-start.29 = (bf16[4,32,2048]{2,1,0:T(8,128)(2,1)S(1)}, bf16[4,32,2048]{2,1,0:T(8,128)(2,1)S(1)}, u32[]{:S(2)}, u32[]{:S(2)}) collective-permute-start(bf16[4,32,2048]{2,1,0:T(8,128)(2,1)S(1)} %get-tuple-element.27), channel_id=1, source_target_pairs={{0,96},{32,0},{64,32},{96,64},{1,97},{33,1},{65,33},{97,65},{2,98}... | collective-permute-start | bytes 1572872 | tf_op jit(solution)/shard_map/ppermute | solution.py:22
  250.3 24.1 %collective-permute-start.30 = (bf16[4,32,2048]{2,1,0:T(8,128)(2,1)S(1)}, bf16[4,32,2048]{2,1,0:T(8,128)(2,1)S(1)}, u32[]{:S(2)}, u32[]{:S(2)}) collective-permute-start(bf16[4,32,2048]{2,1,0:T(8,128)(2,1)S(1)} %get-tuple-element.29), channel_id=1, source_target_pairs={{0,64},{32,96},{64,0},{96,32},{1,65},{33,97},{65,1},{97,33},{2,66}... | collective-permute-start | bytes 1572872 | tf_op jit(solution)/shard_map/ppermute | solution.py:22
  250.3 26.0 %collective-permute-start.31 = (bf16[4,32,2048]{2,1,0:T(8,128)(2,1)S(1)}, bf16[4,32,2048]{2,1,0:T(8,128)(2,1)S(1)}, u32[]{:S(2)}, u32[]{:S(2)}) collective-permute-start(bf16[4,32,2048]{2,1,0:T(8,128)(2,1)S(1)} %get-tuple-element.28), channel_id=1, source_target_pairs={{0,32},{32,64},{64,96},{96,0},{1,33},{33,65},{65,97},{97,1},{2,34}... | collective-permute-start | bytes 1572872 | tf_op jit(solution)/shard_map/ppermute | solution.py:22
  251.7 28.8 %collective-permute-start.35 = (bf16[4,32,2048]{2,1,0:T(8,128)(2,1)S(1)}, bf16[4,32,2048]{2,1,0:T(8,128)(2,1)S(1)}, u32[]{:S(2)}, u32[]{:S(2)}) collective-permute-start(bf16[4,32,2048]{2,1,0:T(8,128)(2,1)S(1)} %get-tuple-element.34), channel_id=1, source_target_pairs={{0,24},{8,0},{16,8},{24,16},{1,25},{9,1},{17,9},{25,17},{2,26},{10... | collective-permute-start | bytes 1572872 | tf_op jit(solution)/shard_map/ppermute | solution.py:22
  252.3 28.3 %collective-permute-start.36 = (bf16[4,32,2048]{2,1,0:T(8,128)(2,1)S(1)}, bf16[4,32,2048]{2,1,0:T(8,128)(2,1)S(1)}, u32[]{:S(2)}, u32[]{:S(2)}) collective-permute-start(bf16[4,32,2048]{2,1,0:T(8,128)(2,1)S(1)} %get-tuple-element.36), channel_id=1, source_target_pairs={{0,16},{8,24},{16,0},{24,8},{1,17},{9,25},{17,1},{25,9},{2,18},{10... | collective-permute-start | bytes 1572872 | tf_op jit(solution)/shard_map/ppermute | solution.py:22
  272.7 18.1 %collective-permute-start.37 = (bf16[4,32,2048]{2,1,0:T(8,128)(2,1)S(1)}, bf16[4,32,2048]{2,1,0:T(8,128)(2,1)S(1)}, u32[]{:S(2)}, u32[]{:S(2)}) collective-permute-start(bf16[4,32,2048]{2,1,0:T(8,128)(2,1)S(1)} %get-tuple-element.35), channel_id=1, source_target_pairs={{0,8},{8,16},{16,24},{24,0},{1,9},{9,17},{17,25},{25,1},{2,10},{10... | collective-permute-start | bytes 1572872 | tf_op jit(solution)/shard_map/ppermute | solution.py:22
  276.7 18.4 %collective-permute-start.32 = (bf16[32,2048]{1,0:T(8,128)(2,1)S(1)}, bf16[32,2048]{1,0:T(8,128)(2,1)S(1)}, u32[]{:S(2)}, u32[]{:S(2)}) collective-permute-start(bf16[32,2048]{1,0:T(8,128)(2,1)S(1)} %get-tuple-element.48), channel_id=1, source_target_pairs={{0,24},{8,0},{16,8},{24,16},{1,25},{9,1},{17,9},{25,17},{2,26},{10... | collective-permute-start | bytes 393224 | tf_op jit(solution)/shard_map/ppermute | solution.py:22
  277.2 18.8 %collective-permute-start.33 = (bf16[32,2048]{1,0:T(8,128)(2,1)S(1)}, bf16[32,2048]{1,0:T(8,128)(2,1)S(1)}, u32[]{:S(2)}, u32[]{:S(2)}) collective-permute-start(bf16[32,2048]{1,0:T(8,128)(2,1)S(1)} %get-tuple-element.50), channel_id=1, source_target_pairs={{0,16},{8,24},{16,0},{24,8},{1,17},{9,25},{17,1},{25,9},{2,18},{10... | collective-permute-start | bytes 393224 | tf_op jit(solution)/shard_map/ppermute | solution.py:22
  280.5 15.5 %collective-permute-start.34 = (bf16[32,2048]{1,0:T(8,128)(2,1)S(1)}, bf16[32,2048]{1,0:T(8,128)(2,1)S(1)}, u32[]{:S(2)}, u32[]{:S(2)}) collective-permute-start(bf16[32,2048]{1,0:T(8,128)(2,1)S(1)} %get-tuple-element.49), channel_id=1, source_target_pairs={{0,8},{8,16},{16,24},{24,0},{1,9},{9,17},{17,25},{25,1},{2,10},{10... | collective-permute-start | bytes 393224 | tf_op jit(solution)/shard_map/ppermute | solution.py:22
  291.2 7.8 %collective-permute-start.38 = (bf16[32,2048]{1,0:T(8,128)(2,1)S(1)}, bf16[32,2048]{1,0:T(8,128)(2,1)S(1)}, u32[]{:S(2)}, u32[]{:S(2)}) collective-permute-start(bf16[32,2048]{1,0:T(8,128)(2,1)S(1)} %get-tuple-element.51), channel_id=1, source_target_pairs={{0,96},{32,0},{64,32},{96,64},{1,97},{33,1},{65,33},{97,65},{2,98}... | collective-permute-start | bytes 393224 | tf_op jit(solution)/shard_map/ppermute | solution.py:22
  295.1 6.6 %collective-permute-start.39 = (bf16[32,2048]{1,0:T(8,128)(2,1)S(1)}, bf16[32,2048]{1,0:T(8,128)(2,1)S(1)}, u32[]{:S(2)}, u32[]{:S(2)}) collective-permute-start(bf16[32,2048]{1,0:T(8,128)(2,1)S(1)} %get-tuple-element.53), channel_id=1, source_target_pairs={{0,64},{32,96},{64,0},{96,32},{1,65},{33,97},{65,1},{97,33},{2,66}... | collective-permute-start | bytes 393224 | tf_op jit(solution)/shard_map/ppermute | solution.py:22
  295.1 7.6 %collective-permute-start.40 = (bf16[32,2048]{1,0:T(8,128)(2,1)S(1)}, bf16[32,2048]{1,0:T(8,128)(2,1)S(1)}, u32[]{:S(2)}, u32[]{:S(2)}) collective-permute-start(bf16[32,2048]{1,0:T(8,128)(2,1)S(1)} %get-tuple-element.52), channel_id=1, source_target_pairs={{0,32},{32,64},{64,96},{96,0},{1,33},{33,65},{65,97},{97,1},{2,34}... | collective-permute-start | bytes 393224 | tf_op jit(solution)/shard_map/ppermute | solution.py:22
  302.6 9.7 %copy-start.1 = (bf16[4096,128]{1,0:T(8,128)(2,1)S(1)}, bf16[4096,128]{1,0:T(8,128)(2,1)}, u32[]{:S(2)}) copy-start(bf16[4096,128]{1,0:T(8,128)(2,1)} %param.16) | copy-start | bytes 3145732
  303.6 6.2 %collective-permute-start.41 = (bf16[32,1024]{1,0:T(8,128)(2,1)S(1)}, bf16[32,1024]{1,0:T(8,128)(2,1)S(1)}, u32[]{:S(2)}, u32[]{:S(2)}) collective-permute-start(bf16[32,1024]{1,0:T(8,128)(2,1)S(1)} %get-tuple-element.61), channel_id=1, source_target_pairs={{0,1},{1,2},{2,3},{3,0},{4,5},{5,6},{6,7},{7,4},{8,9},{9,10},{10,1... | collective-permute-start | bytes 196616 | tf_op jit(solution)/shard_map/ppermute | solution.py:22
  303.7 6.2 %collective-permute-start.42 = (bf16[32,1024]{1,0:T(8,128)(2,1)S(1)}, bf16[32,1024]{1,0:T(8,128)(2,1)S(1)}, u32[]{:S(2)}, u32[]{:S(2)}) collective-permute-start(bf16[32,1024]{1,0:T(8,128)(2,1)S(1)} %get-tuple-element.60), channel_id=1, source_target_pairs={{0,2},{1,3},{2,0},{3,1},{4,6},{5,7},{6,4},{7,5},{8,10},{9,11},{10,... | collective-permute-start | bytes 196616 | tf_op jit(solution)/shard_map/ppermute | solution.py:22
  306.6 4.3 %collective-permute-start.43 = (bf16[32,1024]{1,0:T(8,128)(2,1)S(1)}, bf16[32,1024]{1,0:T(8,128)(2,1)S(1)}, u32[]{:S(2)}, u32[]{:S(2)}) collective-permute-start(bf16[32,1024]{1,0:T(8,128)(2,1)S(1)} %get-tuple-element.59), channel_id=1, source_target_pairs={{0,3},{1,0},{2,1},{3,2},{4,7},{5,4},{6,5},{7,6},{8,11},{9,8},{10,9... | collective-permute-start | bytes 196616 | tf_op jit(solution)/shard_map/ppermute | solution.py:22
